TPU v7x, 128 devices: a whole 4x4x4 slice. The times are simulated.
128 devices in a mesh: row: 16 (over z, y), col: 8 (over x, core).
Axes of the slice: x: 4, y: 4, z: 4, core: 2. Of those that a mesh axis runs over, the one named last changes fastest.
Arguments:
- child_inverse: float32 [16384, 8192], P('row', 'col'), may hold values from -0.0625 to 0.0625
- child_border: float32 [32768, 8192], P('row', 'col'), may hold values from -0.0625 to 0.0625
- child_sep_rhs: float32 [16384, 128], P('row'), may hold values from -6 to 6
- child_border_rhs: float32 [32768, 128], P(('row', 'col')), may hold values from -6 to 6
- child_map: int32 [32768], P(('row', 'col')), may hold values from 0 to 24575, as said below
- parent_inverse: float32 [8192, 8192], P('row', 'col'), may hold values from -0.0625 to 0.0625
- parent_border: float32 [16384, 8192], P('row', 'col'), may hold values from -0.0625 to 0.0625
- parent_sep_rhs: float32 [8192, 128], P(('row', 'col')), may hold values from -6 to 6
- parent_border_rhs: float32 [16384, 128], P(('row', 'col')), may hold values from -6 to 6
Outputs:
- child_solution: float32 [8192, 256], P('col', 'row')
- parent_solution: float32 [8192, 128], P('col')
- parent_contribution: float32 [16384, 128], P(('row', 'col'))
Inputs may be any that keep to these rules, and one draw needn't show every extreme that they name: `child_map`: within one child (entries c * 16384 to (c + 1) * 16384 - 1) all entries are distinct; each child names every separator row 0 to 8191 and, of each owner's 128 border rows, exactly half. The owner of parent row p is p // 64 if p < 8192, else (p - 8192) // 128; every owner is named by exactly 128 entries of each child. Of the 256 entries of one device (aligned blocks), at most 4 name the same owner, and this is reached in every draw.
All inputs are finite; a program needn't handle non-finite values.
Results may differ from a plain program's by a relative error of at most 0.00012.
Values sent between devices are 32-bit elements; how exact they have to be, the bound alone decides.
No kernel may reach another device: no remote copies, remote signals or barrier semaphores. Data moves between devices by JAX's collectives and lax.ppermute only.
A program may use at most 64 MiB of HBM per device.

v0:
```python
import jax
import jax.numpy as jnp
from jax import lax
from jax.sharding import PartitionSpec as P

SP = 8192


def swapped(value, axis, distance):
    mask = 2**distance
    pairs = [(source, source ^ mask) for source in range(lax.axis_size(axis))]
    return lax.ppermute(value, axis, pairs)


def local(
    child_inverse,
    child_border,
    child_sep_rhs,
    child_border_rhs,
    child_map,
    parent_inverse,
    parent_border,
    parent_sep_rhs,
    parent_border_rhs,
):
    highest = lax.Precision.HIGHEST
    contract_rows = (((0,), (0,)), ((), ()))
    rows_axis = lax.axis_size("row")
    cols_axis = lax.axis_size("col")
    half_rows = rows_axis // 2
    levels = half_rows.bit_length() - 1
    row_index = lax.axis_index("row")
    within = row_index % half_rows
    partial_term = lax.dot_general(
        child_inverse,
        child_sep_rhs,
        contract_rows,
        precision=highest,
        preferred_element_type=jnp.float32,
    )
    width_rhs = partial_term.shape[1]
    current = partial_term
    for section_bit in reversed(range(levels)):
        half_width = current.shape[1] // 2
        lower = current[:, :half_width]
        upper = current[:, half_width:]
        is_upper = within >> section_bit & 1 == 1
        outgoing_half = jnp.where(is_upper, lower, upper)
        arrived = swapped(outgoing_half, "row", section_bit)
        current = jnp.where(is_upper, upper, lower) + arrived
    child_part = current
    for section_bit in range(levels):
        is_upper = within >> section_bit & 1 == 1
        arrived = swapped(current, "row", section_bit)
        current = jnp.where(
            is_upper,
            jnp.concatenate([arrived, current], axis=1),
            jnp.concatenate([current, arrived], axis=1),
        )
    block_rows = child_border
    carried = lax.psum_scatter(
        jnp.dot(block_rows, current, precision=highest, preferred_element_type=jnp.float32),
        "col",
        scatter_dimension=0,
        tiled=True,
    )
    outgoing = child_border_rhs - carried
    devices_all = rows_axis * cols_axis
    sep_dev = parent_sep_rhs.shape[0]
    bord_dev = parent_border_rhs.shape[0]
    rows_src = child_map.shape[0]
    capacity = rows_src // devices_all + 2
    is_sep = child_map < SP
    owner_id = jnp.where(is_sep, child_map // sep_dev, (child_map - SP) // bord_dev)
    target = jnp.where(is_sep, child_map % sep_dev, sep_dev + (child_map - SP) % bord_dev)
    onehot = (owner_id[:, None] == jnp.arange(devices_all, dtype=jnp.int32)[None, :]).astype(
        jnp.int32
    )
    running = jnp.cumsum(onehot, axis=0)
    placed = owner_id * capacity + jnp.sum(onehot * running, axis=1) - 1
    send_rows = jnp.zeros((devices_all * capacity, width_rhs), jnp.float32).at[placed].set(outgoing)
    send_index = (
        jnp.full((devices_all * capacity,), sep_dev + bord_dev, jnp.int32).at[placed].set(target)
    )
    got_rows, got_index = (
        lax.all_to_all(
            send_rows.reshape(devices_all, capacity, width_rhs),
            ("row", "col"),
            split_axis=0,
            concat_axis=0,
            tiled=True,
        ),
        lax.all_to_all(
            send_index.reshape(devices_all, capacity),
            ("row", "col"),
            split_axis=0,
            concat_axis=0,
            tiled=True,
        ),
    )
    received = (
        jnp.zeros((sep_dev + bord_dev, width_rhs), jnp.float32)
        .at[got_index.reshape(-1)]
        .add(got_rows.reshape(-1, width_rhs), mode="drop")
    )
    sep_rows = parent_sep_rhs + received[:sep_dev]
    border_rows = parent_border_rhs + received[sep_dev:]
    block_rows = parent_inverse
    partial_sep = lax.dot_general(
        block_rows,
        lax.all_gather(sep_rows, "col", axis=0, tiled=True),
        contract_rows,
        precision=highest,
        preferred_element_type=jnp.float32,
    )
    parent_solution = lax.psum(partial_sep, "row")
    block_rows = parent_border
    carried_parent = lax.psum_scatter(
        jnp.dot(block_rows, parent_solution, precision=highest, preferred_element_type=jnp.float32),
        "col",
        scatter_dimension=0,
        tiled=True,
    )
    parent_contribution = border_rows - carried_parent
    return (child_part, parent_solution, parent_contribution)


def solution(mesh):
    placed = (
        P("row", "col"),
        P("row", "col"),
        P("row", None),
        P(("row", "col"), None),
        P(("row", "col")),
        P("row", "col"),
        P("row", "col"),
        P(("row", "col"), None),
        P(("row", "col"), None),
    )
    return jax.shard_map(
        local,
        mesh=mesh,
        in_specs=placed,
        out_specs=(P("col", "row"), P("col", None), P(("row", "col"), None)),
        check_vma=False,
    )
```

profile of v0, /device:TPU:1, one launch (start us, length us, event | category | flops | bytes accessed | tf_op | source)
XLA Modules:
  0.0 262.3 jit_solution(705122187382554297)
XLA Ops:
  7.2 5.0 %fusion.20 = f32[1024,128]{0,1:T(8,128)S(1)} fusion(f32[1024,1024]{1,0:T(8,128)} %param.9, f32[1024,128]{1,0:T(8,128)} %param.11), kind=kOutput, calls=%fused_computation.59 | convolution fusion | flops 1610612736 | bytes 5242880 | tf_op jit(solution)/shard_map/dot_general | solution.py:34
  12.2 2.5 collective-permute-start
  14.8 6.0 %collective-permute-done = f32[1024,64]{0,1:T(8,128)S(1)} collective-permute-done((f32[1024,64]{0,1:T(8,128)S(1)}, f32[1024,64]{0,1:T(8,128)S(1)}, u32[]{:S(2)}, u32[]{:S(2)}) %collective-permute-start) | collective-permute-done | bytes 262176 | tf_op jit(solution)/shard_map/ppermute | solution.py:12
  20.9 2.9 %collective-permute-start.1 = (f32[1024,32]{0,1:T(8,128)S(1)}, f32[1024,32]{0,1:T(8,128)S(1)}, u32[]{:S(2)}, u32[]{:S(2)}) collective-permute-start(f32[1024,32]{0,1:T(8,128)S(1)} %slice_select_fusion.1), channel_id=1, source_target_pairs={{0,16},{8,24},{16,0},{24,8},{32,48},{40,56},{48,32},{56,40},{64,80... | collective-permute-start | bytes 393224 | tf_op jit(solution)/shard_map/ppermute | solution.py:12
  23.7 2.5 collective-permute-done.1
  26.3 1.3 collective-permute-start.2
  27.6 1.9 collective-permute-done.2
  29.5 1.3 collective-permute-start.3
  30.8 2.3 collective-permute-done.3
  33.1 3.0 %collective-permute-start.4 = (f32[1024,32]{0,1:T(8,128)S(1)}, f32[1024,32]{0,1:T(8,128)S(1)}, u32[]{:S(2)}, u32[]{:S(2)}) collective-permute-start(f32[1024,32]{0,1:T(8,128)S(1)} %maximum_select_fusion.3), channel_id=1, source_target_pairs={{0,16},{8,24},{16,0},{24,8},{32,48},{40,56},{48,32},{56,40},{64,80... | collective-permute-start | bytes 393224 | tf_op jit(solution)/shard_map/ppermute | solution.py:12
  36.1 2.4 collective-permute-done.4
  38.5 1.7 collective-permute-start.5
  40.3 4.1 %collective-permute-done.5 = f32[1024,64]{0,1:T(8,128)S(1)} collective-permute-done((f32[1024,64]{0,1:T(8,128)S(1)}, f32[1024,64]{0,1:T(8,128)S(1)}, u32[]{:S(2)}, u32[]{:S(2)}) %collective-permute-start.5) | collective-permute-done | bytes 262176 | tf_op jit(solution)/shard_map/ppermute | solution.py:12
  44.3 11.9 %convolution_bitcast_fusion = f32[2048,128]{0,1:T(8,128)} fusion(f32[2048,1024]{1,0:T(8,128)} %param.10, f32[1024,64]{0,1:T(8,128)S(1)} %maximum_select_fusion.2, f32[1024,64]{0,1:T(8,128)S(1)} %collective-permute-done.5, pred[]{:T(512)S(6)} %eq.42), kind=kOutput, calls=%fused_computation.3 | convolution fusion | flops 3221618688 | bytes 9961473 | tf_op jit(solution)/shard_map/dot_general | solution.py:62
  56.9 1.4 scatter_custom_fusion
  58.3 0.7 all_to_all.9
  59.0 17.3 %all-to-all-start = ((s32[128,1,4]{2,1,0:T(1,128)}), s32[128,1,4]{2,1,0:T(1,128)S(1)}, u32[]{:S(2)}, u32[]{:S(2)}) async-start(s32[128,1,4]{2,1,0:T(1,128)} %bitcast.4), calls=%async_computation | async-start | bytes 131072 | tf_op jit(solution)/shard_map/all_to_all | solution.py:93
  76.5 19.0 %reduce-scatter.3.cloned.1.call-done = f32[256,128]{0,1:T(8,128)} async-done(((f32[2048,128]{0,1:T(8,128)}), f32[256,128]{0,1:T(8,128)}) %reduce-scatter.3.cloned.1.call-update) | async-done | bytes 131088 | tf_op jit(solution)/shard_map/reduce_scatter | solution.py:61
  95.5 0.9 sub.28
  96.5 1.8 scatter_custom_fusion.1
  98.3 9.6 %all-to-all-start.1 = ((f32[128,4,128]{2,1,0:T(4,128)}), f32[128,4,128]{2,1,0:T(4,128)S(1)}, u32[]{:S(2)}, u32[]{:S(2)}) async-start(f32[128,4,128]{2,1,0:T(4,128)} %bitcast.7), calls=%async_computation.2 | async-start | bytes 524288 | tf_op jit(solution)/shard_map/all_to_all | solution.py:86
  108.7 0.8 reduce.3
  109.7 9.4 %all-to-all-done.1 = f32[128,4,128]{2,1,0:T(4,128)S(1)} async-done(((f32[128,4,128]{2,1,0:T(4,128)}), f32[128,4,128]{2,1,0:T(4,128)S(1)}, u32[]{:S(2)}, u32[]{:S(2)}) %all-to-all-start.1) | async-done | bytes 262176 | tf_op jit(solution)/shard_map/all_to_all | solution.py:86
  119.0 2.3 scatter_custom_fusion.2
  121.4 13.4 %all_gather.3 = f32[512,128]{1,0:T(8,128)S(1)} all-gather(f32[64,128]{1,0:T(8,128)S(1)} %slice_add_fusion), channel_id=1, replica_groups=mesh['row'=16,'col'=8] {'col'}, dimensions={0}, use_global_device_ids=true | all-gather | bytes 294912 | tf_op jit(solution)/shard_map/all_gather | solution.py:111
  134.7 2.1 convolution_bitcast_fusion.1
  136.9 79.6 %all-reduce.2.cloned.1.call-done = f32[1024,128]{0,1:T(8,128)} async-done(((f32[1024,128]{0,1:T(8,128)}), f32[1024,128]{0,1:T(8,128)}) %all-reduce.2.cloned.1.call-update) | async-done | bytes 524304 | tf_op jit(solution)/shard_map/psum | solution.py:116
  216.4 7.6 %convolution_bitcast_fusion.2 = f32[1024,128]{0,1:T(8,128)} fusion(f32[1024,128]{0,1:T(8,128)} %all-reduce.2.cloned.1.call-done, f32[1024,1024]{1,0:T(8,128)} %param.15), kind=kOutput, calls=%fused_computation.5 | convolution fusion | flops 1610612736 | bytes 5242880 | tf_op jit(solution)/shard_map/dot_general | solution.py:119
  224.3 1.0 copy.32
  225.3 28.9 %reduce-scatter.5.cloned.1.call-done = f32[128,128]{0,1:T(8,128)} async-done(((f32[1024,128]{0,1:T(8,128)}), f32[128,128]{0,1:T(8,128)}) %reduce-scatter.5.cloned.1.call-update) | async-done | bytes 65552 | tf_op jit(solution)/shard_map/reduce_scatter | solution.py:118
  254.2 0.9 add_subtract_fusion
  255.0 0.7 copy.33
  (49 shorter events, 2.1 us)
Async XLA Ops:
  7.2 127.6 %copy-start = (f32[512,1024]{1,0:T(8,128)S(1)}, f32[512,1024]{1,0:T(8,128)}, u32[]{:S(2)}) copy-start(f32[512,1024]{1,0:T(8,128)} %param.14) | copy-start | bytes 6291460
  7.2 88.3 %reduce-scatter.3.cloned.1.call-start = ((), (), s32[]{:S(2)}) async-start(), calls=%async_computation.4 | async-start | bytes 1179648 | tf_op jit(solution)/shard_map/reduce_scatter | solution.py:61
  12.2 8.5 %collective-permute-start = (f32[1024,64]{0,1:T(8,128)S(1)}, f32[1024,64]{0,1:T(8,128)S(1)}, u32[]{:S(2)}, u32[]{:S(2)}) collective-permute-start(f32[1024,64]{0,1:T(8,128)S(1)} %slice_select_fusion), channel_id=1, source_target_pairs={{0,32},{8,40},{16,48},{24,56},{32,0},{40,8},{48,16},{56,24},{64,96... | collective-permute-start | bytes 786440 | tf_op jit(solution)/shard_map/ppermute | solution.py:12
  20.9 5.4 %collective-permute-start.1 = (f32[1024,32]{0,1:T(8,128)S(1)}, f32[1024,32]{0,1:T(8,128)S(1)}, u32[]{:S(2)}, u32[]{:S(2)}) collective-permute-start(f32[1024,32]{0,1:T(8,128)S(1)} %slice_select_fusion.1), channel_id=1, source_target_pairs={{0,16},{8,24},{16,0},{24,8},{32,48},{40,56},{48,32},{56,40},{64,80... | collective-permute-start | bytes 393224 | tf_op jit(solution)/shard_map/ppermute | solution.py:12
  26.3 3.2 %collective-permute-start.2 = (f32[1024,16]{0,1:T(8,128)S(1)}, f32[1024,16]{0,1:T(8,128)S(1)}, u32[]{:S(2)}, u32[]{:S(2)}) collective-permute-start(f32[1024,16]{0,1:T(8,128)S(1)} %slice_select_fusion.2), channel_id=1, source_target_pairs={{0,8},{8,0},{16,24},{24,16},{32,40},{40,32},{48,56},{56,48},{64,72... | collective-permute-start | bytes 196616 | tf_op jit(solution)/shard_map/ppermute | solution.py:12
  29.5 26.7 %copy-start.2 = (f32[1024,16]{0,1:T(8,128)}, f32[1024,16]{0,1:T(8,128)S(1)}, u32[]{:S(2)}) copy-start(f32[1024,16]{0,1:T(8,128)S(1)} %select_add_fusion.2) | copy-start | bytes 196612
  29.5 3.5 %collective-permute-start.3 = (f32[1024,16]{0,1:T(8,128)S(1)}, f32[1024,16]{0,1:T(8,128)S(1)}, u32[]{:S(2)}, u32[]{:S(2)}) collective-permute-start(f32[1024,16]{0,1:T(8,128)S(1)} %select_add_fusion.2), channel_id=1, source_target_pairs={{0,8},{8,0},{16,24},{24,16},{32,40},{40,32},{48,56},{56,48},{64,72... | collective-permute-start | bytes 196616 | tf_op jit(solution)/shard_map/ppermute | solution.py:12
  33.1 5.4 %collective-permute-start.4 = (f32[1024,32]{0,1:T(8,128)S(1)}, f32[1024,32]{0,1:T(8,128)S(1)}, u32[]{:S(2)}, u32[]{:S(2)}) collective-permute-start(f32[1024,32]{0,1:T(8,128)S(1)} %maximum_select_fusion.3), channel_id=1, source_target_pairs={{0,16},{8,24},{16,0},{24,8},{32,48},{40,56},{48,32},{56,40},{64,80... | collective-permute-start | bytes 393224 | tf_op jit(solution)/shard_map/ppermute | solution.py:12
  38.5 17.8 %copy-start.6 = (s32[256]{0:T(256)S(1)}, s32[256]{0:T(256)}, u32[]{:S(2)}) copy-start(s32[256]{0:T(256)} %param.13) | copy-start | bytes 3076
  38.5 37.8 %copy-start.3 = (f32[256,128]{1,0:T(8,128)S(1)}, f32[256,128]{1,0:T(8,128)}, u32[]{:S(2)}) copy-start(f32[256,128]{1,0:T(8,128)} %param.12) | copy-start | bytes 393220
  38.5 5.8 %collective-permute-start.5 = (f32[1024,64]{0,1:T(8,128)S(1)}, f32[1024,64]{0,1:T(8,128)S(1)}, u32[]{:S(2)}, u32[]{:S(2)}) collective-permute-start(f32[1024,64]{0,1:T(8,128)S(1)} %maximum_select_fusion.2), channel_id=1, source_target_pairs={{0,32},{8,40},{16,48},{24,56},{32,0},{40,8},{48,16},{56,24},{64,96... | collective-permute-start | bytes 786440 | tf_op jit(solution)/shard_map/ppermute | solution.py:12
  56.2 65.1 %copy-start.5 = (f32[64,128]{1,0:T(8,128)S(1)}, f32[64,128]{1,0:T(8,128)}, u32[]{:S(2)}) copy-start(f32[64,128]{1,0:T(8,128)} %param.16) | copy-start | bytes 98308
  59.0 39.3 %all-to-all-start = ((s32[128,1,4]{2,1,0:T(1,128)}), s32[128,1,4]{2,1,0:T(1,128)S(1)}, u32[]{:S(2)}, u32[]{:S(2)}) async-start(s32[128,1,4]{2,1,0:T(1,128)} %bitcast.4), calls=%async_computation | async-start | bytes 131072 | tf_op jit(solution)/shard_map/all_to_all | solution.py:93
  98.3 20.7 %all-to-all-start.1 = ((f32[128,4,128]{2,1,0:T(4,128)}), f32[128,4,128]{2,1,0:T(4,128)S(1)}, u32[]{:S(2)}, u32[]{:S(2)}) async-start(f32[128,4,128]{2,1,0:T(4,128)} %bitcast.7), calls=%async_computation.2 | async-start | bytes 524288 | tf_op jit(solution)/shard_map/all_to_all | solution.py:86
  108.0 108.4 %all-reduce.2.cloned.1.call-start = ((), (), s32[]{:S(2)}) async-start(), calls=%async_computation.5 | async-start | bytes 1048576 | tf_op jit(solution)/shard_map/psum | solution.py:116
  134.7 89.3 %copy-start.4 = (f32[128,128]{1,0:T(8,128)S(1)}, f32[128,128]{1,0:T(8,128)}, u32[]{:S(2)}) copy-start(f32[128,128]{1,0:T(8,128)} %param.17) | copy-start | bytes 196612
  136.8 117.4 %reduce-scatter.5.cloned.1.call-start = ((), (), s32[]{:S(2)}) async-start(), calls=%async_computation.6 | async-start | bytes 589824 | tf_op jit(solution)/shard_map/reduce_scatter | solution.py:118
  216.4 7.8 %copy-start.1 = (f32[1024,128]{0,1:T(8,128)S(1)}, f32[1024,128]{0,1:T(8,128)}, u32[]{:S(2)}) copy-start(f32[1024,128]{0,1:T(8,128)} %all-reduce.2.cloned.1.call-done) | copy-start | bytes 1572868
Sparse Core Ops, SparseCore 0:
  56.4 39.0 reduce-scatter.2
  136.9 79.4 all-reduce.1
  224.2 29.9 reduce-scatter.4
where the time goes:
time: 264 us; the launch traced here: 262 us
  waiting for transfers between devices  156 us (59%)
  starting transfers between devices  40 us (15%)
  matrix products  26.5 us (10%)
  between operations  14 us (5%)
  blocking collectives  13.4 us (5%)
  local copies, waits for them, and re-layouts  6.84 us (3%)
  other arithmetic  5.48 us (2%)
    psum x1, waiting for transfers between devices, local(): parent_solution = lax.psum(partial_sep, 'row')  79.6 us
    reduce_scatter x1, waiting for transfers between devices, local(): lax.psum_scatter(jnp.dot(block_rows, parent_solution, precision=highest,...  28.9 us
    ppermute x6, waiting for transfers between devices, swapped(): return lax.ppermute(value, axis, pairs)  19.1 us
    reduce_scatter x1, waiting for transfers between devices, local(): lax.psum_scatter(jnp.dot(block_rows, current, precision=highest, preferre...  19 us
    all_to_all x1, starting transfers between devices, local(): lax.all_to_all(send_index.reshape(devices_all, capacity), ('row', 'col'),...  17.3 us
    all_gather x1, blocking collectives, local(): lax.all_gather(sep_rows, 'col', axis=0, tiled=True)  13.4 us
    ppermute x6, starting transfers between devices, swapped(): return lax.ppermute(value, axis, pairs)  12.7 us
    dot_general x1, matrix products, local(): jnp.dot(block_rows, current, precision=highest, preferred_element_type=jn...  11.9 us
  transfers between devices with their start and end apart: 11, of which 10 were waited for; matrix products, arithmetic and copies ran while one was open for 3% of the time, Pallas kernels for 0%

commit v1 on v0

v1 whole, which is shorter than its diff:
```python
import jax
import jax.numpy as jnp
from jax import lax
from jax.sharding import Mesh
from jax.sharding import PartitionSpec as P

SP = 8192
ROW = ("h", "r8")
ALL = ("h", "r8", "col")


def reduce_scatter(x, axis, n):
    got = lax.all_to_all(x.reshape(n, x.shape[0] // n, x.shape[1]), axis, 0, 0, tiled=False)
    return got.sum(axis=0)


def gather(x, axis, n):
    got = lax.all_to_all(jnp.broadcast_to(x[None], (n,) + x.shape), axis, 0, 0, tiled=False)
    return got.reshape(n * x.shape[0], x.shape[1])


def local(
    child_inverse,
    child_border,
    child_sep_rhs,
    child_border_rhs,
    child_map,
    parent_inverse,
    parent_border,
    parent_sep_rhs,
    parent_border_rhs,
):
    highest = lax.Precision.HIGHEST
    contract_rows = (((0,), (0,)), ((), ()))
    half_rows = lax.axis_size("r8")
    rows_axis = lax.axis_size("h") * half_rows
    cols_axis = lax.axis_size("col")
    within = lax.axis_index("r8")
    partial_term = lax.dot_general(
        child_inverse,
        child_sep_rhs,
        contract_rows,
        precision=highest,
        preferred_element_type=jnp.float32,
    )
    width_rhs = partial_term.shape[1]
    solved = gather(reduce_scatter(partial_term, "r8", half_rows), "r8", half_rows)
    share = width_rhs // half_rows
    child_part = lax.dynamic_slice_in_dim(solved, within * share, share, axis=1)
    carried = reduce_scatter(
        jnp.dot(child_border, solved, precision=highest, preferred_element_type=jnp.float32),
        "col",
        cols_axis,
    )
    outgoing = child_border_rhs - carried
    devices_all = rows_axis * cols_axis
    sep_dev = parent_sep_rhs.shape[0]
    bord_dev = parent_border_rhs.shape[0]
    rows_src = child_map.shape[0]
    capacity = rows_src // devices_all + 2
    is_sep = child_map < SP
    owner_id = jnp.where(is_sep, child_map // sep_dev, (child_map - SP) // bord_dev)
    target = jnp.where(is_sep, child_map % sep_dev, sep_dev + (child_map - SP) % bord_dev)
    onehot = (owner_id[:, None] == jnp.arange(devices_all, dtype=jnp.int32)[None, :]).astype(
        jnp.int32
    )
    running = jnp.cumsum(onehot, axis=0)
    placed = owner_id * capacity + jnp.sum(onehot * running, axis=1) - 1
    send_rows = jnp.zeros((devices_all * capacity, width_rhs), jnp.float32).at[placed].set(outgoing)
    send_index = (
        jnp.full((devices_all * capacity,), sep_dev + bord_dev, jnp.int32).at[placed].set(target)
    )
    got_rows = lax.all_to_all(
        send_rows.reshape(devices_all, capacity, width_rhs), ALL, 0, 0, tiled=True
    )
    got_index = lax.all_to_all(send_index.reshape(devices_all, capacity), ALL, 0, 0, tiled=True)
    received = (
        jnp.zeros((sep_dev + bord_dev, width_rhs), jnp.float32)
        .at[got_index.reshape(-1)]
        .add(got_rows.reshape(-1, width_rhs), mode="drop")
    )
    sep_rows = parent_sep_rhs + received[:sep_dev]
    border_rows = parent_border_rhs + received[sep_dev:]
    partial_sep = lax.dot_general(
        parent_inverse,
        gather(sep_rows, "col", cols_axis),
        contract_rows,
        precision=highest,
        preferred_element_type=jnp.float32,
    )
    parent_solution = gather(reduce_scatter(partial_sep, ROW, rows_axis), ROW, rows_axis)
    carried_parent = reduce_scatter(
        jnp.dot(parent_border, parent_solution, precision=highest, preferred_element_type=jnp.float32),
        "col",
        cols_axis,
    )
    parent_contribution = border_rows - carried_parent
    return (child_part, parent_solution, parent_contribution)


def solution(mesh):
    rows, cols = mesh.devices.shape
    split = Mesh(mesh.devices.reshape(2, rows // 2, cols), ("h", "r8", "col"))
    placed = (
        P(ROW, "col"),
        P(ROW, "col"),
        P(ROW, None),
        P(ALL, None),
        P(ALL),
        P(ROW, "col"),
        P(ROW, "col"),
        P(ALL, None),
        P(ALL, None),
    )
    return jax.shard_map(
        local,
        mesh=split,
        in_specs=placed,
        out_specs=(P("col", ROW), P("col", None), P(ALL, None)),
        check_vma=False,
    )
```

time: 264 us -> 172 us (0.65)
  waiting for transfers between devices: 156 us -> 44.3 us
  blocking collectives: 13.4 us -> 52.1 us
  starting transfers between devices: 40 us -> 26.7 us
  between operations: 14 us -> 0.91 us
  local copies, waits for them, and re-layouts: 6.84 us -> 12.8 us
    psum x1 -> x0, waiting for transfers between devices: 79.6 us -> none  [local(): parent_solution = lax.psum(partial_sep, 'row')]
    all_to_all x0 -> x4, blocking collectives: none -> 52.1 us  [the longest x2 29.4 us: reduce_scatter(): lax.all_to_all(x.reshape(n, x.shape[0] // n, x.shape[1]), axis, 0, 0, til...]
    reduce_scatter x2 -> x0, waiting for transfers between devices: 48 us -> none  [the longest x1 28.9 us: local(): lax.psum_scatter(jnp.dot(block_rows, parent_solution, precision=highest,...]
    all_to_all x2 -> x5, waiting for transfers between devices: 9.4 us -> 44.3 us  [the longest x2 19.1 us: reduce_scatter(): lax.all_to_all(x.reshape(n, x.shape[0] // n, x.shape[1]), axis, 0, 0, til...]
    ppermute x6 -> x0, waiting for transfers between devices: 19.1 us -> none  [swapped(): return lax.ppermute(value, axis, pairs)]
    all_gather x1 -> x0, blocking collectives: 13.4 us -> none  [local(): lax.all_gather(sep_rows, 'col', axis=0, tiled=True)]
    ppermute x6 -> x0, starting transfers between devices: 12.7 us -> none  [swapped(): return lax.ppermute(value, axis, pairs)]
    dot_general x1, matrix products: 4.96 us -> 8.7 us  [local(): lax.dot_general(child_inverse, child_sep_rhs, contract_rows, precision=hi...]
  transfers between devices with their start and end apart: 11 -> 5, of which waited for: 10 -> 5; matrix products, arithmetic and copies ran while one was open for 3% -> 6% of each run, Pallas kernels for 0% -> 0%
where the time goes in v1:
time: 172 us; the launch traced here: 171 us
  blocking collectives  52.1 us (30%)
  waiting for transfers between devices  44.3 us (26%)
  matrix products  27.9 us (16%)
  starting transfers between devices  26.7 us (16%)
  local copies, waits for them, and re-layouts  12.8 us (7%)
  other arithmetic  6.65 us (4%)
    all_to_all x2, blocking collectives, reduce_scatter(): lax.all_to_all(x.reshape(n, x.shape[0] // n, x.shape[1]), axis, 0, 0, til...  29.4 us
    all_to_all x2, blocking collectives, gather(): lax.all_to_all(jnp.broadcast_to(x[None], (n,) + x.shape), axis, 0, 0, til...  22.6 us
    all_to_all x2, waiting for transfers between devices, reduce_scatter(): lax.all_to_all(x.reshape(n, x.shape[0] // n, x.shape[1]), axis, 0, 0, til...  19.1 us
    all_to_all x2, starting transfers between devices, reduce_scatter(): lax.all_to_all(x.reshape(n, x.shape[0] // n, x.shape[1]), axis, 0, 0, til...  12.3 us
    dot_general x1, matrix products, local(): jnp.dot(child_border, solved, precision=highest, preferred_element_type=j...  11.2 us
    all_to_all x1, waiting for transfers between devices, local(): lax.all_to_all(send_rows.reshape(devices_all, capacity, width_rhs), ALL,...  9.62 us
    all_to_all x1, waiting for transfers between devices, gather(): lax.all_to_all(jnp.broadcast_to(x[None], (n,) + x.shape), axis, 0, 0, til...  9.36 us
    dot_general x1, matrix products, local(): lax.dot_general(child_inverse, child_sep_rhs, contract_rows, precision=hi...  8.7 us
  transfers between devices with their start and end apart: 5, of which 5 were waited for; matrix products, arithmetic and copies ran while one was open for 6% of the time, Pallas kernels for 0%

profile of v1, /device:TPU:1, one launch (start us, length us, event | category | flops | bytes accessed | tf_op | source)
XLA Modules:
  0.0 171.2 jit_solution(8010269458104946515)
XLA Ops:
  0.7 8.7 %fusion.14 = f32[1024,128]{1,0:T(8,128)S(1)} fusion(f32[1024,1024]{1,0:T(8,128)} %param.9, f32[1024,128]{1,0:T(8,128)} %param.11), kind=kOutput, calls=%fused_computation.46 | convolution fusion | flops 1610612736 | bytes 5242880 | tf_op jit(solution)/shard_map/dot_general | solution.py:39
  9.4 15.4 %all_to_all.49 = f32[8,128,128]{2,1,0:T(8,128)S(1)} all-to-all(f32[8,128,128]{2,1,0:T(8,128)S(1)} %bitcast.50), channel_id=1, replica_groups=mesh['h'=2,'r8'=8,'col'=8] {'r8'}, dimensions={0} | all-to-all | bytes 1048576 | tf_op jit(solution)/shard_map/all_to_all | solution.py:13
  24.9 0.8 broadcast_in_dim.12
  25.7 3.5 %all-to-all-start.1 = ((f32[8,128,128]{1,2,0:T(8,128)}), f32[8,128,128]{1,2,0:T(8,128)S(1)}, u32[]{:S(2)}, u32[]{:S(2)}) async-start(f32[8,128,128]{1,2,0:T(8,128)} %broadcast_in_dim.12), calls=%async_computation.1 | async-start | bytes 1048576 | tf_op jit(solution)/shard_map/all_to_all | solution.py:18
  29.4 9.4 %all-to-all-done.1 = f32[8,128,128]{1,2,0:T(8,128)S(1)} async-done(((f32[8,128,128]{1,2,0:T(8,128)}), f32[8,128,128]{1,2,0:T(8,128)S(1)}, u32[]{:S(2)}, u32[]{:S(2)}) %all-to-all-start.1) | async-done | bytes 524320 | tf_op jit(solution)/shard_map/all_to_all | solution.py:18
  38.9 11.2 %fusion.15 = f32[128,2048]{1,0:T(8,128)S(1)} fusion(f32[1024,128]{1,0:T(8,128)S(1)} %bitcast.44, f32[2048,1024]{1,0:T(8,128)} %param.10), kind=kOutput, calls=%fused_computation.47 | convolution fusion | flops 3221225472 | bytes 9961472 | tf_op jit(solution)/shard_map/dot_general | solution.py:51
  50.2 1.1 copy.47
  51.3 5.8 %all-to-all-start.3 = ((f32[8,256,128]{1,2,0:T(8,128)}), f32[8,256,128]{1,2,0:T(8,128)}, u32[]{:S(2)}, u32[]{:S(2)}) async-start(f32[8,256,128]{1,2,0:T(8,128)} %bitcast.49), calls=%async_computation.3 | async-start | bytes 2097152 | tf_op jit(solution)/shard_map/all_to_all | solution.py:13
  57.5 1.4 scatter_custom_fusion
  58.9 0.7 all_to_all.32
  59.7 12.4 %all-to-all-done.3 = f32[8,256,128]{1,2,0:T(8,128)} async-done(((f32[8,256,128]{1,2,0:T(8,128)}), f32[8,256,128]{1,2,0:T(8,128)}, u32[]{:S(2)}, u32[]{:S(2)}) %all-to-all-start.3) | async-done | bytes 1048608 | tf_op jit(solution)/shard_map/all_to_all | solution.py:13
  72.1 6.4 %all-to-all-start.2 = ((s32[128,1,4]{2,1,0:T(1,128)}), s32[128,1,4]{2,1,0:T(1,128)S(1)}, u32[]{:S(2)}, u32[]{:S(2)}) async-start(s32[128,1,4]{2,1,0:T(1,128)} %bitcast.6), calls=%async_computation.2 | async-start | bytes 131072 | tf_op jit(solution)/shard_map/all_to_all | solution.py:76
  78.6 1.3 reduce_sum.47
  80.0 1.8 %scatter_custom_fusion.1 = f32[512,128]{1,0:T(8,128)} fusion(s32[256]{0:T(256)S(1)} %compare_select_fusion.1, f32[256,128]{1,0:T(8,128)S(1)} %copy.35, f32[]{:T(128)} %constant.62.clone.1), kind=kCustom, calls=%fused_computation.11 | custom fusion | bytes 262148 | tf_op jit(solution)/shard_map/scatter | solution.py:69
  81.9 6.2 %all-to-all-done.2 = s32[128,1,4]{2,1,0:T(1,128)S(1)} async-done(((s32[128,1,4]{2,1,0:T(1,128)}), s32[128,1,4]{2,1,0:T(1,128)S(1)}, u32[]{:S(2)}, u32[]{:S(2)}) %all-to-all-start.2) | async-done | bytes 2080 | tf_op jit(solution)/shard_map/all_to_all | solution.py:76
  88.0 4.5 %all-to-all-start.4 = ((f32[128,4,128]{2,1,0:T(4,128)}), f32[128,4,128]{2,1,0:T(4,128)S(1)}, u32[]{:S(2)}, u32[]{:S(2)}) async-start(f32[128,4,128]{2,1,0:T(4,128)} %bitcast.9), calls=%async_computation.4 | async-start | bytes 524288 | tf_op jit(solution)/shard_map/all_to_all | solution.py:73
  93.1 0.8 reduce.3
  94.0 9.6 %all-to-all-done.4 = f32[128,4,128]{2,1,0:T(4,128)S(1)} async-done(((f32[128,4,128]{2,1,0:T(4,128)}), f32[128,4,128]{2,1,0:T(4,128)S(1)}, u32[]{:S(2)}, u32[]{:S(2)}) %all-to-all-start.4) | async-done | bytes 262176 | tf_op jit(solution)/shard_map/all_to_all | solution.py:73
  103.6 2.3 %scatter_custom_fusion.2 = f32[192,128]{1,0:T(8,128)S(1)} fusion(s32[512]{0:T(512)S(1)} %bitcast.59, f32[512,128]{1,0:T(8,128)S(1)} %bitcast.56, f32[]{:T(128)} %constant.62.clone.1), kind=kCustom, calls=%fused_computation.19 | custom fusion | flops 65536 | bytes 98308 | tf_op jit(solution)/shard_map/scatter-add | solution.py:80
  106.0 9.6 %all_to_all.50 = f32[8,64,128]{2,1,0:T(8,128)S(1)} all-to-all(f32[8,64,128]{2,1,0:T(8,128)S(1)} %broadcast_in_dim.16), channel_id=1, replica_groups=mesh['h'=2,'r8'=8,'col'=8] {'col'}, dimensions={0} | all-to-all | bytes 524288 | tf_op jit(solution)/shard_map/all_to_all | solution.py:18
  115.5 1.3 convolution_bitcast_fusion
  116.8 1.0 copy.36
  117.8 14.1 %all_to_all.51 = f32[16,64,128]{2,1,0:T(8,128)S(1)} all-to-all(f32[16,64,128]{2,1,0:T(8,128)} %bitcast.52), channel_id=1, replica_groups=mesh['h'=2,'r8'=8,'col'=8] {'h','r8'}, dimensions={0} | all-to-all | bytes 1048576 | tf_op jit(solution)/shard_map/all_to_all | solution.py:13
  132.0 13.1 %all_to_all.52 = f32[16,64,128]{2,1,0:T(8,128)S(1)} all-to-all(f32[16,64,128]{2,1,0:T(8,128)S(1)} %broadcast_in_dim.17), channel_id=1, replica_groups=mesh['h'=2,'r8'=8,'col'=8] {'h','r8'}, dimensions={0} | all-to-all | bytes 1048576 | tf_op jit(solution)/shard_map/all_to_all | solution.py:18
  145.0 6.7 %convolution_bitcast_fusion.1 = f32[16,8,8,128]{3,2,1,0:T(8,128)S(1)} fusion(f32[1024,128]{1,0:T(8,128)S(1)} %bitcast.46, f32[1024,1024]{1,0:T(8,128)} %param.15), kind=kOutput, calls=%fused_computation.4 | convolution fusion | flops 1610612736 | bytes 5242880 | tf_op jit(solution)/shard_map/dot_general | solution.py:93
  151.7 0.8 copy.48
  152.6 6.5 %all-to-all-start.8 = ((f32[8,128,128]{1,2,0:T(8,128)}), f32[8,128,128]{1,2,0:T(8,128)}, u32[]{:S(2)}, u32[]{:S(2)}) async-start(f32[8,128,128]{1,2,0:T(8,128)} %bitcast.51), calls=%async_computation.8 | async-start | bytes 1048576 | tf_op jit(solution)/shard_map/all_to_all | solution.py:13
  159.1 1.0 constant_dynamic-slice_fusion
  160.1 1.8 %copy.40 = f32[1024,16]{0,1:T(8,128)} copy(f32[1024,16]{1,0:T(8,128)} %constant_dynamic-slice_fusion) | data formatting | bytes 131072
  162.0 6.6 %all-to-all-done.8 = f32[8,128,128]{1,2,0:T(8,128)} async-done(((f32[8,128,128]{1,2,0:T(8,128)}), f32[8,128,128]{1,2,0:T(8,128)}, u32[]{:S(2)}, u32[]{:S(2)}) %all-to-all-start.8) | async-done | bytes 524320 | tf_op jit(solution)/shard_map/all_to_all | solution.py:13
  168.6 1.1 reduce_sum.49
  170.4 0.8 copy.50
  (36 shorter events, 2.6 us)
Async XLA Ops:
  0.6 114.9 %copy-start = (f32[512,1024]{1,0:T(8,128)S(1)}, f32[512,1024]{1,0:T(8,128)}, u32[]{:S(2)}) copy-start(f32[512,1024]{1,0:T(8,128)} %param.14) | copy-start | bytes 6291460
  0.6 28.6 %copy-start.4 = (s32[256]{0:T(256)S(1)}, s32[256]{0:T(256)}, u32[]{:S(2)}) copy-start(s32[256]{0:T(256)} %param.13) | copy-start | bytes 3076
  25.7 13.0 %all-to-all-start.1 = ((f32[8,128,128]{1,2,0:T(8,128)}), f32[8,128,128]{1,2,0:T(8,128)S(1)}, u32[]{:S(2)}, u32[]{:S(2)}) async-start(f32[8,128,128]{1,2,0:T(8,128)} %broadcast_in_dim.12), calls=%async_computation.1 | async-start | bytes 1048576 | tf_op jit(solution)/shard_map/all_to_all | solution.py:18
  50.1 28.4 %copy-start.1 = (f32[256,128]{1,0:T(8,128)S(1)}, f32[256,128]{1,0:T(8,128)}, u32[]{:S(2)}) copy-start(f32[256,128]{1,0:T(8,128)} %param.12) | copy-start | bytes 393220
  50.1 55.8 %copy-start.3 = (f32[64,128]{1,0:T(8,128)S(1)}, f32[64,128]{1,0:T(8,128)}, u32[]{:S(2)}) copy-start(f32[64,128]{1,0:T(8,128)} %param.16) | copy-start | bytes 98308
  51.3 20.8 %all-to-all-start.3 = ((f32[8,256,128]{1,2,0:T(8,128)}), f32[8,256,128]{1,2,0:T(8,128)}, u32[]{:S(2)}, u32[]{:S(2)}) async-start(f32[8,256,128]{1,2,0:T(8,128)} %bitcast.49), calls=%async_computation.3 | async-start | bytes 2097152 | tf_op jit(solution)/shard_map/all_to_all | solution.py:13
  72.1 15.9 %all-to-all-start.2 = ((s32[128,1,4]{2,1,0:T(1,128)}), s32[128,1,4]{2,1,0:T(1,128)S(1)}, u32[]{:S(2)}, u32[]{:S(2)}) async-start(s32[128,1,4]{2,1,0:T(1,128)} %bitcast.6), calls=%async_computation.2 | async-start | bytes 131072 | tf_op jit(solution)/shard_map/all_to_all | solution.py:76
  88.0 15.6 %all-to-all-start.4 = ((f32[128,4,128]{2,1,0:T(4,128)}), f32[128,4,128]{2,1,0:T(4,128)S(1)}, u32[]{:S(2)}, u32[]{:S(2)}) async-start(f32[128,4,128]{2,1,0:T(4,128)} %bitcast.9), calls=%async_computation.4 | async-start | bytes 524288 | tf_op jit(solution)/shard_map/all_to_all | solution.py:73
  145.0 24.8 %copy-start.2 = (f32[128,128]{1,0:T(8,128)S(1)}, f32[128,128]{1,0:T(8,128)}, u32[]{:S(2)}) copy-start(f32[128,128]{1,0:T(8,128)} %param.17) | copy-start | bytes 196612
  152.6 16.0 %all-to-all-start.8 = ((f32[8,128,128]{1,2,0:T(8,128)}), f32[8,128,128]{1,2,0:T(8,128)}, u32[]{:S(2)}, u32[]{:S(2)}) async-start(f32[8,128,128]{1,2,0:T(8,128)} %bitcast.51), calls=%async_computation.8 | async-start | bytes 1048576 | tf_op jit(solution)/shard_map/all_to_all | solution.py:13

commit v2 on v1

--- a/solution.py
+++ b/solution.py
@@ -70,10 +70,15 @@
     send_index = (
         jnp.full((devices_all * capacity,), sep_dev + bord_dev, jnp.int32).at[placed].set(target)
     )
-    got_rows = lax.all_to_all(
-        send_rows.reshape(devices_all, capacity, width_rhs), ALL, 0, 0, tiled=True
+    index_row = jnp.zeros((devices_all, 1, width_rhs), jnp.float32).at[:, 0, :capacity].set(
+        send_index.reshape(devices_all, capacity).astype(jnp.float32)
     )
-    got_index = lax.all_to_all(send_index.reshape(devices_all, capacity), ALL, 0, 0, tiled=True)
+    packed = jnp.concatenate(
+        [send_rows.reshape(devices_all, capacity, width_rhs), index_row], axis=1
+    )
+    got = lax.all_to_all(packed, ALL, 0, 0, tiled=True)
+    got_rows = got[:, :capacity]
+    got_index = got[:, capacity, :capacity].astype(jnp.int32)
     received = (
         jnp.zeros((sep_dev + bord_dev, width_rhs), jnp.float32)
         .at[got_index.reshape(-1)]

time: 172 us -> 164 us (0.953)
  blocking collectives: 52.1 us -> 72.1 us
  waiting for transfers between devices: 44.3 us -> 28.9 us
  starting transfers between devices: 26.7 us -> 15.9 us
    all_to_all x0 -> x1, blocking collectives: none -> 19.8 us  [local(): got = lax.all_to_all(packed, ALL, 0, 0, tiled=True)]
    all_to_all x2 -> x0, waiting for transfers between devices: 15.8 us -> none  [the longest x1 9.62 us: local(): lax.all_to_all(send_rows.reshape(devices_all, capacity, width_rhs), ALL,...]
    all_to_all x2 -> x0, starting transfers between devices: 10.9 us -> none  [the longest x1 6.36 us: local(): lax.all_to_all(send_index.reshape(devices_all, capacity), ALL, 0, 0, tile...]
  transfers between devices with their start and end apart: 5 -> 3, of which waited for: 5 -> 3; matrix products, arithmetic and copies ran while one was open for 6% -> 3% of each run, Pallas kernels for 0% -> 0%
where the time goes in v2:
time: 164 us; the launch traced here: 163 us
  blocking collectives  72.1 us (44%)
  waiting for transfers between devices  28.9 us (18%)
  matrix products  27.9 us (17%)
  starting transfers between devices  15.9 us (10%)
  local copies, waits for them, and re-layouts  11.1 us (7%)
  other arithmetic  6.18 us (4%)
    all_to_all x2, blocking collectives, reduce_scatter(): lax.all_to_all(x.reshape(n, x.shape[0] // n, x.shape[1]), axis, 0, 0, til...  29.4 us
    all_to_all x2, blocking collectives, gather(): lax.all_to_all(jnp.broadcast_to(x[None], (n,) + x.shape), axis, 0, 0, til...  22.9 us
    all_to_all x1, blocking collectives, local(): got = lax.all_to_all(packed, ALL, 0, 0, tiled=True)  19.8 us
    all_to_all x2, waiting for transfers between devices, reduce_scatter(): lax.all_to_all(x.reshape(n, x.shape[0] // n, x.shape[1]), axis, 0, 0, til...  19.6 us
    all_to_all x2, starting transfers between devices, reduce_scatter(): lax.all_to_all(x.reshape(n, x.shape[0] // n, x.shape[1]), axis, 0, 0, til...  12.4 us
    dot_general x1, matrix products, local(): jnp.dot(child_border, solved, precision=highest, preferred_element_type=j...  11.2 us
    all_to_all x1, waiting for transfers between devices, gather(): lax.all_to_all(jnp.broadcast_to(x[None], (n,) + x.shape), axis, 0, 0, til...  9.36 us
    dot_general x1, matrix products, local(): lax.dot_general(child_inverse, child_sep_rhs, contract_rows, precision=hi...  8.7 us
  transfers between devices with their start and end apart: 3, of which 3 were waited for; matrix products, arithmetic and copies ran while one was open for 3% of the time, Pallas kernels for 0%

profile of v2, /device:TPU:1, one launch (start us, length us, event | category | flops | bytes accessed | tf_op | source)
XLA Modules:
  0.0 163.1 jit_solution(16856010376624821868)
XLA Ops:
  0.7 8.7 %fusion.15 = f32[1024,128]{1,0:T(8,128)S(1)} fusion(f32[1024,1024]{1,0:T(8,128)} %param.11, f32[1024,128]{1,0:T(8,128)} %param.13), kind=kOutput, calls=%fused_computation.49 | convolution fusion | flops 1610612736 | bytes 5242880 | tf_op jit(solution)/shard_map/dot_general | solution.py:39
  9.4 15.4 %all_to_all.40 = f32[8,128,128]{2,1,0:T(8,128)S(1)} all-to-all(f32[8,128,128]{2,1,0:T(8,128)S(1)} %bitcast.50), channel_id=1, replica_groups=mesh['h'=2,'r8'=8,'col'=8] {'r8'}, dimensions={0} | all-to-all | bytes 1048576 | tf_op jit(solution)/shard_map/all_to_all | solution.py:13
  24.9 0.8 broadcast_in_dim.12
  25.7 3.5 %all-to-all-start.1 = ((f32[8,128,128]{1,2,0:T(8,128)}), f32[8,128,128]{1,2,0:T(8,128)S(1)}, u32[]{:S(2)}, u32[]{:S(2)}) async-start(f32[8,128,128]{1,2,0:T(8,128)} %broadcast_in_dim.12), calls=%async_computation.1 | async-start | bytes 1048576 | tf_op jit(solution)/shard_map/all_to_all | solution.py:18
  29.4 9.4 %all-to-all-done.1 = f32[8,128,128]{1,2,0:T(8,128)S(1)} async-done(((f32[8,128,128]{1,2,0:T(8,128)}), f32[8,128,128]{1,2,0:T(8,128)S(1)}, u32[]{:S(2)}, u32[]{:S(2)}) %all-to-all-start.1) | async-done | bytes 524320 | tf_op jit(solution)/shard_map/all_to_all | solution.py:18
  38.7 0.2 copy.33
  38.9 11.2 %fusion.16 = f32[128,2048]{1,0:T(8,128)S(1)} fusion(f32[1024,128]{1,0:T(8,128)S(1)} %bitcast.44, f32[2048,1024]{1,0:T(8,128)} %param.12), kind=kOutput, calls=%fused_computation.50 | convolution fusion | flops 3221225472 | bytes 9961472 | tf_op jit(solution)/shard_map/dot_general | solution.py:51
  50.1 1.1 copy.52
  51.3 5.9 %all-to-all-start.2 = ((f32[8,256,128]{1,2,0:T(8,128)}), f32[8,256,128]{1,2,0:T(8,128)}, u32[]{:S(2)}, u32[]{:S(2)}) async-start(f32[8,256,128]{1,2,0:T(8,128)} %bitcast.49), calls=%async_computation.2 | async-start | bytes 2097152 | tf_op jit(solution)/shard_map/all_to_all | solution.py:13
  57.2 0.2 fusion
  57.5 0.2 fusion.1
  57.7 1.4 scatter_custom_fusion.1
  59.3 12.9 %all-to-all-done.2 = f32[8,256,128]{1,2,0:T(8,128)} async-done(((f32[8,256,128]{1,2,0:T(8,128)}), f32[8,256,128]{1,2,0:T(8,128)}, u32[]{:S(2)}, u32[]{:S(2)}) %all-to-all-start.2) | async-done | bytes 1048608 | tf_op jit(solution)/shard_map/all_to_all | solution.py:13
  72.2 1.3 reduce_sum.47
  73.7 1.2 scatter_custom_fusion
  75.0 19.8 %all_to_all.41 = f32[128,5,128]{2,1,0:T(8,128)S(1)} all-to-all(f32[128,5,128]{2,1,0:T(8,128)S(1)} %pad_maximum_fusion), channel_id=1, replica_groups=mesh['h'=2,'r8'=8,'col'=8] {'h','r8','col'}, dimensions={0} | all-to-all | bytes 655360 | tf_op jit(solution)/shard_map/all_to_all | solution.py:79
  94.8 0.2 fusion.6
  95.2 2.3 %scatter_custom_fusion.2 = f32[192,128]{1,0:T(8,128)S(1)} fusion(s32[512]{0:T(512)S(1)} %bitcast.61, f32[512,128]{1,0:T(8,128)S(1)} %bitcast.57, f32[]{:T(128)} %constant.91.clone.1), kind=kCustom, calls=%fused_computation.22 | custom fusion | flops 65536 | bytes 98308 | tf_op jit(solution)/shard_map/scatter-add | solution.py:85
  97.5 9.8 %all_to_all.42 = f32[8,64,128]{2,1,0:T(8,128)S(1)} all-to-all(f32[8,64,128]{2,1,0:T(8,128)S(1)} %broadcast_in_dim.16), channel_id=1, replica_groups=mesh['h'=2,'r8'=8,'col'=8] {'col'}, dimensions={0} | all-to-all | bytes 524288 | tf_op jit(solution)/shard_map/all_to_all | solution.py:18
  107.4 1.3 convolution_bitcast_fusion
  108.7 1.0 copy.41
  109.7 14.1 %all_to_all.43 = f32[16,64,128]{2,1,0:T(8,128)S(1)} all-to-all(f32[16,64,128]{2,1,0:T(8,128)} %bitcast.52), channel_id=1, replica_groups=mesh['h'=2,'r8'=8,'col'=8] {'h','r8'}, dimensions={0} | all-to-all | bytes 1048576 | tf_op jit(solution)/shard_map/all_to_all | solution.py:13
  123.8 13.1 %all_to_all.44 = f32[16,64,128]{2,1,0:T(8,128)S(1)} all-to-all(f32[16,64,128]{2,1,0:T(8,128)S(1)} %broadcast_in_dim.17), channel_id=1, replica_groups=mesh['h'=2,'r8'=8,'col'=8] {'h','r8'}, dimensions={0} | all-to-all | bytes 1048576 | tf_op jit(solution)/shard_map/all_to_all | solution.py:18
  136.9 6.7 %convolution_bitcast_fusion.1 = f32[16,8,8,128]{3,2,1,0:T(8,128)S(1)} fusion(f32[1024,128]{1,0:T(8,128)S(1)} %bitcast.46, f32[1024,1024]{1,0:T(8,128)} %param.17), kind=kOutput, calls=%fused_computation.4 | convolution fusion | flops 1610612736 | bytes 5242880 | tf_op jit(solution)/shard_map/dot_general | solution.py:98
  143.6 0.8 copy.53
  144.4 6.5 %all-to-all-start.7 = ((f32[8,128,128]{1,2,0:T(8,128)}), f32[8,128,128]{1,2,0:T(8,128)}, u32[]{:S(2)}, u32[]{:S(2)}) async-start(f32[8,128,128]{1,2,0:T(8,128)} %bitcast.51), calls=%async_computation.7 | async-start | bytes 1048576 | tf_op jit(solution)/shard_map/all_to_all | solution.py:13
  151.0 1.0 constant_dynamic-slice_fusion
  152.0 1.8 %copy.45 = f32[1024,16]{0,1:T(8,128)} copy(f32[1024,16]{1,0:T(8,128)} %constant_dynamic-slice_fusion) | data formatting | bytes 131072
  153.8 6.6 %all-to-all-done.7 = f32[8,128,128]{1,2,0:T(8,128)} async-done(((f32[8,128,128]{1,2,0:T(8,128)}), f32[8,128,128]{1,2,0:T(8,128)}, u32[]{:S(2)}, u32[]{:S(2)}) %all-to-all-start.7) | async-done | bytes 524320 | tf_op jit(solution)/shard_map/all_to_all | solution.py:13
  160.4 1.1 reduce_sum.49
  161.6 0.6 fusion.5
  162.3 0.8 copy.55
  (36 shorter events, 1.1 us)
Async XLA Ops:
  0.6 106.7 %copy-start = (f32[512,1024]{1,0:T(8,128)S(1)}, f32[512,1024]{1,0:T(8,128)}, u32[]{:S(2)}) copy-start(f32[512,1024]{1,0:T(8,128)} %param.16) | copy-start | bytes 6291460
  0.6 28.6 %copy-start.4 = (s32[256]{0:T(256)S(1)}, s32[256]{0:T(256)}, u32[]{:S(2)}) copy-start(s32[256]{0:T(256)} %param.15) | copy-start | bytes 3076
  25.7 13.0 %all-to-all-start.1 = ((f32[8,128,128]{1,2,0:T(8,128)}), f32[8,128,128]{1,2,0:T(8,128)S(1)}, u32[]{:S(2)}, u32[]{:S(2)}) async-start(f32[8,128,128]{1,2,0:T(8,128)} %broadcast_in_dim.12), calls=%async_computation.1 | async-start | bytes 1048576 | tf_op jit(solution)/shard_map/all_to_all | solution.py:18
  50.1 9.1 %copy-start.1 = (f32[256,128]{1,0:T(8,128)S(1)}, f32[256,128]{1,0:T(8,128)}, u32[]{:S(2)}) copy-start(f32[256,128]{1,0:T(8,128)} %param.14) | copy-start | bytes 393220
  51.3 46.2 %copy-start.3 = (f32[64,128]{1,0:T(8,128)S(1)}, f32[64,128]{1,0:T(8,128)}, u32[]{:S(2)}) copy-start(f32[64,128]{1,0:T(8,128)} %param.18) | copy-start | bytes 98308
  51.3 21.0 %all-to-all-start.2 = ((f32[8,256,128]{1,2,0:T(8,128)}), f32[8,256,128]{1,2,0:T(8,128)}, u32[]{:S(2)}, u32[]{:S(2)}) async-start(f32[8,256,128]{1,2,0:T(8,128)} %bitcast.49), calls=%async_computation.2 | async-start | bytes 2097152 | tf_op jit(solution)/shard_map/all_to_all | solution.py:13
  136.9 24.7 %copy-start.2 = (f32[128,128]{1,0:T(8,128)S(1)}, f32[128,128]{1,0:T(8,128)}, u32[]{:S(2)}) copy-start(f32[128,128]{1,0:T(8,128)} %param.19) | copy-start | bytes 196612
  144.4 16.0 %all-to-all-start.7 = ((f32[8,128,128]{1,2,0:T(8,128)}), f32[8,128,128]{1,2,0:T(8,128)}, u32[]{:S(2)}, u32[]{:S(2)}) async-start(f32[8,128,128]{1,2,0:T(8,128)} %bitcast.51), calls=%async_computation.7 | async-start | bytes 1048576 | tf_op jit(solution)/shard_map/all_to_all | solution.py:13

commit v3 on v2

--- a/solution.py
+++ b/solution.py
@@ -30,7 +30,7 @@
     parent_sep_rhs,
     parent_border_rhs,
 ):
-    highest = lax.Precision.HIGHEST
+    highest = lax.Precision.HIGH
     contract_rows = (((0,), (0,)), ((), ()))
     half_rows = lax.axis_size("r8")
     rows_axis = lax.axis_size("h") * half_rows

time: 164 us -> 155 us (0.945)
  matrix products: 27.9 us -> 18.8 us
    dot_general x1, matrix products: 11.2 us -> 7.73 us  [local(): jnp.dot(child_border, solved, precision=highest, preferred_element_type=j...]
    dot_general x1, matrix products: 8.7 us -> 5.88 us  [local(): lax.dot_general(child_inverse, child_sep_rhs, contract_rows, precision=hi...]
    dot_general x1, matrix products: 6.69 us -> 4.48 us  [local(): jnp.dot(parent_border, parent_solution, precision=highest, preferred_elem...]
where the time goes in v3:
time: 155 us; the launch traced here: 154 us
  blocking collectives  72.1 us (47%)
  waiting for transfers between devices  28.9 us (19%)
  matrix products  18.8 us (12%)
  starting transfers between devices  15.9 us (10%)
  local copies, waits for them, and re-layouts  11.1 us (7%)
  other arithmetic  6.18 us (4%)
    all_to_all x2, blocking collectives, reduce_scatter(): lax.all_to_all(x.reshape(n, x.shape[0] // n, x.shape[1]), axis, 0, 0, til...  29.4 us
    all_to_all x2, blocking collectives, gather(): lax.all_to_all(jnp.broadcast_to(x[None], (n,) + x.shape), axis, 0, 0, til...  22.9 us
    all_to_all x1, blocking collectives, local(): got = lax.all_to_all(packed, ALL, 0, 0, tiled=True)  19.8 us
    all_to_all x2, waiting for transfers between devices, reduce_scatter(): lax.all_to_all(x.reshape(n, x.shape[0] // n, x.shape[1]), axis, 0, 0, til...  19.6 us
    all_to_all x2, starting transfers between devices, reduce_scatter(): lax.all_to_all(x.reshape(n, x.shape[0] // n, x.shape[1]), axis, 0, 0, til...  12.4 us
    all_to_all x1, waiting for transfers between devices, gather(): lax.all_to_all(jnp.broadcast_to(x[None], (n,) + x.shape), axis, 0, 0, til...  9.36 us
    dot_general x1, matrix products, local(): jnp.dot(child_border, solved, precision=highest, preferred_element_type=j...  7.73 us
    dot_general x1, matrix products, local(): lax.dot_general(child_inverse, child_sep_rhs, contract_rows, precision=hi...  5.88 us
  transfers between devices with their start and end apart: 3, of which 3 were waited for; matrix products, arithmetic and copies ran while one was open for 3% of the time, Pallas kernels for 0%

profile of v3, /device:TPU:1, one launch (start us, length us, event | category | flops | bytes accessed | tf_op | source)
XLA Modules:
  0.0 154.0 jit_solution(3160338599321913607)
XLA Ops:
  0.7 5.9 %fusion.15 = f32[1024,128]{1,0:T(8,128)S(1)} fusion(f32[1024,1024]{1,0:T(8,128)} %param.11, f32[1024,128]{1,0:T(8,128)} %param.13), kind=kOutput, calls=%fused_computation.49 | convolution fusion | flops 805306368 | bytes 5242880 | tf_op jit(solution)/shard_map/dot_general | solution.py:39
  6.5 15.4 %all_to_all.40 = f32[8,128,128]{2,1,0:T(8,128)S(1)} all-to-all(f32[8,128,128]{2,1,0:T(8,128)S(1)} %bitcast.50), channel_id=1, replica_groups=mesh['h'=2,'r8'=8,'col'=8] {'r8'}, dimensions={0} | all-to-all | bytes 1048576 | tf_op jit(solution)/shard_map/all_to_all | solution.py:13
  22.1 0.8 broadcast_in_dim.12
  22.9 3.5 %all-to-all-start.1 = ((f32[8,128,128]{1,2,0:T(8,128)}), f32[8,128,128]{1,2,0:T(8,128)S(1)}, u32[]{:S(2)}, u32[]{:S(2)}) async-start(f32[8,128,128]{1,2,0:T(8,128)} %broadcast_in_dim.12), calls=%async_computation.1 | async-start | bytes 1048576 | tf_op jit(solution)/shard_map/all_to_all | solution.py:18
  26.5 9.4 %all-to-all-done.1 = f32[8,128,128]{1,2,0:T(8,128)S(1)} async-done(((f32[8,128,128]{1,2,0:T(8,128)}), f32[8,128,128]{1,2,0:T(8,128)S(1)}, u32[]{:S(2)}, u32[]{:S(2)}) %all-to-all-start.1) | async-done | bytes 524320 | tf_op jit(solution)/shard_map/all_to_all | solution.py:18
  35.9 0.2 copy.33
  36.1 7.7 %fusion.16 = f32[128,2048]{1,0:T(8,128)S(1)} fusion(f32[1024,128]{1,0:T(8,128)S(1)} %bitcast.44, f32[2048,1024]{1,0:T(8,128)} %param.12), kind=kOutput, calls=%fused_computation.50 | convolution fusion | flops 1610612736 | bytes 9961472 | tf_op jit(solution)/shard_map/dot_general | solution.py:51
  43.9 1.1 copy.52
  45.0 5.9 %all-to-all-start.2 = ((f32[8,256,128]{1,2,0:T(8,128)}), f32[8,256,128]{1,2,0:T(8,128)}, u32[]{:S(2)}, u32[]{:S(2)}) async-start(f32[8,256,128]{1,2,0:T(8,128)} %bitcast.49), calls=%async_computation.2 | async-start | bytes 2097152 | tf_op jit(solution)/shard_map/all_to_all | solution.py:13
  50.9 0.2 fusion
  51.2 0.2 fusion.1
  51.4 1.4 scatter_custom_fusion.1
  53.0 12.9 %all-to-all-done.2 = f32[8,256,128]{1,2,0:T(8,128)} async-done(((f32[8,256,128]{1,2,0:T(8,128)}), f32[8,256,128]{1,2,0:T(8,128)}, u32[]{:S(2)}, u32[]{:S(2)}) %all-to-all-start.2) | async-done | bytes 1048608 | tf_op jit(solution)/shard_map/all_to_all | solution.py:13
  66.0 1.3 reduce_sum.47
  67.4 1.2 scatter_custom_fusion
  68.7 19.8 %all_to_all.41 = f32[128,5,128]{2,1,0:T(8,128)S(1)} all-to-all(f32[128,5,128]{2,1,0:T(8,128)S(1)} %pad_maximum_fusion), channel_id=1, replica_groups=mesh['h'=2,'r8'=8,'col'=8] {'h','r8','col'}, dimensions={0} | all-to-all | bytes 655360 | tf_op jit(solution)/shard_map/all_to_all | solution.py:79
  88.5 0.2 fusion.6
  88.9 2.3 %scatter_custom_fusion.2 = f32[192,128]{1,0:T(8,128)S(1)} fusion(s32[512]{0:T(512)S(1)} %bitcast.61, f32[512,128]{1,0:T(8,128)S(1)} %bitcast.57, f32[]{:T(128)} %constant.91.clone.1), kind=kCustom, calls=%fused_computation.22 | custom fusion | flops 65536 | bytes 98308 | tf_op jit(solution)/shard_map/scatter-add | solution.py:85
  91.2 9.8 %all_to_all.42 = f32[8,64,128]{2,1,0:T(8,128)S(1)} all-to-all(f32[8,64,128]{2,1,0:T(8,128)S(1)} %broadcast_in_dim.16), channel_id=1, replica_groups=mesh['h'=2,'r8'=8,'col'=8] {'col'}, dimensions={0} | all-to-all | bytes 524288 | tf_op jit(solution)/shard_map/all_to_all | solution.py:18
  101.1 0.7 convolution_bitcast_fusion
  101.8 1.0 copy.41
  102.8 14.1 %all_to_all.43 = f32[16,64,128]{2,1,0:T(8,128)S(1)} all-to-all(f32[16,64,128]{2,1,0:T(8,128)} %bitcast.52), channel_id=1, replica_groups=mesh['h'=2,'r8'=8,'col'=8] {'h','r8'}, dimensions={0} | all-to-all | bytes 1048576 | tf_op jit(solution)/shard_map/all_to_all | solution.py:13
  117.0 13.1 %all_to_all.44 = f32[16,64,128]{2,1,0:T(8,128)S(1)} all-to-all(f32[16,64,128]{2,1,0:T(8,128)S(1)} %broadcast_in_dim.17), channel_id=1, replica_groups=mesh['h'=2,'r8'=8,'col'=8] {'h','r8'}, dimensions={0} | all-to-all | bytes 1048576 | tf_op jit(solution)/shard_map/all_to_all | solution.py:18
  130.0 4.5 %convolution_bitcast_fusion.1 = f32[16,8,8,128]{3,2,1,0:T(8,128)S(1)} fusion(f32[1024,128]{1,0:T(8,128)S(1)} %bitcast.46, f32[1024,1024]{1,0:T(8,128)} %param.17), kind=kOutput, calls=%fused_computation.4 | convolution fusion | flops 805306368 | bytes 5242880 | tf_op jit(solution)/shard_map/dot_general | solution.py:98
  134.5 0.8 copy.53
  135.4 6.5 %all-to-all-start.7 = ((f32[8,128,128]{1,2,0:T(8,128)}), f32[8,128,128]{1,2,0:T(8,128)}, u32[]{:S(2)}, u32[]{:S(2)}) async-start(f32[8,128,128]{1,2,0:T(8,128)} %bitcast.51), calls=%async_computation.7 | async-start | bytes 1048576 | tf_op jit(solution)/shard_map/all_to_all | solution.py:13
  141.9 1.0 constant_dynamic-slice_fusion
  142.9 1.8 %copy.45 = f32[1024,16]{0,1:T(8,128)} copy(f32[1024,16]{1,0:T(8,128)} %constant_dynamic-slice_fusion) | data formatting | bytes 131072
  144.8 6.6 %all-to-all-done.7 = f32[8,128,128]{1,2,0:T(8,128)} async-done(((f32[8,128,128]{1,2,0:T(8,128)}), f32[8,128,128]{1,2,0:T(8,128)}, u32[]{:S(2)}, u32[]{:S(2)}) %all-to-all-start.7) | async-done | bytes 524320 | tf_op jit(solution)/shard_map/all_to_all | solution.py:13
  151.4 1.1 reduce_sum.49
  152.6 0.6 fusion.5
  153.2 0.8 copy.55
  (36 shorter events, 1.1 us)
Async XLA Ops:
  0.6 100.5 %copy-start = (f32[512,1024]{1,0:T(8,128)S(1)}, f32[512,1024]{1,0:T(8,128)}, u32[]{:S(2)}) copy-start(f32[512,1024]{1,0:T(8,128)} %param.16) | copy-start | bytes 6291460
  0.6 25.7 %copy-start.4 = (s32[256]{0:T(256)S(1)}, s32[256]{0:T(256)}, u32[]{:S(2)}) copy-start(s32[256]{0:T(256)} %param.15) | copy-start | bytes 3076
  22.9 13.0 %all-to-all-start.1 = ((f32[8,128,128]{1,2,0:T(8,128)}), f32[8,128,128]{1,2,0:T(8,128)S(1)}, u32[]{:S(2)}, u32[]{:S(2)}) async-start(f32[8,128,128]{1,2,0:T(8,128)} %broadcast_in_dim.12), calls=%async_computation.1 | async-start | bytes 1048576 | tf_op jit(solution)/shard_map/all_to_all | solution.py:18
  43.8 9.1 %copy-start.1 = (f32[256,128]{1,0:T(8,128)S(1)}, f32[256,128]{1,0:T(8,128)}, u32[]{:S(2)}) copy-start(f32[256,128]{1,0:T(8,128)} %param.14) | copy-start | bytes 393220
  45.0 46.2 %copy-start.3 = (f32[64,128]{1,0:T(8,128)S(1)}, f32[64,128]{1,0:T(8,128)}, u32[]{:S(2)}) copy-start(f32[64,128]{1,0:T(8,128)} %param.18) | copy-start | bytes 98308
  45.0 21.0 %all-to-all-start.2 = ((f32[8,256,128]{1,2,0:T(8,128)}), f32[8,256,128]{1,2,0:T(8,128)}, u32[]{:S(2)}, u32[]{:S(2)}) async-start(f32[8,256,128]{1,2,0:T(8,128)} %bitcast.49), calls=%async_computation.2 | async-start | bytes 2097152 | tf_op jit(solution)/shard_map/all_to_all | solution.py:13
  130.0 22.5 %copy-start.2 = (f32[128,128]{1,0:T(8,128)S(1)}, f32[128,128]{1,0:T(8,128)}, u32[]{:S(2)}) copy-start(f32[128,128]{1,0:T(8,128)} %param.19) | copy-start | bytes 196612
  135.4 16.0 %all-to-all-start.7 = ((f32[8,128,128]{1,2,0:T(8,128)}), f32[8,128,128]{1,2,0:T(8,128)}, u32[]{:S(2)}, u32[]{:S(2)}) async-start(f32[8,128,128]{1,2,0:T(8,128)} %bitcast.51), calls=%async_computation.7 | async-start | bytes 1048576 | tf_op jit(solution)/shard_map/all_to_all | solution.py:13

commit v4 on v3

--- a/solution.py
+++ b/solution.py
@@ -31,6 +31,7 @@
     parent_border_rhs,
 ):
     highest = lax.Precision.HIGH
+    exact = lax.Precision.HIGHEST
     contract_rows = (((0,), (0,)), ((), ()))
     half_rows = lax.axis_size("r8")
     rows_axis = lax.axis_size("h") * half_rows
@@ -61,29 +62,30 @@
     is_sep = child_map < SP
     owner_id = jnp.where(is_sep, child_map // sep_dev, (child_map - SP) // bord_dev)
     target = jnp.where(is_sep, child_map % sep_dev, sep_dev + (child_map - SP) % bord_dev)
+    slots = devices_all * capacity
     onehot = (owner_id[:, None] == jnp.arange(devices_all, dtype=jnp.int32)[None, :]).astype(
         jnp.int32
     )
     running = jnp.cumsum(onehot, axis=0)
     placed = owner_id * capacity + jnp.sum(onehot * running, axis=1) - 1
-    send_rows = jnp.zeros((devices_all * capacity, width_rhs), jnp.float32).at[placed].set(outgoing)
+    spread = (jnp.arange(slots, dtype=jnp.int32)[:, None] == placed[None, :]).astype(jnp.float32)
     send_index = (
-        jnp.full((devices_all * capacity,), sep_dev + bord_dev, jnp.int32).at[placed].set(target)
+        jnp.full((slots,), sep_dev + bord_dev, jnp.int32).at[placed].set(target)
     )
     index_row = jnp.zeros((devices_all, 1, width_rhs), jnp.float32).at[:, 0, :capacity].set(
         send_index.reshape(devices_all, capacity).astype(jnp.float32)
     )
+    send_rows = jnp.dot(spread, outgoing, precision=exact, preferred_element_type=jnp.float32)
     packed = jnp.concatenate(
         [send_rows.reshape(devices_all, capacity, width_rhs), index_row], axis=1
     )
     got = lax.all_to_all(packed, ALL, 0, 0, tiled=True)
-    got_rows = got[:, :capacity]
-    got_index = got[:, capacity, :capacity].astype(jnp.int32)
-    received = (
-        jnp.zeros((sep_dev + bord_dev, width_rhs), jnp.float32)
-        .at[got_index.reshape(-1)]
-        .add(got_rows.reshape(-1, width_rhs), mode="drop")
-    )
+    got_rows = got[:, :capacity].reshape(slots, width_rhs)
+    got_index = got[:, capacity, :capacity].astype(jnp.int32).reshape(slots)
+    gather_map = (
+        jnp.arange(sep_dev + bord_dev, dtype=jnp.int32)[:, None] == got_index[None, :]
+    ).astype(jnp.float32)
+    received = jnp.dot(gather_map, got_rows, precision=exact, preferred_element_type=jnp.float32)
     sep_rows = parent_sep_rhs + received[:sep_dev]
     border_rows = parent_border_rhs + received[sep_dev:]
     partial_sep = lax.dot_general(

time: 155 us -> 152 us (0.981)
  other arithmetic: 6.18 us -> 3.89 us
    scatter-add x1 -> x0, other arithmetic: 2.27 us -> none  [local(): received = jnp.zeros((sep_dev + bord_dev, width_rhs), jnp.float32).at[got...]
where the time goes in v4:
time: 152 us; the launch traced here: 151 us
  blocking collectives  72.3 us (48%)
  waiting for transfers between devices  28.9 us (19%)
  matrix products  19.6 us (13%)
  starting transfers between devices  15.9 us (10%)
  local copies, waits for them, and re-layouts  9.8 us (6%)
  other arithmetic  3.89 us (3%)
    all_to_all x2, blocking collectives, reduce_scatter(): lax.all_to_all(x.reshape(n, x.shape[0] // n, x.shape[1]), axis, 0, 0, til...  29.6 us
    all_to_all x2, blocking collectives, gather(): lax.all_to_all(jnp.broadcast_to(x[None], (n,) + x.shape), axis, 0, 0, til...  22.9 us
    all_to_all x1, blocking collectives, local(): got = lax.all_to_all(packed, ALL, 0, 0, tiled=True)  19.8 us
    all_to_all x2, waiting for transfers between devices, reduce_scatter(): lax.all_to_all(x.reshape(n, x.shape[0] // n, x.shape[1]), axis, 0, 0, til...  19.6 us
    all_to_all x2, starting transfers between devices, reduce_scatter(): lax.all_to_all(x.reshape(n, x.shape[0] // n, x.shape[1]), axis, 0, 0, til...  12.4 us
    all_to_all x1, waiting for transfers between devices, gather(): lax.all_to_all(jnp.broadcast_to(x[None], (n,) + x.shape), axis, 0, 0, til...  9.36 us
    dot_general x1, matrix products, local(): jnp.dot(child_border, solved, precision=highest, preferred_element_type=j...  7.73 us
    dot_general x1, matrix products, local(): lax.dot_general(child_inverse, child_sep_rhs, contract_rows, precision=hi...  5.88 us
  transfers between devices with their start and end apart: 3, of which 3 were waited for; matrix products, arithmetic and copies ran while one was open for 3% of the time, Pallas kernels for 0%

profile of v4, /device:TPU:1, one launch (start us, length us, event | category | flops | bytes accessed | tf_op | source)
XLA Modules:
  0.0 151.3 jit_solution(7059298641696775777)
XLA Ops:
  0.7 5.9 %fusion.16 = f32[1024,128]{1,0:T(8,128)S(1)} fusion(f32[1024,1024]{1,0:T(8,128)} %param.11, f32[1024,128]{1,0:T(8,128)} %param.13), kind=kOutput, calls=%fused_computation.51 | convolution fusion | flops 805306368 | bytes 5242880 | tf_op jit(solution)/shard_map/dot_general | solution.py:40
  6.5 15.4 %all_to_all.40 = f32[8,128,128]{2,1,0:T(8,128)S(1)} all-to-all(f32[8,128,128]{2,1,0:T(8,128)S(1)} %bitcast.49), channel_id=1, replica_groups=mesh['h'=2,'r8'=8,'col'=8] {'r8'}, dimensions={0} | all-to-all | bytes 1048576 | tf_op jit(solution)/shard_map/all_to_all | solution.py:13
  22.1 0.8 broadcast_in_dim.10
  22.9 3.5 %all-to-all-start.1 = ((f32[8,128,128]{1,2,0:T(8,128)}), f32[8,128,128]{1,2,0:T(8,128)S(1)}, u32[]{:S(2)}, u32[]{:S(2)}) async-start(f32[8,128,128]{1,2,0:T(8,128)} %broadcast_in_dim.10), calls=%async_computation.1 | async-start | bytes 1048576 | tf_op jit(solution)/shard_map/all_to_all | solution.py:18
  26.5 9.4 %all-to-all-done.1 = f32[8,128,128]{1,2,0:T(8,128)S(1)} async-done(((f32[8,128,128]{1,2,0:T(8,128)}), f32[8,128,128]{1,2,0:T(8,128)S(1)}, u32[]{:S(2)}, u32[]{:S(2)}) %all-to-all-start.1) | async-done | bytes 524320 | tf_op jit(solution)/shard_map/all_to_all | solution.py:18
  35.9 0.2 copy.32
  36.1 7.7 %fusion.17 = f32[128,2048]{1,0:T(8,128)S(1)} fusion(f32[1024,128]{1,0:T(8,128)S(1)} %bitcast.43, f32[2048,1024]{1,0:T(8,128)} %param.12), kind=kOutput, calls=%fused_computation.52 | convolution fusion | flops 1610612736 | bytes 9961472 | tf_op jit(solution)/shard_map/dot_general | solution.py:52
  43.9 1.1 copy.50
  45.0 5.9 %all-to-all-start.2 = ((f32[8,256,128]{1,2,0:T(8,128)}), f32[8,256,128]{1,2,0:T(8,128)}, u32[]{:S(2)}, u32[]{:S(2)}) async-start(f32[8,256,128]{1,2,0:T(8,128)} %bitcast.48), calls=%async_computation.2 | async-start | bytes 2097152 | tf_op jit(solution)/shard_map/all_to_all | solution.py:13
  50.9 0.2 fusion.4
  51.2 0.2 fusion.5
  51.4 1.4 scatter_custom_fusion
  53.0 12.9 %all-to-all-done.2 = f32[8,256,128]{1,2,0:T(8,128)} async-done(((f32[8,256,128]{1,2,0:T(8,128)}), f32[8,256,128]{1,2,0:T(8,128)}, u32[]{:S(2)}, u32[]{:S(2)}) %all-to-all-start.2) | async-done | bytes 1048608 | tf_op jit(solution)/shard_map/all_to_all | solution.py:13
  66.0 1.3 reduce_sum.47
  67.3 0.4 fusion
  67.8 19.8 %all_to_all.41 = f32[128,5,128]{2,1,0:T(8,128)S(1)} all-to-all(f32[128,5,128]{2,1,0:T(8,128)S(1)} %pad_maximum_fusion), channel_id=1, replica_groups=mesh['h'=2,'r8'=8,'col'=8] {'h','r8','col'}, dimensions={0} | all-to-all | bytes 655360 | tf_op jit(solution)/shard_map/all_to_all | solution.py:82
  87.5 0.2 fusion.9
  87.9 0.3 fusion.1
  88.4 9.8 %all_to_all.42 = f32[8,64,128]{2,1,0:T(8,128)S(1)} all-to-all(f32[8,64,128]{2,1,0:T(8,128)S(1)} %broadcast_in_dim.13), channel_id=1, replica_groups=mesh['h'=2,'r8'=8,'col'=8] {'col'}, dimensions={0} | all-to-all | bytes 524288 | tf_op jit(solution)/shard_map/all_to_all | solution.py:18
  98.2 0.7 convolution_bitcast_fusion
  98.9 1.0 copy.39
  99.9 14.2 %all_to_all.43 = f32[16,64,128]{2,1,0:T(8,128)S(1)} all-to-all(f32[16,64,128]{2,1,0:T(8,128)} %bitcast.51), channel_id=1, replica_groups=mesh['h'=2,'r8'=8,'col'=8] {'h','r8'}, dimensions={0} | all-to-all | bytes 1048576 | tf_op jit(solution)/shard_map/all_to_all | solution.py:13
  114.3 13.1 %all_to_all.44 = f32[16,64,128]{2,1,0:T(8,128)S(1)} all-to-all(f32[16,64,128]{2,1,0:T(8,128)S(1)} %broadcast_in_dim.14), channel_id=1, replica_groups=mesh['h'=2,'r8'=8,'col'=8] {'h','r8'}, dimensions={0} | all-to-all | bytes 1048576 | tf_op jit(solution)/shard_map/all_to_all | solution.py:18
  127.3 4.5 %convolution_bitcast_fusion.1 = f32[16,8,8,128]{3,2,1,0:T(8,128)S(1)} fusion(f32[1024,128]{1,0:T(8,128)S(1)} %bitcast.45, f32[1024,1024]{1,0:T(8,128)} %param.17), kind=kOutput, calls=%fused_computation.2 | convolution fusion | flops 805306368 | bytes 5242880 | tf_op jit(solution)/shard_map/dot_general | solution.py:100
  131.8 0.8 copy.51
  132.7 6.5 %all-to-all-start.7 = ((f32[8,128,128]{1,2,0:T(8,128)}), f32[8,128,128]{1,2,0:T(8,128)}, u32[]{:S(2)}, u32[]{:S(2)}) async-start(f32[8,128,128]{1,2,0:T(8,128)} %bitcast.50), calls=%async_computation.7 | async-start | bytes 1048576 | tf_op jit(solution)/shard_map/all_to_all | solution.py:13
  139.2 1.0 constant_dynamic-slice_fusion
  140.2 1.8 %copy.43 = f32[1024,16]{0,1:T(8,128)} copy(f32[1024,16]{1,0:T(8,128)} %constant_dynamic-slice_fusion) | data formatting | bytes 131072
  142.0 6.6 %all-to-all-done.7 = f32[8,128,128]{1,2,0:T(8,128)} async-done(((f32[8,128,128]{1,2,0:T(8,128)}), f32[8,128,128]{1,2,0:T(8,128)}, u32[]{:S(2)}, u32[]{:S(2)}) %all-to-all-start.7) | async-done | bytes 524320 | tf_op jit(solution)/shard_map/all_to_all | solution.py:13
  148.7 1.1 reduce_sum.49
  149.9 0.6 fusion.8
  150.5 0.8 copy.53
  (33 shorter events, 1.0 us)
Async XLA Ops:
  0.6 97.6 %copy-start = (f32[512,1024]{1,0:T(8,128)S(1)}, f32[512,1024]{1,0:T(8,128)}, u32[]{:S(2)}) copy-start(f32[512,1024]{1,0:T(8,128)} %param.16) | copy-start | bytes 6291460
  0.6 25.7 %copy-start.4 = (s32[256]{0:T(256)S(1)}, s32[256]{0:T(256)}, u32[]{:S(2)}) copy-start(s32[256]{0:T(256)} %param.15) | copy-start | bytes 3076
  22.9 13.0 %all-to-all-start.1 = ((f32[8,128,128]{1,2,0:T(8,128)}), f32[8,128,128]{1,2,0:T(8,128)S(1)}, u32[]{:S(2)}, u32[]{:S(2)}) async-start(f32[8,128,128]{1,2,0:T(8,128)} %broadcast_in_dim.10), calls=%async_computation.1 | async-start | bytes 1048576 | tf_op jit(solution)/shard_map/all_to_all | solution.py:18
  43.8 9.1 %copy-start.1 = (f32[256,128]{1,0:T(8,128)S(1)}, f32[256,128]{1,0:T(8,128)}, u32[]{:S(2)}) copy-start(f32[256,128]{1,0:T(8,128)} %param.14) | copy-start | bytes 393220
  45.0 43.3 %copy-start.3 = (f32[64,128]{1,0:T(8,128)S(1)}, f32[64,128]{1,0:T(8,128)}, u32[]{:S(2)}) copy-start(f32[64,128]{1,0:T(8,128)} %param.18) | copy-start | bytes 98308
  45.0 21.0 %all-to-all-start.2 = ((f32[8,256,128]{1,2,0:T(8,128)}), f32[8,256,128]{1,2,0:T(8,128)}, u32[]{:S(2)}, u32[]{:S(2)}) async-start(f32[8,256,128]{1,2,0:T(8,128)} %bitcast.48), calls=%async_computation.2 | async-start | bytes 2097152 | tf_op jit(solution)/shard_map/all_to_all | solution.py:13
  127.3 22.5 %copy-start.2 = (f32[128,128]{1,0:T(8,128)S(1)}, f32[128,128]{1,0:T(8,128)}, u32[]{:S(2)}) copy-start(f32[128,128]{1,0:T(8,128)} %param.19) | copy-start | bytes 196612
  132.7 16.0 %all-to-all-start.7 = ((f32[8,128,128]{1,2,0:T(8,128)}), f32[8,128,128]{1,2,0:T(8,128)}, u32[]{:S(2)}, u32[]{:S(2)}) async-start(f32[8,128,128]{1,2,0:T(8,128)} %bitcast.50), calls=%async_computation.7 | async-start | bytes 1048576 | tf_op jit(solution)/shard_map/all_to_all | solution.py:13

commit v5 on v4

--- a/solution.py
+++ b/solution.py
@@ -6,11 +6,22 @@
 
 SP = 8192
 ROW = ("h", "r8")
-ALL = ("h", "r8", "col")
+COL = ("x", "k")
+ALL = ("h", "r8", "x", "k")
 
 
 def reduce_scatter(x, axis, n):
     got = lax.all_to_all(x.reshape(n, x.shape[0] // n, x.shape[1]), axis, 0, 0, tiled=False)
+    return got.sum(axis=0)
+
+
+def reduce_scatter_chip(x, chips):
+    core = lax.axis_index("k")
+    blocks = x.reshape(chips, 2, x.shape[0] // (2 * chips), x.shape[1])
+    mine = lax.dynamic_index_in_dim(blocks, core, 1, keepdims=False)
+    other = lax.dynamic_index_in_dim(blocks, 1 - core, 1, keepdims=False)
+    summed = mine + lax.ppermute(other, "k", [(0, 1), (1, 0)])
+    got = lax.all_to_all(summed, "x", 0, 0, tiled=False)
     return got.sum(axis=0)
 
 
@@ -35,7 +46,8 @@
     contract_rows = (((0,), (0,)), ((), ()))
     half_rows = lax.axis_size("r8")
     rows_axis = lax.axis_size("h") * half_rows
-    cols_axis = lax.axis_size("col")
+    chips = lax.axis_size("x")
+    cols_axis = chips * lax.axis_size("k")
     within = lax.axis_index("r8")
     partial_term = lax.dot_general(
         child_inverse,
@@ -48,10 +60,9 @@
     solved = gather(reduce_scatter(partial_term, "r8", half_rows), "r8", half_rows)
     share = width_rhs // half_rows
     child_part = lax.dynamic_slice_in_dim(solved, within * share, share, axis=1)
-    carried = reduce_scatter(
+    carried = reduce_scatter_chip(
         jnp.dot(child_border, solved, precision=highest, preferred_element_type=jnp.float32),
-        "col",
-        cols_axis,
+        chips,
     )
     outgoing = child_border_rhs - carried
     devices_all = rows_axis * cols_axis
@@ -90,7 +101,7 @@
     border_rows = parent_border_rhs + received[sep_dev:]
     partial_sep = lax.dot_general(
         parent_inverse,
-        gather(sep_rows, "col", cols_axis),
+        gather(sep_rows, COL, cols_axis),
         contract_rows,
         precision=highest,
         preferred_element_type=jnp.float32,
@@ -98,7 +109,7 @@
     parent_solution = gather(reduce_scatter(partial_sep, ROW, rows_axis), ROW, rows_axis)
     carried_parent = reduce_scatter(
         jnp.dot(parent_border, parent_solution, precision=highest, preferred_element_type=jnp.float32),
-        "col",
+        COL,
         cols_axis,
     )
     parent_contribution = border_rows - carried_parent
@@ -107,15 +118,15 @@
 
 def solution(mesh):
     rows, cols = mesh.devices.shape
-    split = Mesh(mesh.devices.reshape(2, rows // 2, cols), ("h", "r8", "col"))
+    split = Mesh(mesh.devices.reshape(2, rows // 2, cols // 2, 2), ALL)
     placed = (
-        P(ROW, "col"),
-        P(ROW, "col"),
+        P(ROW, COL),
+        P(ROW, COL),
         P(ROW, None),
         P(ALL, None),
         P(ALL),
-        P(ROW, "col"),
-        P(ROW, "col"),
+        P(ROW, COL),
+        P(ROW, COL),
         P(ALL, None),
         P(ALL, None),
     )
@@ -123,6 +134,6 @@
         local,
         mesh=split,
         in_specs=placed,
-        out_specs=(P("col", ROW), P("col", None), P(ALL, None)),
+        out_specs=(P(COL, ROW), P(COL, None), P(ALL, None)),
         check_vma=False,
     )

time: 152 us -> 155 us (1.020)
  local copies, waits for them, and re-layouts: 9.8 us -> 16.5 us
  waiting for transfers between devices: 28.9 us -> 23.6 us
    all_to_all x2 -> x1, waiting for transfers between devices: 19.6 us -> 6.65 us  [reduce_scatter(): lax.all_to_all(x.reshape(n, x.shape[0] // n, x.shape[1]), axis, 0, 0, til...]
    all_to_all x0 -> x1, waiting for transfers between devices: none -> 5.95 us  [reduce_scatter_chip(): got = lax.all_to_all(summed, 'x', 0, 0, tiled=False)]
    all_to_all x2 -> x1, starting transfers between devices: 12.4 us -> 6.53 us  [reduce_scatter(): lax.all_to_all(x.reshape(n, x.shape[0] // n, x.shape[1]), axis, 0, 0, til...]
    all_to_all x0 -> x1, starting transfers between devices: none -> 4.01 us  [reduce_scatter_chip(): got = lax.all_to_all(summed, 'x', 0, 0, tiled=False)]
    dynamic_slice x0 -> x2, local copies, waits for them, and re-layouts: none -> 3.63 us  [the longest x1 2.74 us: reduce_scatter_chip(): mine = lax.dynamic_index_in_dim(blocks, core, 1, keepdims=False)]
    reshape x0 -> x1, local copies, waits for them, and re-layouts: none -> 3.16 us  [reduce_scatter_chip(): blocks = x.reshape(chips, 2, x.shape[0] // (2 * chips), x.shape[1])]
    add x0 -> x1, other arithmetic: none -> 1.95 us  [reduce_scatter_chip(): summed = mine + lax.ppermute(other, 'k', [(0, 1), (1, 0)])]
    unnamed x14 -> x12, local copies, waits for them, and re-layouts: 2.76 us -> 3.66 us
  transfers between devices with their start and end apart: 3 -> 4, of which waited for: 3 -> 4; matrix products, arithmetic and copies ran while one was open for 3% -> 4% of each run, Pallas kernels for 0% -> 0%
where the time goes in v5:
time: 155 us; the launch traced here: 154 us
  blocking collectives  72.7 us (47%)
  waiting for transfers between devices  23.6 us (15%)
  matrix products  20.5 us (13%)
  local copies, waits for them, and re-layouts  16.5 us (11%)
  starting transfers between devices  15.5 us (10%)
  other arithmetic  4.58 us (3%)
    all_to_all x2, blocking collectives, reduce_scatter(): lax.all_to_all(x.reshape(n, x.shape[0] // n, x.shape[1]), axis, 0, 0, til...  29.4 us
    all_to_all x2, blocking collectives, gather(): lax.all_to_all(jnp.broadcast_to(x[None], (n,) + x.shape), axis, 0, 0, til...  22.9 us
    all_to_all x1, blocking collectives, local(): got = lax.all_to_all(packed, ALL, 0, 0, tiled=True)  20.3 us
    all_to_all x1, waiting for transfers between devices, gather(): lax.all_to_all(jnp.broadcast_to(x[None], (n,) + x.shape), axis, 0, 0, til...  9.5 us
    dot_general x1, matrix products, local(): jnp.dot(child_border, solved, precision=highest, preferred_element_type=j...  8.73 us
    all_to_all x1, waiting for transfers between devices, reduce_scatter(): lax.all_to_all(x.reshape(n, x.shape[0] // n, x.shape[1]), axis, 0, 0, til...  6.65 us
    all_to_all x1, starting transfers between devices, reduce_scatter(): lax.all_to_all(x.reshape(n, x.shape[0] // n, x.shape[1]), axis, 0, 0, til...  6.53 us
    all_to_all x1, waiting for transfers between devices, reduce_scatter_chip(): got = lax.all_to_all(summed, 'x', 0, 0, tiled=False)  5.95 us
  transfers between devices with their start and end apart: 4, of which 4 were waited for; matrix products, arithmetic and copies ran while one was open for 4% of the time, Pallas kernels for 0%

profile of v5, /device:TPU:1, one launch (start us, length us, event | category | flops | bytes accessed | tf_op | source)
XLA Modules:
  0.0 154.3 jit_solution(16943231492845805356)
XLA Ops:
  0.6 5.9 %fusion.16 = f32[1024,128]{1,0:T(8,128)S(1)} fusion(f32[1024,1024]{1,0:T(8,128)} %param.11, f32[1024,128]{1,0:T(8,128)} %param.13), kind=kOutput, calls=%fused_computation.55 | convolution fusion | flops 805306368 | bytes 5242880 | tf_op jit(solution)/shard_map/dot_general | solution.py:52
  6.5 15.4 %all_to_all.40 = f32[8,128,128]{2,1,0:T(8,128)S(1)} all-to-all(f32[8,128,128]{2,1,0:T(8,128)S(1)} %bitcast.51), channel_id=1, replica_groups=mesh['h'=2,'r8'=8,'x'=4,'k'=2] {'r8'}, dimensions={0} | all-to-all | bytes 1048576 | tf_op jit(solution)/shard_map/all_to_all | solution.py:14
  22.0 0.8 broadcast_in_dim.10
  22.9 3.5 %all-to-all-start.1 = ((f32[8,128,128]{1,2,0:T(8,128)}), f32[8,128,128]{1,2,0:T(8,128)S(1)}, u32[]{:S(2)}, u32[]{:S(2)}) async-start(f32[8,128,128]{1,2,0:T(8,128)} %broadcast_in_dim.10), calls=%async_computation.1 | async-start | bytes 1048576 | tf_op jit(solution)/shard_map/all_to_all | solution.py:29
  26.4 9.5 %all-to-all-done.1 = f32[8,128,128]{1,2,0:T(8,128)S(1)} async-done(((f32[8,128,128]{1,2,0:T(8,128)}), f32[8,128,128]{1,2,0:T(8,128)S(1)}, u32[]{:S(2)}, u32[]{:S(2)}) %all-to-all-start.1) | async-done | bytes 524320 | tf_op jit(solution)/shard_map/all_to_all | solution.py:29
  36.1 8.7 %convolution_bitcast_fusion = f32[2048,128]{0,1:T(8,128)} fusion(f32[1024,128]{1,0:T(8,128)S(1)} %bitcast.47, f32[2048,1024]{1,0:T(8,128)} %param.12), kind=kOutput, calls=%fused_computation.1 | convolution fusion | flops 1610612736 | bytes 9961472 | tf_op jit(solution)/shard_map/dot_general | solution.py:64
  44.8 3.2 %reshape.107 = f32[4,2,256,128]{2,1,0,3:T(2,128)} reshape(f32[2048,128]{0,1:T(8,128)} %convolution_bitcast_fusion) | data formatting | bytes 2097152 | tf_op jit(solution)/shard_map/reshape | solution.py:20
  48.0 2.7 %constant_dynamic-slice_fusion.1 = (f32[4,1,256,128]{2,1,0,3:T(1,128)S(1)}, f32[4,1,256,128]{2,1,0,3:T(1,128)S(1)}) fusion(f32[4,2,256,128]{2,1,0,3:T(2,128)} %reshape.107, s32[]{:T(128)S(6)} %select_n.42, s32[]{:T(128)S(6)} %select_n.43), kind=kLoop, calls=%fused_computation.47 | loop fusion | bytes 2097160 | tf_op jit(solution)/shard_map/jit(dynamic_index_in_dim)/dynamic_slice | solution.py:21
  50.7 0.9 copy.53
  51.6 1.5 collective-permute-start
  53.5 1.5 collective-permute-done
  55.0 2.0 %bitcast_add_fusion = f32[4,256,128]{1,2,0:T(8,128)} fusion(f32[4,256,128]{1,2,0:T(8,128)} %collective-permute-done, f32[4,1,256,128]{2,1,0,3:T(1,128)S(1)} %get-tuple-element.18), kind=kLoop, calls=%fused_computation.6 | loop fusion | flops 131072 | bytes 1572864 | tf_op jit(solution)/shard_map/add | solution.py:23
  56.9 4.0 %all-to-all-start.2 = ((f32[4,256,128]{1,2,0:T(8,128)}), f32[4,256,128]{1,2,0:T(8,128)S(1)}, u32[]{:S(2)}, u32[]{:S(2)}) async-start(f32[4,256,128]{1,2,0:T(8,128)} %bitcast_add_fusion), calls=%async_computation.2 | async-start | bytes 1048576 | tf_op jit(solution)/shard_map/all_to_all | solution.py:24
  61.2 1.6 %scatter_custom_fusion = s32[512]{0:T(512)S(1)} fusion(s32[256]{0:T(256)S(1)} %get-tuple-element.21, s32[256]{0:T(256)S(1)} %get-tuple-element.22, s32[]{:T(128)} %constant.117.clone.1), kind=kCustom, calls=%fused_computation.43 | custom fusion | bytes 2052 | tf_op jit(solution)/shard_map/scatter | solution.py:84
  62.9 1.0 copy.39
  63.9 6.0 %all-to-all-done.2 = f32[4,256,128]{1,2,0:T(8,128)S(1)} async-done(((f32[4,256,128]{1,2,0:T(8,128)}), f32[4,256,128]{1,2,0:T(8,128)S(1)}, u32[]{:S(2)}, u32[]{:S(2)}) %all-to-all-start.2) | async-done | bytes 524320 | tf_op jit(solution)/shard_map/all_to_all | solution.py:24
  69.9 0.4 fusion
  70.4 20.3 %all_to_all.41 = f32[128,5,128]{2,1,0:T(8,128)S(1)} all-to-all(f32[128,5,128]{2,1,0:T(8,128)S(1)} %pad_maximum_fusion), channel_id=1, replica_groups=mesh['h'=2,'r8'=8,'x'=4,'k'=2] {'h','r8','x','k'}, dimensions={0} | all-to-all | bytes 655360 | tf_op jit(solution)/shard_map/all_to_all | solution.py:93
  91.5 9.8 %all_to_all.42 = f32[8,64,128]{2,1,0:T(8,128)S(1)} all-to-all(f32[8,64,128]{2,1,0:T(8,128)S(1)} %broadcast_in_dim.13), channel_id=1, replica_groups=mesh['h'=2,'r8'=8,'x'=4,'k'=2] {'x','k'}, dimensions={0} | all-to-all | bytes 524288 | tf_op jit(solution)/shard_map/all_to_all | solution.py:29
  101.4 0.7 convolution_bitcast_fusion.1
  102.1 1.0 copy.41
  103.1 14.1 %all_to_all.43 = f32[16,64,128]{2,1,0:T(8,128)S(1)} all-to-all(f32[16,64,128]{2,1,0:T(8,128)} %bitcast.53), channel_id=1, replica_groups=mesh['h'=2,'r8'=8,'x'=4,'k'=2] {'h','r8'}, dimensions={0} | all-to-all | bytes 1048576 | tf_op jit(solution)/shard_map/all_to_all | solution.py:14
  117.2 13.1 %all_to_all.44 = f32[16,64,128]{2,1,0:T(8,128)S(1)} all-to-all(f32[16,64,128]{2,1,0:T(8,128)S(1)} %broadcast_in_dim.14), channel_id=1, replica_groups=mesh['h'=2,'r8'=8,'x'=4,'k'=2] {'h','r8'}, dimensions={0} | all-to-all | bytes 1048576 | tf_op jit(solution)/shard_map/all_to_all | solution.py:29
  130.3 4.5 %convolution_bitcast_fusion.2 = f32[16,8,8,128]{3,2,1,0:T(8,128)S(1)} fusion(f32[1024,128]{1,0:T(8,128)S(1)} %bitcast.49, f32[1024,1024]{1,0:T(8,128)} %param.17), kind=kOutput, calls=%fused_computation.3 | convolution fusion | flops 805306368 | bytes 5242880 | tf_op jit(solution)/shard_map/dot_general | solution.py:111
  134.8 0.8 copy.52
  135.6 6.5 %all-to-all-start.7 = ((f32[8,128,128]{1,2,0:T(8,128)}), f32[8,128,128]{1,2,0:T(8,128)}, u32[]{:S(2)}, u32[]{:S(2)}) async-start(f32[8,128,128]{1,2,0:T(8,128)} %bitcast.52), calls=%async_computation.7 | async-start | bytes 1048576 | tf_op jit(solution)/shard_map/all_to_all | solution.py:14
  142.2 1.0 constant_dynamic-slice_fusion.2
  143.2 1.8 %copy.45 = f32[1024,16]{0,1:T(8,128)} copy(f32[1024,16]{1,0:T(8,128)} %constant_dynamic-slice_fusion.2) | data formatting | bytes 131072
  145.0 6.6 %all-to-all-done.7 = f32[8,128,128]{1,2,0:T(8,128)} async-done(((f32[8,128,128]{1,2,0:T(8,128)}), f32[8,128,128]{1,2,0:T(8,128)}, u32[]{:S(2)}, u32[]{:S(2)}) %all-to-all-start.7) | async-done | bytes 524320 | tf_op jit(solution)/shard_map/all_to_all | solution.py:14
  151.7 1.1 reduce_sum.49
  152.8 0.6 fusion.8
  153.5 0.8 copy.55
  (36 shorter events, 2.1 us)
Async XLA Ops:
  0.6 100.7 %copy-start = (f32[512,1024]{1,0:T(8,128)S(1)}, f32[512,1024]{1,0:T(8,128)}, u32[]{:S(2)}) copy-start(f32[512,1024]{1,0:T(8,128)} %param.16) | copy-start | bytes 6291460
  22.9 13.0 %all-to-all-start.1 = ((f32[8,128,128]{1,2,0:T(8,128)}), f32[8,128,128]{1,2,0:T(8,128)S(1)}, u32[]{:S(2)}, u32[]{:S(2)}) async-start(f32[8,128,128]{1,2,0:T(8,128)} %broadcast_in_dim.10), calls=%async_computation.1 | async-start | bytes 1048576 | tf_op jit(solution)/shard_map/all_to_all | solution.py:29
  44.8 8.3 %copy-start.3 = (s32[256]{0:T(256)S(1)}, s32[256]{0:T(256)}, u32[]{:S(2)}) copy-start(s32[256]{0:T(256)} %param.15) | copy-start | bytes 3076
  51.6 39.9 %copy-start.2 = (f32[64,128]{1,0:T(8,128)S(1)}, f32[64,128]{1,0:T(8,128)}, u32[]{:S(2)}) copy-start(f32[64,128]{1,0:T(8,128)} %param.18) | copy-start | bytes 98308
  51.6 3.3 %collective-permute-start = (f32[4,256,128]{1,2,0:T(8,128)}, f32[4,256,128]{1,2,0:T(8,128)}, u32[]{:S(2)}, u32[]{:S(2)}) collective-permute-start(f32[4,256,128]{1,2,0:T(8,128)} %bitcast.42), channel_id=1, source_target_pairs={{0,1},{1,0},{2,3},{3,2},{4,5},{5,4},{6,7},{7,6},{8,9},{9,8},{10,11... | collective-permute-start | bytes 1572872 | tf_op jit(solution)/shard_map/ppermute | solution.py:23
  56.9 12.9 %all-to-all-start.2 = ((f32[4,256,128]{1,2,0:T(8,128)}), f32[4,256,128]{1,2,0:T(8,128)S(1)}, u32[]{:S(2)}, u32[]{:S(2)}) async-start(f32[4,256,128]{1,2,0:T(8,128)} %bitcast_add_fusion), calls=%async_computation.2 | async-start | bytes 1048576 | tf_op jit(solution)/shard_map/all_to_all | solution.py:24
  130.3 22.5 %copy-start.1 = (f32[128,128]{1,0:T(8,128)S(1)}, f32[128,128]{1,0:T(8,128)}, u32[]{:S(2)}) copy-start(f32[128,128]{1,0:T(8,128)} %param.19) | copy-start | bytes 196612
  135.6 16.0 %all-to-all-start.7 = ((f32[8,128,128]{1,2,0:T(8,128)}), f32[8,128,128]{1,2,0:T(8,128)}, u32[]{:S(2)}, u32[]{:S(2)}) async-start(f32[8,128,128]{1,2,0:T(8,128)} %bitcast.52), calls=%async_computation.7 | async-start | bytes 1048576 | tf_op jit(solution)/shard_map/all_to_all | solution.py:14

commit v6 on v5

--- a/solution.py
+++ b/solution.py
@@ -15,11 +15,21 @@
     return got.sum(axis=0)
 
 
-def reduce_scatter_chip(x, chips):
-    core = lax.axis_index("k")
-    blocks = x.reshape(chips, 2, x.shape[0] // (2 * chips), x.shape[1])
-    mine = lax.dynamic_index_in_dim(blocks, core, 1, keepdims=False)
-    other = lax.dynamic_index_in_dim(blocks, 1 - core, 1, keepdims=False)
+def reduce_scatter_chip(matrix, vector, chips, precision):
+    first = lax.axis_index("k") == 0
+    blocks = matrix.reshape(chips, 2, matrix.shape[0] // (2 * chips), matrix.shape[1])
+    even, odd = (
+        jnp.einsum(
+            "xrb,bn->xrn",
+            blocks[:, half],
+            vector,
+            precision=precision,
+            preferred_element_type=jnp.float32,
+        )
+        for half in (0, 1)
+    )
+    mine = jnp.where(first, even, odd)
+    other = jnp.where(first, odd, even)
     summed = mine + lax.ppermute(other, "k", [(0, 1), (1, 0)])
     got = lax.all_to_all(summed, "x", 0, 0, tiled=False)
     return got.sum(axis=0)
@@ -60,10 +70,7 @@
     solved = gather(reduce_scatter(partial_term, "r8", half_rows), "r8", half_rows)
     share = width_rhs // half_rows
     child_part = lax.dynamic_slice_in_dim(solved, within * share, share, axis=1)
-    carried = reduce_scatter_chip(
-        jnp.dot(child_border, solved, precision=highest, preferred_element_type=jnp.float32),
-        chips,
-    )
+    carried = reduce_scatter_chip(child_border, solved, chips, highest)
     outgoing = child_border_rhs - carried
     devices_all = rows_axis * cols_axis
     sep_dev = parent_sep_rhs.shape[0]

time: 155 us -> 151 us (0.974)
  local copies, waits for them, and re-layouts: 16.5 us -> 8.52 us
  waiting for transfers between devices: 23.6 us -> 26.8 us
    dynamic_slice x2 -> x0, local copies, waits for them, and re-layouts: 3.63 us -> none  [the longest x1 2.74 us: reduce_scatter_chip(): mine = lax.dynamic_index_in_dim(blocks, core, 1, keepdims=False)]
    all_to_all x1, waiting for transfers between devices: 6.65 us -> 8.79 us  [reduce_scatter(): lax.all_to_all(x.reshape(n, x.shape[0] // n, x.shape[1]), axis, 0, 0, til...]
    reshape x1 -> x2, local copies, waits for them, and re-layouts: 3.16 us -> 1.17 us  [gather(): return got.reshape(n * x.shape[0], x.shape[1])]
    unnamed x12 -> x19, local copies, waits for them, and re-layouts: 3.66 us -> 1.71 us
    dot_general x1 -> x2, matrix products: 8.73 us -> 8.94 us  [reduce_scatter_chip(): jnp.einsum('xrb,bn->xrn', blocks[:, half], vector, precision=precision, p...]
  transfers between devices with their start and end apart: 4 -> 4, of which waited for: 4 -> 4; matrix products, arithmetic and copies ran while one was open for 4% -> 2% of each run, Pallas kernels for 0% -> 0%
where the time goes in v6:
time: 151 us; the launch traced here: 150 us
  blocking collectives  71.5 us (47%)
  waiting for transfers between devices  26.8 us (18%)
  matrix products  20.8 us (14%)
  starting transfers between devices  16 us (11%)
  local copies, waits for them, and re-layouts  8.52 us (6%)
  other arithmetic  5.46 us (4%)
    all_to_all x2, blocking collectives, reduce_scatter(): lax.all_to_all(x.reshape(n, x.shape[0] // n, x.shape[1]), axis, 0, 0, til...  28.6 us
    all_to_all x2, blocking collectives, gather(): lax.all_to_all(jnp.broadcast_to(x[None], (n,) + x.shape), axis, 0, 0, til...  22.5 us
    all_to_all x1, blocking collectives, local(): got = lax.all_to_all(packed, ALL, 0, 0, tiled=True)  20.3 us
    all_to_all x1, waiting for transfers between devices, gather(): lax.all_to_all(jnp.broadcast_to(x[None], (n,) + x.shape), axis, 0, 0, til...  9.5 us
    dot_general x2, matrix products, reduce_scatter_chip(): jnp.einsum('xrb,bn->xrn', blocks[:, half], vector, precision=precision, p...  8.94 us
    all_to_all x1, waiting for transfers between devices, reduce_scatter(): lax.all_to_all(x.reshape(n, x.shape[0] // n, x.shape[1]), axis, 0, 0, til...  8.79 us
    all_to_all x1, waiting for transfers between devices, reduce_scatter_chip(): got = lax.all_to_all(summed, 'x', 0, 0, tiled=False)  7.03 us
    all_to_all x1, starting transfers between devices, reduce_scatter(): lax.all_to_all(x.reshape(n, x.shape[0] // n, x.shape[1]), axis, 0, 0, til...  6.98 us
  transfers between devices with their start and end apart: 4, of which 4 were waited for; matrix products, arithmetic and copies ran while one was open for 2% of the time, Pallas kernels for 0%

profile of v6, /device:TPU:1, one launch (start us, length us, event | category | flops | bytes accessed | tf_op | source)
XLA Modules:
  0.0 149.9 jit_solution(4438210305739397513)
XLA Ops:
  0.6 5.9 %fusion.18 = f32[1024,128]{1,0:T(8,128)S(1)} fusion(f32[1024,1024]{1,0:T(8,128)} %param.11, f32[1024,128]{1,0:T(8,128)} %param.13), kind=kOutput, calls=%fused_computation.57 | convolution fusion | flops 805306368 | bytes 5242880 | tf_op jit(solution)/shard_map/dot_general | solution.py:62
  6.5 15.4 %all_to_all.40 = f32[8,128,128]{2,1,0:T(8,128)S(1)} all-to-all(f32[8,128,128]{2,1,0:T(8,128)S(1)} %bitcast.63), channel_id=1, replica_groups=mesh['h'=2,'r8'=8,'x'=4,'k'=2] {'r8'}, dimensions={0} | all-to-all | bytes 1048576 | tf_op jit(solution)/shard_map/all_to_all | solution.py:14
  22.0 0.8 broadcast_in_dim.10
  22.9 3.5 %all-to-all-start.1 = ((f32[8,128,128]{1,2,0:T(8,128)}), f32[8,128,128]{1,2,0:T(8,128)S(1)}, u32[]{:S(2)}, u32[]{:S(2)}) async-start(f32[8,128,128]{1,2,0:T(8,128)} %broadcast_in_dim.10), calls=%async_computation.1 | async-start | bytes 1048576 | tf_op jit(solution)/shard_map/all_to_all | solution.py:39
  26.4 9.5 %all-to-all-done.1 = f32[8,128,128]{1,2,0:T(8,128)S(1)} async-done(((f32[8,128,128]{1,2,0:T(8,128)}), f32[8,128,128]{1,2,0:T(8,128)S(1)}, u32[]{:S(2)}, u32[]{:S(2)}) %all-to-all-start.1) | async-done | bytes 524320 | tf_op jit(solution)/shard_map/all_to_all | solution.py:39
  35.9 1.1 copy.25
  37.0 1.1 reshape.123
  38.1 0.8 copy-done.1
  38.9 4.4 %fusion = f32[128,4,256]{2,0,1:T(8,128)S(1)} fusion(f32[1024,128,1]{0,1,2:T(8,128)S(1)} %reshape.123, f32[4,2,256,1024]{3,2,1,0:T(8,128)} %bitcast.59), kind=kOutput, calls=%fused_computation.2 | convolution fusion | flops 805306368 | bytes 5242880 | tf_op jit(solution)/shard_map/xrb,bn->xrn/dot_general | solution.py:22
  43.3 4.6 %fusion.1 = f32[128,4,256]{2,0,1:T(8,128)S(1)} fusion(f32[1024,128,1]{0,1,2:T(8,128)} %copy-done.1, f32[4,2,256,1024]{3,2,1,0:T(8,128)} %bitcast.60), kind=kOutput, calls=%fused_computation.4 | convolution fusion | flops 805306368 | bytes 5242880 | tf_op jit(solution)/shard_map/xrb,bn->xrn/dot_general | solution.py:22
  47.9 0.9 select_bitcast_fusion
  48.8 1.5 collective-permute-start
  50.6 1.5 collective-permute-done
  52.1 2.0 %bitcast_add_fusion = f32[4,256,128]{1,2,0:T(8,128)} fusion(f32[4,256,128]{1,2,0:T(8,128)} %collective-permute-done, f32[128,4,256]{2,0,1:T(8,128)S(1)} %fusion.1, f32[128,4,256]{2,0,1:T(8,128)S(1)} %fusion, pred[]{:T(512)S(6)} %eq.66), kind=kLoop, calls=%fused_computation.10 | loop fusion | flops 262144 | bytes 2097153 | tf_op jit(solution)/shard_map/add | solution.py:33
  54.1 4.0 %all-to-all-start.2 = ((f32[4,256,128]{1,2,0:T(8,128)}), f32[4,256,128]{1,2,0:T(8,128)S(1)}, u32[]{:S(2)}, u32[]{:S(2)}) async-start(f32[4,256,128]{1,2,0:T(8,128)} %bitcast_add_fusion), calls=%async_computation.2 | async-start | bytes 1048576 | tf_op jit(solution)/shard_map/all_to_all | solution.py:34
  58.3 1.4 scatter_custom_fusion
  60.0 7.0 %all-to-all-done.2 = f32[4,256,128]{1,2,0:T(8,128)S(1)} async-done(((f32[4,256,128]{1,2,0:T(8,128)}), f32[4,256,128]{1,2,0:T(8,128)S(1)}, u32[]{:S(2)}, u32[]{:S(2)}) %all-to-all-start.2) | async-done | bytes 524320 | tf_op jit(solution)/shard_map/all_to_all | solution.py:34
  67.0 0.4 fusion.2
  67.6 20.3 %all_to_all.41 = f32[128,5,128]{2,1,0:T(8,128)S(1)} all-to-all(f32[128,5,128]{2,1,0:T(8,128)S(1)} %pad_maximum_fusion), channel_id=1, replica_groups=mesh['h'=2,'r8'=8,'x'=4,'k'=2] {'h','r8','x','k'}, dimensions={0} | all-to-all | bytes 655360 | tf_op jit(solution)/shard_map/all_to_all | solution.py:100
  88.3 0.3 fusion.3
  88.7 9.8 %all_to_all.42 = f32[8,64,128]{2,1,0:T(8,128)S(1)} all-to-all(f32[8,64,128]{2,1,0:T(8,128)S(1)} %broadcast_in_dim.13), channel_id=1, replica_groups=mesh['h'=2,'r8'=8,'x'=4,'k'=2] {'x','k'}, dimensions={0} | all-to-all | bytes 524288 | tf_op jit(solution)/shard_map/all_to_all | solution.py:39
  98.5 0.7 convolution_bitcast_fusion
  99.4 13.3 %all_to_all.43 = f32[16,64,128]{2,1,0:T(8,128)S(1)} all-to-all(f32[16,64,128]{2,1,0:T(8,128)S(1)} %bitcast.65), channel_id=1, replica_groups=mesh['h'=2,'r8'=8,'x'=4,'k'=2] {'h','r8'}, dimensions={0} | all-to-all | bytes 1048576 | tf_op jit(solution)/shard_map/all_to_all | solution.py:14
  112.8 12.7 %all_to_all.44 = f32[16,64,128]{2,1,0:T(8,128)S(1)} all-to-all(f32[16,64,128]{2,1,0:T(8,128)S(1)} %broadcast_in_dim.14), channel_id=1, replica_groups=mesh['h'=2,'r8'=8,'x'=4,'k'=2] {'h','r8'}, dimensions={0} | all-to-all | bytes 1048576 | tf_op jit(solution)/shard_map/all_to_all | solution.py:39
  125.5 4.5 %convolution_bitcast_fusion.1 = f32[16,8,8,128]{3,2,1,0:T(8,128)S(1)} fusion(f32[1024,128]{1,0:T(8,128)S(1)} %bitcast.61, f32[1024,1024]{1,0:T(8,128)} %param.17), kind=kOutput, calls=%fused_computation.6 | convolution fusion | flops 805306368 | bytes 5242880 | tf_op jit(solution)/shard_map/dot_general | solution.py:118
  130.0 0.8 copy.43
  130.8 7.0 %all-to-all-start.7 = ((f32[8,128,128]{1,2,0:T(8,128)}), f32[8,128,128]{1,2,0:T(8,128)}, u32[]{:S(2)}, u32[]{:S(2)}) async-start(f32[8,128,128]{1,2,0:T(8,128)} %bitcast.64), calls=%async_computation.7 | async-start | bytes 1048576 | tf_op jit(solution)/shard_map/all_to_all | solution.py:14
  137.9 0.6 constant_dynamic-slice_fusion
  138.5 8.8 %all-to-all-done.7 = f32[8,128,128]{1,2,0:T(8,128)} async-done(((f32[8,128,128]{1,2,0:T(8,128)}), f32[8,128,128]{1,2,0:T(8,128)}, u32[]{:S(2)}, u32[]{:S(2)}) %all-to-all-start.7) | async-done | bytes 524320 | tf_op jit(solution)/shard_map/all_to_all | solution.py:14
  147.3 1.1 reduce_sum.49
  148.5 0.6 fusion.10
  149.1 0.8 copy.45
  (44 shorter events, 1.9 us)
Async XLA Ops:
  0.6 97.9 %copy-start = (f32[512,1024]{1,0:T(8,128)S(1)}, f32[512,1024]{1,0:T(8,128)}, u32[]{:S(2)}) copy-start(f32[512,1024]{1,0:T(8,128)} %param.16) | copy-start | bytes 6291460
  22.9 13.0 %all-to-all-start.1 = ((f32[8,128,128]{1,2,0:T(8,128)}), f32[8,128,128]{1,2,0:T(8,128)S(1)}, u32[]{:S(2)}, u32[]{:S(2)}) async-start(f32[8,128,128]{1,2,0:T(8,128)} %broadcast_in_dim.10), calls=%async_computation.1 | async-start | bytes 1048576 | tf_op jit(solution)/shard_map/all_to_all | solution.py:39
  35.9 2.2 %copy-start.2 = (f32[8,128,128]{1,2,0:T(8,128)}, f32[8,128,128]{1,2,0:T(8,128)S(1)}, u32[]{:S(2)}) copy-start(f32[8,128,128]{1,2,0:T(8,128)S(1)} %all-to-all-done.1) | copy-start | bytes 1572868
  38.1 0.8 copy-start.1
  43.3 6.9 %copy-start.7 = (s32[256]{0:T(256)S(1)}, s32[256]{0:T(256)}, u32[]{:S(2)}) copy-start(s32[256]{0:T(256)} %param.15) | copy-start | bytes 3076
  47.9 12.0 %copy-start.4 = (f32[256,128]{1,0:T(8,128)S(1)}, f32[256,128]{1,0:T(8,128)}, u32[]{:S(2)}) copy-start(f32[256,128]{1,0:T(8,128)} %param.14) | copy-start | bytes 393220
  48.8 3.3 %collective-permute-start = (f32[4,256,128]{1,2,0:T(8,128)}, f32[4,256,128]{1,2,0:T(8,128)}, u32[]{:S(2)}, u32[]{:S(2)}) collective-permute-start(f32[4,256,128]{1,2,0:T(8,128)} %select_bitcast_fusion), channel_id=1, source_target_pairs={{0,1},{1,0},{2,3},{3,2},{4,5},{5,4},{6,7},{7,6},{8,9},{9,8},{10,11... | collective-permute-start | bytes 1572872 | tf_op jit(solution)/shard_map/ppermute | solution.py:33
  50.6 38.0 %copy-start.6 = (f32[64,128]{1,0:T(8,128)S(1)}, f32[64,128]{1,0:T(8,128)}, u32[]{:S(2)}) copy-start(f32[64,128]{1,0:T(8,128)} %param.18) | copy-start | bytes 98308
  54.1 12.9 %all-to-all-start.2 = ((f32[4,256,128]{1,2,0:T(8,128)}), f32[4,256,128]{1,2,0:T(8,128)S(1)}, u32[]{:S(2)}, u32[]{:S(2)}) async-start(f32[4,256,128]{1,2,0:T(8,128)} %bitcast_add_fusion), calls=%async_computation.2 | async-start | bytes 1048576 | tf_op jit(solution)/shard_map/all_to_all | solution.py:34
  112.8 25.0 %copy-start.3 = (f32[8,128,128]{1,2,0:T(8,128)S(1)}, f32[8,128,128]{1,2,0:T(8,128)}, u32[]{:S(2)}) copy-start(f32[8,128,128]{1,2,0:T(8,128)} %copy-done.2) | copy-start | bytes 1572868
  125.5 23.0 %copy-start.5 = (f32[128,128]{1,0:T(8,128)S(1)}, f32[128,128]{1,0:T(8,128)}, u32[]{:S(2)}) copy-start(f32[128,128]{1,0:T(8,128)} %param.19) | copy-start | bytes 196612
  130.8 16.5 %all-to-all-start.7 = ((f32[8,128,128]{1,2,0:T(8,128)}), f32[8,128,128]{1,2,0:T(8,128)}, u32[]{:S(2)}, u32[]{:S(2)}) async-start(f32[8,128,128]{1,2,0:T(8,128)} %bitcast.64), calls=%async_computation.7 | async-start | bytes 1048576 | tf_op jit(solution)/shard_map/all_to_all | solution.py:14

commit v7 on v6

--- a/solution.py
+++ b/solution.py
@@ -18,14 +18,14 @@
 def reduce_scatter_chip(matrix, vector, chips, precision):
     first = lax.axis_index("k") == 0
     blocks = matrix.reshape(chips, 2, matrix.shape[0] // (2 * chips), matrix.shape[1])
+    rows = blocks.shape[2]
     even, odd = (
-        jnp.einsum(
-            "xrb,bn->xrn",
-            blocks[:, half],
+        jnp.dot(
+            blocks[:, half].reshape(chips * rows, matrix.shape[1]),
             vector,
             precision=precision,
             preferred_element_type=jnp.float32,
-        )
+        ).reshape(chips, rows, vector.shape[1])
         for half in (0, 1)
     )
     mine = jnp.where(first, even, odd)

time: 151 us -> 150 us (level)
  blocking collectives: 71.5 us -> 58 us
  local copies, waits for them, and re-layouts: 8.52 us -> 17.9 us
  starting transfers between devices: 16 us -> 21.2 us
    all_to_all x2 -> x1, blocking collectives: 28.6 us -> 14.1 us  [reduce_scatter(): lax.all_to_all(x.reshape(n, x.shape[0] // n, x.shape[1]), axis, 0, 0, til...]
    slice x0 -> x1, local copies, waits for them, and re-layouts: none -> 8.36 us  [reduce_scatter_chip(): blocks[:, half].reshape(chips * rows, matrix.shape[1])]
    all_to_all x1 -> x2, waiting for transfers between devices: 8.79 us -> 16.9 us  [reduce_scatter(): lax.all_to_all(x.reshape(n, x.shape[0] // n, x.shape[1]), axis, 0, 0, til...]
    all_to_all x1, waiting for transfers between devices: 9.5 us -> 1.83 us  [gather(): lax.all_to_all(jnp.broadcast_to(x[None], (n,) + x.shape), axis, 0, 0, til...]
    all_to_all x1 -> x2, starting transfers between devices: 6.98 us -> 12.9 us  [reduce_scatter(): lax.all_to_all(x.reshape(n, x.shape[0] // n, x.shape[1]), axis, 0, 0, til...]
    dot_general x2, matrix products: 8.94 us -> 7.01 us  [reduce_scatter_chip(): jnp.dot(blocks[:, half].reshape(chips * rows, matrix.shape[1]), vector, p...]
  transfers between devices with their start and end apart: 4 -> 5, of which waited for: 4 -> 5; matrix products, arithmetic and copies ran while one was open for 2% -> 9% of each run, Pallas kernels for 0% -> 0%
where the time goes in v7:
time: 150 us; the launch traced here: 149 us
  blocking collectives  58 us (39%)
  waiting for transfers between devices  27.2 us (18%)
  starting transfers between devices  21.2 us (14%)
  matrix products  19.6 us (13%)
  local copies, waits for them, and re-layouts  17.9 us (12%)
  other arithmetic  4.53 us (3%)
    all_to_all x2, blocking collectives, gather(): lax.all_to_all(jnp.broadcast_to(x[None], (n,) + x.shape), axis, 0, 0, til...  22.9 us
    all_to_all x1, blocking collectives, local(): got = lax.all_to_all(packed, ALL, 0, 0, tiled=True)  21 us
    all_to_all x2, waiting for transfers between devices, reduce_scatter(): lax.all_to_all(x.reshape(n, x.shape[0] // n, x.shape[1]), axis, 0, 0, til...  16.9 us
    all_to_all x1, blocking collectives, reduce_scatter(): lax.all_to_all(x.reshape(n, x.shape[0] // n, x.shape[1]), axis, 0, 0, til...  14.1 us
    all_to_all x2, starting transfers between devices, reduce_scatter(): lax.all_to_all(x.reshape(n, x.shape[0] // n, x.shape[1]), axis, 0, 0, til...  12.9 us
    slice x1, local copies, waits for them, and re-layouts, reduce_scatter_chip(): blocks[:, half].reshape(chips * rows, matrix.shape[1])  8.36 us
    all_to_all x1, waiting for transfers between devices, reduce_scatter_chip(): got = lax.all_to_all(summed, 'x', 0, 0, tiled=False)  7.02 us
    dot_general x2, matrix products, reduce_scatter_chip(): jnp.dot(blocks[:, half].reshape(chips * rows, matrix.shape[1]), vector, p...  7.01 us
  transfers between devices with their start and end apart: 5, of which 5 were waited for; matrix products, arithmetic and copies ran while one was open for 9% of the time, Pallas kernels for 0%

profile of v7, /device:TPU:1, one launch (start us, length us, event | category | flops | bytes accessed | tf_op | source)
XLA Modules:
  0.0 149.4 jit_solution(13815469699833754354)
XLA Ops:
  0.6 6.7 %fusion.17 = f32[1024,128]{1,0:T(8,128)} fusion(f32[1024,1024]{1,0:T(8,128)} %param.11, f32[1024,128]{1,0:T(8,128)} %param.13), kind=kOutput, calls=%fused_computation.55 | convolution fusion | flops 805306368 | bytes 5242880 | tf_op jit(solution)/shard_map/dot_general | solution.py:62
  7.3 6.4 %all-to-all-start = ((f32[8,128,128]{2,1,0:T(8,128)}), f32[8,128,128]{2,1,0:T(8,128)S(1)}, u32[]{:S(2)}, u32[]{:S(2)}) async-start(f32[8,128,128]{2,1,0:T(8,128)} %bitcast), calls=%async_computation | async-start | bytes 1048576 | tf_op jit(solution)/shard_map/all_to_all | solution.py:14
  13.7 10.2 %all-to-all-done = f32[8,128,128]{2,1,0:T(8,128)S(1)} async-done(((f32[8,128,128]{2,1,0:T(8,128)}), f32[8,128,128]{2,1,0:T(8,128)S(1)}, u32[]{:S(2)}, u32[]{:S(2)}) %all-to-all-start) | async-done | bytes 524320 | tf_op jit(solution)/shard_map/all_to_all | solution.py:14
  24.1 0.8 broadcast_in_dim.10
  24.9 3.5 %all-to-all-start.1 = ((f32[8,128,128]{1,2,0:T(8,128)}), f32[8,128,128]{1,2,0:T(8,128)S(1)}, u32[]{:S(2)}, u32[]{:S(2)}) async-start(f32[8,128,128]{1,2,0:T(8,128)} %broadcast_in_dim.10), calls=%async_computation.1 | async-start | bytes 1048576 | tf_op jit(solution)/shard_map/all_to_all | solution.py:39
  28.4 8.4 %fusion.16 = (f32[4,1,256,1024]{3,2,1,0:T(8,128)}, f32[4,1,256,1024]{3,2,1,0:T(8,128)}) fusion(f32[4,2,256,1024]{3,2,1,0:T(8,128)} %bitcast.56), kind=kLoop, calls=%fused_computation.54 | loop fusion | bytes 16777216 | tf_op jit(solution)/shard_map/slice | solution.py:24
  36.8 1.8 %all-to-all-done.1 = f32[8,128,128]{1,2,0:T(8,128)S(1)} async-done(((f32[8,128,128]{1,2,0:T(8,128)}), f32[8,128,128]{1,2,0:T(8,128)S(1)}, u32[]{:S(2)}, u32[]{:S(2)}) %all-to-all-start.1) | async-done | bytes 524320 | tf_op jit(solution)/shard_map/all_to_all | solution.py:39
  38.8 4.6 %fusion.18 = f32[128,1024]{1,0:T(8,128)S(1)} fusion(f32[1024,128]{1,0:T(8,128)S(1)} %bitcast.53, f32[1024,1024]{1,0:T(8,128)} %bitcast.51), kind=kOutput, calls=%fused_computation.56 | convolution fusion | flops 805306368 | bytes 5242880 | tf_op jit(solution)/shard_map/dot_general | solution.py:23
  43.4 2.4 %broadcast_select_fusion.1 = (f32[128,1024]{1,0:T(8,128)S(1)}, f32[128,1024]{1,0:T(8,128)S(1)}) fusion(f32[128,1024]{1,0:T(8,128)S(1)} %fusion.18, pred[]{:T(512)S(6)} %eq.66, f32[1024,128]{1,0:T(8,128)S(1)} %bitcast.54, f32[1024,1024]{1,0:T(8,128)S(1)} %bitcast.52), kind=kOutput, calls=%fused_computation.13 | convolution fusion | flops 805568512 | bytes 6291457 | tf_op jit(solution)/shard_map/dot_general | solution.py:23
  45.9 0.8 copy.55
  46.7 0.8 collective-permute-start
  47.9 1.5 collective-permute-done
  49.4 1.9 %bitcast_add_fusion = f32[4,256,128]{1,2,0:T(8,128)} fusion(f32[4,256,128]{1,2,0:T(8,128)} %collective-permute-done, f32[16,4,8,256]{3,2,1,0:T(8,128)S(1)} %bitcast.59), kind=kLoop, calls=%fused_computation.5 | loop fusion | flops 131072 | bytes 1572864 | tf_op jit(solution)/shard_map/add | solution.py:33
  51.3 4.0 %all-to-all-start.2 = ((f32[4,256,128]{1,2,0:T(8,128)}), f32[4,256,128]{1,2,0:T(8,128)S(1)}, u32[]{:S(2)}, u32[]{:S(2)}) async-start(f32[4,256,128]{1,2,0:T(8,128)} %bitcast_add_fusion), calls=%async_computation.2 | async-start | bytes 1048576 | tf_op jit(solution)/shard_map/all_to_all | solution.py:34
  55.6 1.4 scatter_custom_fusion
  57.2 7.0 %all-to-all-done.2 = f32[4,256,128]{1,2,0:T(8,128)S(1)} async-done(((f32[4,256,128]{1,2,0:T(8,128)}), f32[4,256,128]{1,2,0:T(8,128)S(1)}, u32[]{:S(2)}, u32[]{:S(2)}) %all-to-all-start.2) | async-done | bytes 524320 | tf_op jit(solution)/shard_map/all_to_all | solution.py:34
  64.2 0.4 fusion
  64.7 21.0 %all_to_all.40 = f32[128,5,128]{2,1,0:T(8,128)S(1)} all-to-all(f32[128,5,128]{2,1,0:T(8,128)S(1)} %pad_maximum_fusion), channel_id=1, replica_groups=mesh['h'=2,'r8'=8,'x'=4,'k'=2] {'h','r8','x','k'}, dimensions={0} | all-to-all | bytes 655360 | tf_op jit(solution)/shard_map/all_to_all | solution.py:100
  86.6 9.8 %all_to_all.41 = f32[8,64,128]{2,1,0:T(8,128)S(1)} all-to-all(f32[8,64,128]{2,1,0:T(8,128)S(1)} %broadcast_in_dim.13), channel_id=1, replica_groups=mesh['h'=2,'r8'=8,'x'=4,'k'=2] {'x','k'}, dimensions={0} | all-to-all | bytes 524288 | tf_op jit(solution)/shard_map/all_to_all | solution.py:39
  96.4 0.7 convolution_bitcast_fusion
  97.2 1.0 copy.41
  98.2 14.1 %all_to_all.42 = f32[16,64,128]{2,1,0:T(8,128)S(1)} all-to-all(f32[16,64,128]{2,1,0:T(8,128)} %bitcast.62), channel_id=1, replica_groups=mesh['h'=2,'r8'=8,'x'=4,'k'=2] {'h','r8'}, dimensions={0} | all-to-all | bytes 1048576 | tf_op jit(solution)/shard_map/all_to_all | solution.py:14
  112.3 13.1 %all_to_all.43 = f32[16,64,128]{2,1,0:T(8,128)S(1)} all-to-all(f32[16,64,128]{2,1,0:T(8,128)S(1)} %broadcast_in_dim.14), channel_id=1, replica_groups=mesh['h'=2,'r8'=8,'x'=4,'k'=2] {'h','r8'}, dimensions={0} | all-to-all | bytes 1048576 | tf_op jit(solution)/shard_map/all_to_all | solution.py:39
  125.4 4.5 %convolution_bitcast_fusion.1 = f32[16,8,8,128]{3,2,1,0:T(8,128)S(1)} fusion(f32[1024,128]{1,0:T(8,128)S(1)} %bitcast.57, f32[1024,1024]{1,0:T(8,128)} %param.17), kind=kOutput, calls=%fused_computation.2 | convolution fusion | flops 805306368 | bytes 5242880 | tf_op jit(solution)/shard_map/dot_general | solution.py:118
  129.9 0.8 copy.54
  130.7 6.5 %all-to-all-start.7 = ((f32[8,128,128]{1,2,0:T(8,128)}), f32[8,128,128]{1,2,0:T(8,128)}, u32[]{:S(2)}, u32[]{:S(2)}) async-start(f32[8,128,128]{1,2,0:T(8,128)} %bitcast.61), calls=%async_computation.7 | async-start | bytes 1048576 | tf_op jit(solution)/shard_map/all_to_all | solution.py:14
  137.3 1.0 constant_dynamic-slice_fusion
  138.3 1.8 %copy.45 = f32[1024,16]{0,1:T(8,128)} copy(f32[1024,16]{1,0:T(8,128)} %constant_dynamic-slice_fusion) | data formatting | bytes 131072
  140.1 6.6 %all-to-all-done.7 = f32[8,128,128]{1,2,0:T(8,128)} async-done(((f32[8,128,128]{1,2,0:T(8,128)}), f32[8,128,128]{1,2,0:T(8,128)}, u32[]{:S(2)}, u32[]{:S(2)}) %all-to-all-start.7) | async-done | bytes 524320 | tf_op jit(solution)/shard_map/all_to_all | solution.py:14
  146.7 1.1 reduce_sum.49
  147.9 0.6 fusion.8
  148.6 0.8 copy.57
  (41 shorter events, 2.2 us)
Async XLA Ops:
  0.6 95.8 %copy-start = (f32[512,1024]{1,0:T(8,128)S(1)}, f32[512,1024]{1,0:T(8,128)}, u32[]{:S(2)}) copy-start(f32[512,1024]{1,0:T(8,128)} %param.16) | copy-start | bytes 6291460
  7.3 16.6 %all-to-all-start = ((f32[8,128,128]{2,1,0:T(8,128)}), f32[8,128,128]{2,1,0:T(8,128)S(1)}, u32[]{:S(2)}, u32[]{:S(2)}) async-start(f32[8,128,128]{2,1,0:T(8,128)} %bitcast), calls=%async_computation | async-start | bytes 1048576 | tf_op jit(solution)/shard_map/all_to_all | solution.py:14
  24.9 13.7 %all-to-all-start.1 = ((f32[8,128,128]{1,2,0:T(8,128)}), f32[8,128,128]{1,2,0:T(8,128)S(1)}, u32[]{:S(2)}, u32[]{:S(2)}) async-start(f32[8,128,128]{1,2,0:T(8,128)} %broadcast_in_dim.10), calls=%async_computation.1 | async-start | bytes 1048576 | tf_op jit(solution)/shard_map/all_to_all | solution.py:39
  38.8 4.6 %copy-start.1 = (f32[4,1,256,1024]{3,2,1,0:T(8,128)S(1)}, f32[4,1,256,1024]{3,2,1,0:T(8,128)}, u32[]{:S(2)}) copy-start(f32[4,1,256,1024]{3,2,1,0:T(8,128)} %get-tuple-element.18) | copy-start | bytes 12582916
  43.4 4.1 %copy-start.5 = (s32[256]{0:T(256)S(1)}, s32[256]{0:T(256)}, u32[]{:S(2)}) copy-start(s32[256]{0:T(256)} %param.15) | copy-start | bytes 3076
  43.4 11.9 %copy-start.2 = (f32[256,128]{1,0:T(8,128)S(1)}, f32[256,128]{1,0:T(8,128)}, u32[]{:S(2)}) copy-start(f32[256,128]{1,0:T(8,128)} %param.14) | copy-start | bytes 393220
  46.7 2.7 %collective-permute-start = (f32[4,256,128]{1,2,0:T(8,128)}, f32[4,256,128]{1,2,0:T(8,128)}, u32[]{:S(2)}, u32[]{:S(2)}) collective-permute-start(f32[4,256,128]{1,2,0:T(8,128)} %bitcast.47), channel_id=1, source_target_pairs={{0,1},{1,0},{2,3},{3,2},{4,5},{5,4},{6,7},{7,6},{8,9},{9,8},{10,11... | collective-permute-start | bytes 1572872 | tf_op jit(solution)/shard_map/ppermute | solution.py:33
  51.3 12.9 %all-to-all-start.2 = ((f32[4,256,128]{1,2,0:T(8,128)}), f32[4,256,128]{1,2,0:T(8,128)S(1)}, u32[]{:S(2)}, u32[]{:S(2)}) async-start(f32[4,256,128]{1,2,0:T(8,128)} %bitcast_add_fusion), calls=%async_computation.2 | async-start | bytes 1048576 | tf_op jit(solution)/shard_map/all_to_all | solution.py:34
  55.4 31.1 %copy-start.4 = (f32[64,128]{1,0:T(8,128)S(1)}, f32[64,128]{1,0:T(8,128)}, u32[]{:S(2)}) copy-start(f32[64,128]{1,0:T(8,128)} %param.18) | copy-start | bytes 98308
  125.4 22.5 %copy-start.3 = (f32[128,128]{1,0:T(8,128)S(1)}, f32[128,128]{1,0:T(8,128)}, u32[]{:S(2)}) copy-start(f32[128,128]{1,0:T(8,128)} %param.19) | copy-start | bytes 196612
  130.7 16.0 %all-to-all-start.7 = ((f32[8,128,128]{1,2,0:T(8,128)}), f32[8,128,128]{1,2,0:T(8,128)}, u32[]{:S(2)}, u32[]{:S(2)}) async-start(f32[8,128,128]{1,2,0:T(8,128)} %bitcast.61), calls=%async_computation.7 | async-start | bytes 1048576 | tf_op jit(solution)/shard_map/all_to_all | solution.py:14

commit v8 on v6

--- a/solution.py
+++ b/solution.py
@@ -33,6 +33,13 @@
     summed = mine + lax.ppermute(other, "k", [(0, 1), (1, 0)])
     got = lax.all_to_all(summed, "x", 0, 0, tiled=False)
     return got.sum(axis=0)
+
+
+def gather_chip(x, chips):
+    first = lax.axis_index("k") == 0
+    pair = lax.ppermute(x, "k", [(0, 1), (1, 0)])
+    both = jnp.concatenate([jnp.where(first, x, pair), jnp.where(first, pair, x)], axis=0)
+    return gather(both, "x", chips)
 
 
 def gather(x, axis, n):
@@ -108,17 +115,13 @@
     border_rows = parent_border_rhs + received[sep_dev:]
     partial_sep = lax.dot_general(
         parent_inverse,
-        gather(sep_rows, COL, cols_axis),
+        gather_chip(sep_rows, chips),
         contract_rows,
         precision=highest,
         preferred_element_type=jnp.float32,
     )
     parent_solution = gather(reduce_scatter(partial_sep, ROW, rows_axis), ROW, rows_axis)
-    carried_parent = reduce_scatter(
-        jnp.dot(parent_border, parent_solution, precision=highest, preferred_element_type=jnp.float32),
-        COL,
-        cols_axis,
-    )
+    carried_parent = reduce_scatter_chip(parent_border, parent_solution, chips, highest)
     parent_contribution = border_rows - carried_parent
     return (child_part, parent_solution, parent_contribution)
 

time: 151 us -> 150 us (level)
  other arithmetic: 5.46 us -> 7.68 us
  blocking collectives: 71.5 us -> 69.9 us
    all_to_all x1 -> x0, waiting for transfers between devices: 8.79 us -> none  [reduce_scatter(): lax.all_to_all(x.reshape(n, x.shape[0] // n, x.shape[1]), axis, 0, 0, til...]
    all_to_all x1 -> x0, starting transfers between devices: 6.98 us -> none  [reduce_scatter(): lax.all_to_all(x.reshape(n, x.shape[0] // n, x.shape[1]), axis, 0, 0, til...]
    all_to_all x1 -> x2, waiting for transfers between devices: 7.03 us -> 12.3 us  [reduce_scatter_chip(): got = lax.all_to_all(summed, 'x', 0, 0, tiled=False)]
    dot_general x2 -> x1, matrix products: 5.21 us -> 0.73 us  [local(): lax.dot_general(parent_inverse, gather_chip(sep_rows, chips), contract_ro...]
    dot_general x2 -> x4, matrix products: 8.94 us -> 13 us  [reduce_scatter_chip(): jnp.einsum('xrb,bn->xrn', blocks[:, half], vector, precision=precision, p...]
    all_to_all x1 -> x2, starting transfers between devices: 4.02 us -> 7.42 us  [reduce_scatter_chip(): got = lax.all_to_all(summed, 'x', 0, 0, tiled=False)]
    ppermute x1 -> x2, starting transfers between devices: 1.47 us -> 4.59 us  [reduce_scatter_chip(): summed = mine + lax.ppermute(other, 'k', [(0, 1), (1, 0)])]
    add x1 -> x2, other arithmetic: 1.95 us -> 3.65 us  [reduce_scatter_chip(): summed = mine + lax.ppermute(other, 'k', [(0, 1), (1, 0)])]
  transfers between devices with their start and end apart: 4 -> 6, of which waited for: 4 -> 6; matrix products, arithmetic and copies ran while one was open for 2% -> 2% of each run, Pallas kernels for 0% -> 0%
where the time goes in v8:
time: 150 us; the launch traced here: 149 us
  blocking collectives  69.9 us (47%)
  waiting for transfers between devices  25.7 us (17%)
  matrix products  20.4 us (14%)
  starting transfers between devices  16.6 us (11%)
  local copies, waits for them, and re-layouts  8.36 us (6%)
  other arithmetic  7.68 us (5%)
    all_to_all x2, blocking collectives, reduce_scatter(): lax.all_to_all(x.reshape(n, x.shape[0] // n, x.shape[1]), axis, 0, 0, til...  28.2 us
    all_to_all x2, blocking collectives, gather(): lax.all_to_all(jnp.broadcast_to(x[None], (n,) + x.shape), axis, 0, 0, til...  21.4 us
    all_to_all x1, blocking collectives, local(): got = lax.all_to_all(packed, ALL, 0, 0, tiled=True)  20.3 us
    dot_general x4, matrix products, reduce_scatter_chip(): jnp.einsum('xrb,bn->xrn', blocks[:, half], vector, precision=precision, p...  13 us
    all_to_all x2, waiting for transfers between devices, reduce_scatter_chip(): got = lax.all_to_all(summed, 'x', 0, 0, tiled=False)  12.3 us
    all_to_all x1, waiting for transfers between devices, gather(): lax.all_to_all(jnp.broadcast_to(x[None], (n,) + x.shape), axis, 0, 0, til...  9.5 us
    all_to_all x2, starting transfers between devices, reduce_scatter_chip(): got = lax.all_to_all(summed, 'x', 0, 0, tiled=False)  7.42 us
    dot_general x1, matrix products, local(): lax.dot_general(child_inverse, child_sep_rhs, contract_rows, precision=hi...  5.88 us
  transfers between devices with their start and end apart: 6, of which 6 were waited for; matrix products, arithmetic and copies ran while one was open for 2% of the time, Pallas kernels for 0%

profile of v8, /device:TPU:1, one launch (start us, length us, event | category | flops | bytes accessed | tf_op | source)
XLA Modules:
  0.0 149.5 jit_solution(10592320375007044171)
XLA Ops:
  0.6 5.9 %fusion.20 = f32[1024,128]{1,0:T(8,128)S(1)} fusion(f32[1024,1024]{1,0:T(8,128)} %param.11, f32[1024,128]{1,0:T(8,128)} %param.13), kind=kOutput, calls=%fused_computation.64 | convolution fusion | flops 805306368 | bytes 5242880 | tf_op jit(solution)/shard_map/dot_general | solution.py:69
  6.5 15.4 %all_to_all.40 = f32[8,128,128]{2,1,0:T(8,128)S(1)} all-to-all(f32[8,128,128]{2,1,0:T(8,128)S(1)} %bitcast.78), channel_id=1, replica_groups=mesh['h'=2,'r8'=8,'x'=4,'k'=2] {'r8'}, dimensions={0} | all-to-all | bytes 1048576 | tf_op jit(solution)/shard_map/all_to_all | solution.py:14
  22.0 0.8 broadcast_in_dim.10
  22.9 3.5 %all-to-all-start.1 = ((f32[8,128,128]{1,2,0:T(8,128)}), f32[8,128,128]{1,2,0:T(8,128)S(1)}, u32[]{:S(2)}, u32[]{:S(2)}) async-start(f32[8,128,128]{1,2,0:T(8,128)} %broadcast_in_dim.10), calls=%async_computation.1 | async-start | bytes 1048576 | tf_op jit(solution)/shard_map/all_to_all | solution.py:46
  26.4 9.5 %all-to-all-done.1 = f32[8,128,128]{1,2,0:T(8,128)S(1)} async-done(((f32[8,128,128]{1,2,0:T(8,128)}), f32[8,128,128]{1,2,0:T(8,128)S(1)}, u32[]{:S(2)}, u32[]{:S(2)}) %all-to-all-start.1) | async-done | bytes 524320 | tf_op jit(solution)/shard_map/all_to_all | solution.py:46
  35.9 1.1 copy.34
  37.0 1.1 reshape.123
  38.1 0.8 copy-done.1
  38.9 4.4 %fusion = f32[128,4,256]{2,0,1:T(8,128)S(1)} fusion(f32[1024,128,1]{0,1,2:T(8,128)S(1)} %reshape.123, f32[4,2,256,1024]{3,2,1,0:T(8,128)} %bitcast.71), kind=kOutput, calls=%fused_computation.2 | convolution fusion | flops 805306368 | bytes 5242880 | tf_op jit(solution)/shard_map/xrb,bn->xrn/dot_general | solution.py:22
  43.3 4.6 %fusion.1 = f32[128,4,256]{2,0,1:T(8,128)S(1)} fusion(f32[1024,128,1]{0,1,2:T(8,128)} %copy-done.1, f32[4,2,256,1024]{3,2,1,0:T(8,128)} %bitcast.72), kind=kOutput, calls=%fused_computation.4 | convolution fusion | flops 805306368 | bytes 5242880 | tf_op jit(solution)/shard_map/xrb,bn->xrn/dot_general | solution.py:22
  47.9 0.9 select_bitcast_fusion
  48.8 1.5 collective-permute-start
  50.6 1.5 collective-permute-done
  52.1 2.0 %bitcast_add_fusion = f32[4,256,128]{1,2,0:T(8,128)} fusion(f32[4,256,128]{1,2,0:T(8,128)} %collective-permute-done, f32[128,4,256]{2,0,1:T(8,128)S(1)} %fusion.1, f32[128,4,256]{2,0,1:T(8,128)S(1)} %fusion, pred[]{:T(512)S(6)} %eq.57), kind=kLoop, calls=%fused_computation.12 | loop fusion | flops 262144 | bytes 2097153 | tf_op jit(solution)/shard_map/add | solution.py:33
  54.1 4.0 %all-to-all-start.2 = ((f32[4,256,128]{1,2,0:T(8,128)}), f32[4,256,128]{1,2,0:T(8,128)S(1)}, u32[]{:S(2)}, u32[]{:S(2)}) async-start(f32[4,256,128]{1,2,0:T(8,128)} %bitcast_add_fusion), calls=%async_computation.2 | async-start | bytes 1048576 | tf_op jit(solution)/shard_map/all_to_all | solution.py:34
  58.3 1.4 scatter_custom_fusion
  60.0 7.0 %all-to-all-done.2 = f32[4,256,128]{1,2,0:T(8,128)S(1)} async-done(((f32[4,256,128]{1,2,0:T(8,128)}), f32[4,256,128]{1,2,0:T(8,128)S(1)}, u32[]{:S(2)}, u32[]{:S(2)}) %all-to-all-start.2) | async-done | bytes 524320 | tf_op jit(solution)/shard_map/all_to_all | solution.py:34
  67.6 20.3 %all_to_all.41 = f32[128,5,128]{2,1,0:T(8,128)S(1)} all-to-all(f32[128,5,128]{2,1,0:T(8,128)S(1)} %pad_maximum_fusion), channel_id=1, replica_groups=mesh['h'=2,'r8'=8,'x'=4,'k'=2] {'h','r8','x','k'}, dimensions={0} | all-to-all | bytes 655360 | tf_op jit(solution)/shard_map/all_to_all | solution.py:107
  88.6 1.0 collective-permute-start.1
  89.7 0.9 collective-permute-done.1
  90.6 8.8 %all_to_all.42 = f32[4,128,128]{2,1,0:T(8,128)S(1)} all-to-all(f32[4,128,128]{2,1,0:T(8,128)S(1)} %broadcast_in_dim.13), channel_id=1, replica_groups=mesh['h'=2,'r8'=8,'x'=4,'k'=2] {'x'}, dimensions={0} | all-to-all | bytes 524288 | tf_op jit(solution)/shard_map/all_to_all | solution.py:46
  100.3 12.8 %all_to_all.43 = f32[16,64,128]{2,1,0:T(8,128)S(1)} all-to-all(f32[16,64,128]{2,1,0:T(8,128)S(1)} %bitcast.79), channel_id=1, replica_groups=mesh['h'=2,'r8'=8,'x'=4,'k'=2] {'h','r8'}, dimensions={0} | all-to-all | bytes 1048576 | tf_op jit(solution)/shard_map/all_to_all | solution.py:14
  113.2 12.6 %all_to_all.44 = f32[16,64,128]{2,1,0:T(8,128)S(1)} all-to-all(f32[16,64,128]{2,1,0:T(8,128)S(1)} %broadcast_in_dim.14), channel_id=1, replica_groups=mesh['h'=2,'r8'=8,'x'=4,'k'=2] {'h','r8'}, dimensions={0} | all-to-all | bytes 1048576 | tf_op jit(solution)/shard_map/all_to_all | solution.py:46
  125.8 2.9 %fusion.2 = f32[128,4,128]{2,0,1:T(8,128)S(1)} fusion(f32[1024,128,1]{1,0,2:T(8,128)S(1)} %bitcast.73, f32[4,2,128,1024]{3,2,1,0:T(8,128)} %bitcast.76), kind=kOutput, calls=%fused_computation.6 | convolution fusion | flops 402653184 | bytes 2883584 | tf_op jit(solution)/shard_map/xrb,bn->xrn/dot_general | solution.py:22
  128.7 1.2 fusion.3
  131.4 3.1 %collective-permute-start.2 = (f32[4,128,128]{1,2,0:T(8,128)}, f32[4,128,128]{1,2,0:T(8,128)}, u32[]{:S(2)}, u32[]{:S(2)}) collective-permute-start(f32[4,128,128]{1,2,0:T(8,128)} %select_bitcast_fusion.1), channel_id=1, source_target_pairs={{0,1},{1,0},{2,3},{3,2},{4,5},{5,4},{6,7},{7,6},{8,9},{9,8},{10,11... | collective-permute-start | bytes 786440 | tf_op jit(solution)/shard_map/ppermute | solution.py:33
  134.5 1.5 %collective-permute-done.2 = f32[4,128,128]{1,2,0:T(8,128)} collective-permute-done((f32[4,128,128]{1,2,0:T(8,128)}, f32[4,128,128]{1,2,0:T(8,128)}, u32[]{:S(2)}, u32[]{:S(2)}) %collective-permute-start.2) | collective-permute-done | bytes 262176 | tf_op jit(solution)/shard_map/ppermute | solution.py:33
  136.0 1.7 %bitcast_add_fusion.1 = f32[4,128,128]{1,2,0:T(8,128)} fusion(f32[4,128,128]{1,2,0:T(8,128)} %collective-permute-done.2, f32[128,4,128]{2,0,1:T(8,128)} %copy-done.5, f32[128,4,128]{2,0,1:T(8,128)S(1)} %fusion.2, pred[]{:T(512)S(6)} %eq.57), kind=kLoop, calls=%fused_computation.18 | loop fusion | flops 131072 | bytes 1048577 | tf_op jit(solution)/shard_map/add | solution.py:33
  137.7 3.4 %all-to-all-start.7 = ((f32[4,128,128]{1,2,0:T(8,128)}), f32[4,128,128]{1,2,0:T(8,128)S(1)}, u32[]{:S(2)}, u32[]{:S(2)}) async-start(f32[4,128,128]{1,2,0:T(8,128)} %bitcast_add_fusion.1), calls=%async_computation.7 | async-start | bytes 524288 | tf_op jit(solution)/shard_map/all_to_all | solution.py:34
  141.8 5.3 %all-to-all-done.7 = f32[4,128,128]{1,2,0:T(8,128)S(1)} async-done(((f32[4,128,128]{1,2,0:T(8,128)}), f32[4,128,128]{1,2,0:T(8,128)S(1)}, u32[]{:S(2)}, u32[]{:S(2)}) %all-to-all-start.7) | async-done | bytes 262176 | tf_op jit(solution)/shard_map/all_to_all | solution.py:34
  147.2 1.5 fusion.12
  148.7 0.8 copy.58
  (54 shorter events, 5.5 us)
Async XLA Ops:
  0.6 98.8 %copy-start = (f32[512,1024]{1,0:T(8,128)S(1)}, f32[512,1024]{1,0:T(8,128)}, u32[]{:S(2)}) copy-start(f32[512,1024]{1,0:T(8,128)} %param.16) | copy-start | bytes 6291460
  22.9 13.0 %all-to-all-start.1 = ((f32[8,128,128]{1,2,0:T(8,128)}), f32[8,128,128]{1,2,0:T(8,128)S(1)}, u32[]{:S(2)}, u32[]{:S(2)}) async-start(f32[8,128,128]{1,2,0:T(8,128)} %broadcast_in_dim.10), calls=%async_computation.1 | async-start | bytes 1048576 | tf_op jit(solution)/shard_map/all_to_all | solution.py:46
  35.9 2.2 %copy-start.2 = (f32[8,128,128]{1,2,0:T(8,128)}, f32[8,128,128]{1,2,0:T(8,128)S(1)}, u32[]{:S(2)}) copy-start(f32[8,128,128]{1,2,0:T(8,128)S(1)} %all-to-all-done.1) | copy-start | bytes 1572868
  38.1 0.8 copy-start.1
  43.3 6.9 %copy-start.8 = (s32[256]{0:T(256)S(1)}, s32[256]{0:T(256)}, u32[]{:S(2)}) copy-start(s32[256]{0:T(256)} %param.15) | copy-start | bytes 3076
  47.9 12.0 %copy-start.6 = (f32[256,128]{1,0:T(8,128)S(1)}, f32[256,128]{1,0:T(8,128)}, u32[]{:S(2)}) copy-start(f32[256,128]{1,0:T(8,128)} %param.14) | copy-start | bytes 393220
  48.8 3.3 %collective-permute-start = (f32[4,256,128]{1,2,0:T(8,128)}, f32[4,256,128]{1,2,0:T(8,128)}, u32[]{:S(2)}, u32[]{:S(2)}) collective-permute-start(f32[4,256,128]{1,2,0:T(8,128)} %select_bitcast_fusion), channel_id=1, source_target_pairs={{0,1},{1,0},{2,3},{3,2},{4,5},{5,4},{6,7},{7,6},{8,9},{9,8},{10,11... | collective-permute-start | bytes 1572872 | tf_op jit(solution)/shard_map/ppermute | solution.py:33
  50.6 38.0 %copy-start.7 = (f32[64,128]{1,0:T(8,128)S(1)}, f32[64,128]{1,0:T(8,128)}, u32[]{:S(2)}) copy-start(f32[64,128]{1,0:T(8,128)} %param.18) | copy-start | bytes 98308
  54.1 12.9 %all-to-all-start.2 = ((f32[4,256,128]{1,2,0:T(8,128)}), f32[4,256,128]{1,2,0:T(8,128)S(1)}, u32[]{:S(2)}, u32[]{:S(2)}) async-start(f32[4,256,128]{1,2,0:T(8,128)} %bitcast_add_fusion), calls=%async_computation.2 | async-start | bytes 1048576 | tf_op jit(solution)/shard_map/all_to_all | solution.py:34
  88.6 1.9 %collective-permute-start.1 = (f32[64,128]{1,0:T(8,128)S(1)}, f32[64,128]{1,0:T(8,128)S(1)}, u32[]{:S(2)}, u32[]{:S(2)}) collective-permute-start(f32[64,128]{1,0:T(8,128)S(1)} %slice_add_fusion.1), channel_id=1, source_target_pairs={{0,1},{1,0},{2,3},{3,2},{4,5},{5,4},{6,7},{7,6},{8,9},{9,8},{10,11... | collective-permute-start | bytes 98312 | tf_op jit(solution)/shard_map/ppermute | solution.py:40
  113.1 15.6 %copy-start.4 = (f32[1024,1024]{1,0:T(8,128)S(1)}, f32[1024,1024]{1,0:T(8,128)}, u32[]{:S(2)}) copy-start(f32[1024,1024]{1,0:T(8,128)} %param.17) | copy-start | bytes 12582916
  125.8 15.3 %copy-start.3 = (f32[8,128,128]{1,2,0:T(8,128)S(1)}, f32[8,128,128]{1,2,0:T(8,128)}, u32[]{:S(2)}) copy-start(f32[8,128,128]{1,2,0:T(8,128)} %copy-done.2) | copy-start | bytes 1572868
  129.9 0.7 copy-start.5
  131.4 4.6 %collective-permute-start.2 = (f32[4,128,128]{1,2,0:T(8,128)}, f32[4,128,128]{1,2,0:T(8,128)}, u32[]{:S(2)}, u32[]{:S(2)}) collective-permute-start(f32[4,128,128]{1,2,0:T(8,128)} %select_bitcast_fusion.1), channel_id=1, source_target_pairs={{0,1},{1,0},{2,3},{3,2},{4,5},{5,4},{6,7},{7,6},{8,9},{9,8},{10,11... | collective-permute-start | bytes 786440 | tf_op jit(solution)/shard_map/ppermute | solution.py:33
  137.7 9.4 %all-to-all-start.7 = ((f32[4,128,128]{1,2,0:T(8,128)}), f32[4,128,128]{1,2,0:T(8,128)S(1)}, u32[]{:S(2)}, u32[]{:S(2)}) async-start(f32[4,128,128]{1,2,0:T(8,128)} %bitcast_add_fusion.1), calls=%async_computation.7 | async-start | bytes 524288 | tf_op jit(solution)/shard_map/all_to_all | solution.py:34

commit v9 on v7

--- a/solution.py
+++ b/solution.py
@@ -17,22 +17,20 @@
 
 def reduce_scatter_chip(matrix, vector, chips, precision):
     first = lax.axis_index("k") == 0
-    blocks = matrix.reshape(chips, 2, matrix.shape[0] // (2 * chips), matrix.shape[1])
-    rows = blocks.shape[2]
-    even, odd = (
-        jnp.dot(
-            blocks[:, half].reshape(chips * rows, matrix.shape[1]),
-            vector,
-            precision=precision,
-            preferred_element_type=jnp.float32,
-        ).reshape(chips, rows, vector.shape[1])
-        for half in (0, 1)
+    product = lax.dot_general(
+        vector,
+        matrix,
+        (((0,), (1,)), ((), ())),
+        precision=precision,
+        preferred_element_type=jnp.float32,
     )
+    blocks = product.reshape(product.shape[0], chips, 2, matrix.shape[0] // (2 * chips))
+    even, odd = blocks[:, :, 0], blocks[:, :, 1]
     mine = jnp.where(first, even, odd)
     other = jnp.where(first, odd, even)
     summed = mine + lax.ppermute(other, "k", [(0, 1), (1, 0)])
-    got = lax.all_to_all(summed, "x", 0, 0, tiled=False)
-    return got.sum(axis=0)
+    got = lax.all_to_all(summed, "x", 1, 1, tiled=False)
+    return got.sum(axis=1).T
 
 
 def gather(x, axis, n):

time: 150 us -> 148 us (0.987)
  blocking collectives: 58 us -> 71.5 us
  local copies, waits for them, and re-layouts: 17.9 us -> 6.7 us
  starting transfers between devices: 21.2 us -> 15.9 us
    all_to_all x1 -> x2, blocking collectives: 14.1 us -> 28.6 us  [reduce_scatter(): lax.all_to_all(x.reshape(n, x.shape[0] // n, x.shape[1]), axis, 0, 0, til...]
    slice x1 -> x0, local copies, waits for them, and re-layouts: 8.36 us -> none  [reduce_scatter_chip(): blocks[:, half].reshape(chips * rows, matrix.shape[1])]
    all_to_all x2 -> x1, waiting for transfers between devices: 16.9 us -> 8.79 us  [reduce_scatter(): lax.all_to_all(x.reshape(n, x.shape[0] // n, x.shape[1]), axis, 0, 0, til...]
    all_to_all x1, waiting for transfers between devices: 1.83 us -> 9.5 us  [gather(): lax.all_to_all(jnp.broadcast_to(x[None], (n,) + x.shape), axis, 0, 0, til...]
    all_to_all x2 -> x1, starting transfers between devices: 12.9 us -> 6.97 us  [reduce_scatter(): lax.all_to_all(x.reshape(n, x.shape[0] // n, x.shape[1]), axis, 0, 0, til...]
    unnamed x16 -> x17, local copies, waits for them, and re-layouts: 2.77 us -> 0.93 us
    dot_general x2 -> x1, matrix products: 7.01 us -> 7.82 us  [reduce_scatter_chip(): lax.dot_general(vector, matrix, (((0,), (1,)), ((), ())), precision=preci...]
  transfers between devices with their start and end apart: 5 -> 4, of which waited for: 5 -> 4; matrix products, arithmetic and copies ran while one was open for 9% -> 2% of each run, Pallas kernels for 0% -> 0%
where the time goes in v9:
time: 148 us; the launch traced here: 147 us
  blocking collectives  71.5 us (48%)
  waiting for transfers between devices  26.8 us (18%)
  matrix products  19.6 us (13%)
  starting transfers between devices  15.9 us (11%)
  local copies, waits for them, and re-layouts  6.7 us (5%)
  other arithmetic  5.46 us (4%)
    all_to_all x2, blocking collectives, reduce_scatter(): lax.all_to_all(x.reshape(n, x.shape[0] // n, x.shape[1]), axis, 0, 0, til...  28.6 us
    all_to_all x2, blocking collectives, gather(): lax.all_to_all(jnp.broadcast_to(x[None], (n,) + x.shape), axis, 0, 0, til...  22.5 us
    all_to_all x1, blocking collectives, local(): got = lax.all_to_all(packed, ALL, 0, 0, tiled=True)  20.3 us
    all_to_all x1, waiting for transfers between devices, gather(): lax.all_to_all(jnp.broadcast_to(x[None], (n,) + x.shape), axis, 0, 0, til...  9.5 us
    all_to_all x1, waiting for transfers between devices, reduce_scatter(): lax.all_to_all(x.reshape(n, x.shape[0] // n, x.shape[1]), axis, 0, 0, til...  8.79 us
    dot_general x1, matrix products, reduce_scatter_chip(): lax.dot_general(vector, matrix, (((0,), (1,)), ((), ())), precision=preci...  7.82 us
    all_to_all x1, waiting for transfers between devices, reduce_scatter_chip(): got = lax.all_to_all(summed, 'x', 1, 1, tiled=False)  7.03 us
    all_to_all x1, starting transfers between devices, reduce_scatter(): lax.all_to_all(x.reshape(n, x.shape[0] // n, x.shape[1]), axis, 0, 0, til...  6.97 us
  transfers between devices with their start and end apart: 4, of which 4 were waited for; matrix products, arithmetic and copies ran while one was open for 2% of the time, Pallas kernels for 0%

profile of v9, /device:TPU:1, one launch (start us, length us, event | category | flops | bytes accessed | tf_op | source)
XLA Modules:
  0.0 146.9 jit_solution(13642801063027654376)
XLA Ops:
  0.6 5.9 %fusion.19 = f32[1024,128]{1,0:T(8,128)S(1)} fusion(f32[1024,1024]{1,0:T(8,128)} %param.11, f32[1024,128]{1,0:T(8,128)} %param.13), kind=kOutput, calls=%fused_computation.57 | convolution fusion | flops 805306368 | bytes 5242880 | tf_op jit(solution)/shard_map/dot_general | solution.py:60
  6.5 15.4 %all_to_all.40 = f32[8,128,128]{2,1,0:T(8,128)S(1)} all-to-all(f32[8,128,128]{2,1,0:T(8,128)S(1)} %bitcast.71), channel_id=1, replica_groups=mesh['h'=2,'r8'=8,'x'=4,'k'=2] {'r8'}, dimensions={0} | all-to-all | bytes 1048576 | tf_op jit(solution)/shard_map/all_to_all | solution.py:14
  22.0 0.8 broadcast_in_dim.10
  22.9 3.5 %all-to-all-start.1 = ((f32[8,128,128]{1,2,0:T(8,128)}), f32[8,128,128]{1,2,0:T(8,128)S(1)}, u32[]{:S(2)}, u32[]{:S(2)}) async-start(f32[8,128,128]{1,2,0:T(8,128)} %broadcast_in_dim.10), calls=%async_computation.1 | async-start | bytes 1048576 | tf_op jit(solution)/shard_map/all_to_all | solution.py:37
  26.4 9.5 %all-to-all-done.1 = f32[8,128,128]{1,2,0:T(8,128)S(1)} async-done(((f32[8,128,128]{1,2,0:T(8,128)}), f32[8,128,128]{1,2,0:T(8,128)S(1)}, u32[]{:S(2)}, u32[]{:S(2)}) %all-to-all-start.1) | async-done | bytes 524320 | tf_op jit(solution)/shard_map/all_to_all | solution.py:37
  35.9 0.3 copy.33
  36.2 0.9 reshape.125
  37.1 7.8 %fusion.2 = f32[128,4,2,256]{3,0,2,1:T(8,128)S(1)} fusion(f32[4,2,256,1024]{3,2,1,0:T(8,128)} %bitcast.68, f32[1024,128,1,1]{0,1,2,3:T(8,128)} %reshape.125), kind=kOutput, calls=%fused_computation.9 | convolution fusion | flops 1610612736 | bytes 9961472 | tf_op jit(solution)/shard_map/dot_general | solution.py:20
  44.9 0.9 select_bitcast_fusion
  45.8 1.5 collective-permute-start
  47.4 0.2 fusion.8
  47.7 1.5 %collective-permute-done = f32[128,4,256]{2,0,1:T(8,128)} collective-permute-done((f32[128,4,256]{2,0,1:T(8,128)}, f32[128,4,256]{2,0,1:T(8,128)}, u32[]{:S(2)}, u32[]{:S(2)}) %collective-permute-start) | collective-permute-done | bytes 524320 | tf_op jit(solution)/shard_map/ppermute | solution.py:31
  49.1 2.0 %fusion.1 = f32[128,4,256]{2,0,1:T(8,128)} fusion(f32[128,4,256]{2,0,1:T(8,128)} %collective-permute-done, f32[128,4,2,256]{3,0,2,1:T(8,128)S(1)} %fusion.2, pred[]{:T(512)S(6)} %eq.66), kind=kLoop, calls=%fused_computation.8 | loop fusion | flops 262144 | bytes 2097153 | tf_op jit(solution)/shard_map/add | solution.py:31
  51.1 4.0 %all-to-all-start.2 = ((f32[128,4,256]{2,0,1:T(8,128)}), f32[128,4,256]{2,0,1:T(8,128)S(1)}, u32[]{:S(2)}, u32[]{:S(2)}) async-start(f32[128,4,256]{2,0,1:T(8,128)} %fusion.1), calls=%async_computation.2 | async-start | bytes 1048576 | tf_op jit(solution)/shard_map/all_to_all | solution.py:32
  55.3 1.4 scatter_custom_fusion
  57.0 7.0 %all-to-all-done.2 = f32[128,4,256]{2,0,1:T(8,128)S(1)} async-done(((f32[128,4,256]{2,0,1:T(8,128)}), f32[128,4,256]{2,0,1:T(8,128)S(1)}, u32[]{:S(2)}, u32[]{:S(2)}) %all-to-all-start.2) | async-done | bytes 524320 | tf_op jit(solution)/shard_map/all_to_all | solution.py:32
  64.1 0.4 fusion.4
  64.6 20.3 %all_to_all.41 = f32[128,5,128]{2,1,0:T(8,128)S(1)} all-to-all(f32[128,5,128]{2,1,0:T(8,128)S(1)} %pad_maximum_fusion), channel_id=1, replica_groups=mesh['h'=2,'r8'=8,'x'=4,'k'=2] {'h','r8','x','k'}, dimensions={0} | all-to-all | bytes 655360 | tf_op jit(solution)/shard_map/all_to_all | solution.py:98
  84.9 0.2 fusion.12
  85.3 0.3 fusion.5
  85.7 9.8 %all_to_all.42 = f32[8,64,128]{2,1,0:T(8,128)S(1)} all-to-all(f32[8,64,128]{2,1,0:T(8,128)S(1)} %broadcast_in_dim.13), channel_id=1, replica_groups=mesh['h'=2,'r8'=8,'x'=4,'k'=2] {'x','k'}, dimensions={0} | all-to-all | bytes 524288 | tf_op jit(solution)/shard_map/all_to_all | solution.py:37
  95.5 0.7 convolution_bitcast_fusion
  96.5 13.3 %all_to_all.43 = f32[16,64,128]{2,1,0:T(8,128)S(1)} all-to-all(f32[16,64,128]{2,1,0:T(8,128)S(1)} %bitcast.73), channel_id=1, replica_groups=mesh['h'=2,'r8'=8,'x'=4,'k'=2] {'h','r8'}, dimensions={0} | all-to-all | bytes 1048576 | tf_op jit(solution)/shard_map/all_to_all | solution.py:14
  109.8 12.7 %all_to_all.44 = f32[16,64,128]{2,1,0:T(8,128)S(1)} all-to-all(f32[16,64,128]{2,1,0:T(8,128)S(1)} %broadcast_in_dim.14), channel_id=1, replica_groups=mesh['h'=2,'r8'=8,'x'=4,'k'=2] {'h','r8'}, dimensions={0} | all-to-all | bytes 1048576 | tf_op jit(solution)/shard_map/all_to_all | solution.py:37
  122.5 4.5 %convolution_bitcast_fusion.1 = f32[16,8,8,128]{3,2,1,0:T(8,128)S(1)} fusion(f32[1024,128]{1,0:T(8,128)S(1)} %bitcast.69, f32[1024,1024]{1,0:T(8,128)} %param.17), kind=kOutput, calls=%fused_computation.2 | convolution fusion | flops 805306368 | bytes 5242880 | tf_op jit(solution)/shard_map/dot_general | solution.py:116
  127.0 0.8 copy.53
  127.9 7.0 %all-to-all-start.7 = ((f32[8,128,128]{1,2,0:T(8,128)}), f32[8,128,128]{1,2,0:T(8,128)}, u32[]{:S(2)}, u32[]{:S(2)}) async-start(f32[8,128,128]{1,2,0:T(8,128)} %bitcast.72), calls=%async_computation.7 | async-start | bytes 1048576 | tf_op jit(solution)/shard_map/all_to_all | solution.py:14
  134.9 0.6 constant_dynamic-slice_fusion
  135.5 8.8 %all-to-all-done.7 = f32[8,128,128]{1,2,0:T(8,128)} async-done(((f32[8,128,128]{1,2,0:T(8,128)}), f32[8,128,128]{1,2,0:T(8,128)}, u32[]{:S(2)}, u32[]{:S(2)}) %all-to-all-start.7) | async-done | bytes 524320 | tf_op jit(solution)/shard_map/all_to_all | solution.py:14
  144.3 1.1 reduce_sum.49
  145.5 0.6 fusion.11
  146.1 0.8 copy.55
  (41 shorter events, 1.5 us)
Async XLA Ops:
  0.6 94.9 %copy-start = (f32[512,1024]{1,0:T(8,128)S(1)}, f32[512,1024]{1,0:T(8,128)}, u32[]{:S(2)}) copy-start(f32[512,1024]{1,0:T(8,128)} %param.16) | copy-start | bytes 6291460
  22.9 13.0 %all-to-all-start.1 = ((f32[8,128,128]{1,2,0:T(8,128)}), f32[8,128,128]{1,2,0:T(8,128)S(1)}, u32[]{:S(2)}, u32[]{:S(2)}) async-start(f32[8,128,128]{1,2,0:T(8,128)} %broadcast_in_dim.10), calls=%async_computation.1 | async-start | bytes 1048576 | tf_op jit(solution)/shard_map/all_to_all | solution.py:37
  35.9 1.2 copy-start.1
  37.1 10.2 %copy-start.6 = (s32[256]{0:T(256)S(1)}, s32[256]{0:T(256)}, u32[]{:S(2)}) copy-start(s32[256]{0:T(256)} %param.15) | copy-start | bytes 3076
  44.9 12.0 %copy-start.3 = (f32[256,128]{1,0:T(8,128)S(1)}, f32[256,128]{1,0:T(8,128)}, u32[]{:S(2)}) copy-start(f32[256,128]{1,0:T(8,128)} %param.14) | copy-start | bytes 393220
  45.8 3.3 %collective-permute-start = (f32[128,4,256]{2,0,1:T(8,128)}, f32[128,4,256]{2,0,1:T(8,128)}, u32[]{:S(2)}, u32[]{:S(2)}) collective-permute-start(f32[128,4,256]{2,0,1:T(8,128)} %select_bitcast_fusion), channel_id=1, source_target_pairs={{0,1},{1,0},{2,3},{3,2},{4,5},{5,4},{6,7},{7,6},{8,9},{9,8},{10,11... | collective-permute-start | bytes 1572872 | tf_op jit(solution)/shard_map/ppermute | solution.py:31
  47.7 38.0 %copy-start.5 = (f32[64,128]{1,0:T(8,128)S(1)}, f32[64,128]{1,0:T(8,128)}, u32[]{:S(2)}) copy-start(f32[64,128]{1,0:T(8,128)} %param.18) | copy-start | bytes 98308
  51.1 12.9 %all-to-all-start.2 = ((f32[128,4,256]{2,0,1:T(8,128)}), f32[128,4,256]{2,0,1:T(8,128)S(1)}, u32[]{:S(2)}, u32[]{:S(2)}) async-start(f32[128,4,256]{2,0,1:T(8,128)} %fusion.1), calls=%async_computation.2 | async-start | bytes 1048576 | tf_op jit(solution)/shard_map/all_to_all | solution.py:32
  109.8 25.0 %copy-start.2 = (f32[8,128,128]{1,2,0:T(8,128)S(1)}, f32[8,128,128]{1,2,0:T(8,128)}, u32[]{:S(2)}) copy-start(f32[8,128,128]{1,2,0:T(8,128)} %copy-done.1) | copy-start | bytes 1572868
  122.5 23.0 %copy-start.4 = (f32[128,128]{1,0:T(8,128)S(1)}, f32[128,128]{1,0:T(8,128)}, u32[]{:S(2)}) copy-start(f32[128,128]{1,0:T(8,128)} %param.19) | copy-start | bytes 196612
  127.9 16.5 %all-to-all-start.7 = ((f32[8,128,128]{1,2,0:T(8,128)}), f32[8,128,128]{1,2,0:T(8,128)}, u32[]{:S(2)}, u32[]{:S(2)}) async-start(f32[8,128,128]{1,2,0:T(8,128)} %bitcast.72), calls=%async_computation.7 | async-start | bytes 1048576 | tf_op jit(solution)/shard_map/all_to_all | solution.py:14

commit v10 on v9

--- a/solution.py
+++ b/solution.py
@@ -13,6 +13,19 @@
 def reduce_scatter(x, axis, n):
     got = lax.all_to_all(x.reshape(n, x.shape[0] // n, x.shape[1]), axis, 0, 0, tiled=False)
     return got.sum(axis=0)
+
+
+def reduce_scatter_cols(matrix, vector, n, precision):
+    product = lax.dot_general(
+        vector,
+        matrix,
+        (((0,), (1,)), ((), ())),
+        precision=precision,
+        preferred_element_type=jnp.float32,
+    )
+    blocks = product.reshape(product.shape[0], n, matrix.shape[0] // n)
+    got = lax.all_to_all(blocks, COL, 1, 1, tiled=False)
+    return got.sum(axis=1).T
 
 
 def reduce_scatter_chip(matrix, vector, chips, precision):
@@ -112,11 +125,7 @@
         preferred_element_type=jnp.float32,
     )
     parent_solution = gather(reduce_scatter(partial_sep, ROW, rows_axis), ROW, rows_axis)
-    carried_parent = reduce_scatter(
-        jnp.dot(parent_border, parent_solution, precision=highest, preferred_element_type=jnp.float32),
-        COL,
-        cols_axis,
-    )
+    carried_parent = reduce_scatter_cols(parent_border, parent_solution, cols_axis, highest)
     parent_contribution = border_rows - carried_parent
     return (child_part, parent_solution, parent_contribution)
 

time: 148 us -> 148 us (level)
  no operation moved by 1% of the time
where the time goes in v10:
time: 148 us; the launch traced here: 147 us
  blocking collectives  71.5 us (48%)
  waiting for transfers between devices  26.8 us (18%)
  matrix products  20.5 us (14%)
  starting transfers between devices  15.9 us (11%)
  local copies, waits for them, and re-layouts  5.85 us (4%)
  other arithmetic  5.46 us (4%)
    all_to_all x2, blocking collectives, reduce_scatter(): lax.all_to_all(x.reshape(n, x.shape[0] // n, x.shape[1]), axis, 0, 0, til...  28.6 us
    all_to_all x2, blocking collectives, gather(): lax.all_to_all(jnp.broadcast_to(x[None], (n,) + x.shape), axis, 0, 0, til...  22.5 us
    all_to_all x1, blocking collectives, local(): got = lax.all_to_all(packed, ALL, 0, 0, tiled=True)  20.3 us
    all_to_all x1, waiting for transfers between devices, gather(): lax.all_to_all(jnp.broadcast_to(x[None], (n,) + x.shape), axis, 0, 0, til...  9.5 us
    all_to_all x1, waiting for transfers between devices, reduce_scatter_cols(): got = lax.all_to_all(blocks, COL, 1, 1, tiled=False)  8.79 us
    dot_general x1, matrix products, reduce_scatter_chip(): lax.dot_general(vector, matrix, (((0,), (1,)), ((), ())), precision=preci...  7.82 us
    all_to_all x1, waiting for transfers between devices, reduce_scatter_chip(): got = lax.all_to_all(summed, 'x', 1, 1, tiled=False)  7.03 us
    all_to_all x1, starting transfers between devices, reduce_scatter_cols(): got = lax.all_to_all(blocks, COL, 1, 1, tiled=False)  6.98 us
  transfers between devices with their start and end apart: 4, of which 4 were waited for; matrix products, arithmetic and copies ran while one was open for 2% of the time, Pallas kernels for 0%

profile of v10, /device:TPU:1, one launch (start us, length us, event | category | flops | bytes accessed | tf_op | source)
XLA Modules:
  0.0 146.9 jit_solution(8199510547544445710)
XLA Ops:
  0.6 5.9 %fusion.19 = f32[1024,128]{1,0:T(8,128)S(1)} fusion(f32[1024,1024]{1,0:T(8,128)} %param.11, f32[1024,128]{1,0:T(8,128)} %param.13), kind=kOutput, calls=%fused_computation.55 | convolution fusion | flops 805306368 | bytes 5242880 | tf_op jit(solution)/shard_map/dot_general | solution.py:73
  6.5 15.4 %all_to_all.40 = f32[8,128,128]{2,1,0:T(8,128)S(1)} all-to-all(f32[8,128,128]{2,1,0:T(8,128)S(1)} %bitcast.71), channel_id=1, replica_groups=mesh['h'=2,'r8'=8,'x'=4,'k'=2] {'r8'}, dimensions={0} | all-to-all | bytes 1048576 | tf_op jit(solution)/shard_map/all_to_all | solution.py:14
  22.0 0.8 broadcast_in_dim.10
  22.9 3.5 %all-to-all-start.1 = ((f32[8,128,128]{1,2,0:T(8,128)}), f32[8,128,128]{1,2,0:T(8,128)S(1)}, u32[]{:S(2)}, u32[]{:S(2)}) async-start(f32[8,128,128]{1,2,0:T(8,128)} %broadcast_in_dim.10), calls=%async_computation.1 | async-start | bytes 1048576 | tf_op jit(solution)/shard_map/all_to_all | solution.py:50
  26.4 9.5 %all-to-all-done.1 = f32[8,128,128]{1,2,0:T(8,128)S(1)} async-done(((f32[8,128,128]{1,2,0:T(8,128)}), f32[8,128,128]{1,2,0:T(8,128)S(1)}, u32[]{:S(2)}, u32[]{:S(2)}) %all-to-all-start.1) | async-done | bytes 524320 | tf_op jit(solution)/shard_map/all_to_all | solution.py:50
  35.9 0.3 copy.36
  36.2 0.9 reshape.123
  37.1 7.8 %fusion.2 = f32[128,4,2,256]{3,0,2,1:T(8,128)S(1)} fusion(f32[4,2,256,1024]{3,2,1,0:T(8,128)} %bitcast.67, f32[1024,128,1,1]{0,1,2,3:T(8,128)} %reshape.123), kind=kOutput, calls=%fused_computation.7 | convolution fusion | flops 1610612736 | bytes 9961472 | tf_op jit(solution)/shard_map/dot_general | solution.py:33
  44.9 0.9 select_bitcast_fusion
  45.8 1.5 collective-permute-start
  47.4 0.2 fusion.8
  47.7 1.5 %collective-permute-done = f32[128,4,256]{2,0,1:T(8,128)} collective-permute-done((f32[128,4,256]{2,0,1:T(8,128)}, f32[128,4,256]{2,0,1:T(8,128)}, u32[]{:S(2)}, u32[]{:S(2)}) %collective-permute-start) | collective-permute-done | bytes 524320 | tf_op jit(solution)/shard_map/ppermute | solution.py:44
  49.1 2.0 %fusion.1 = f32[128,4,256]{2,0,1:T(8,128)} fusion(f32[128,4,256]{2,0,1:T(8,128)} %collective-permute-done, f32[128,4,2,256]{3,0,2,1:T(8,128)S(1)} %fusion.2, pred[]{:T(512)S(6)} %eq.66), kind=kLoop, calls=%fused_computation.6 | loop fusion | flops 262144 | bytes 2097153 | tf_op jit(solution)/shard_map/add | solution.py:44
  51.1 4.0 %all-to-all-start.2 = ((f32[128,4,256]{2,0,1:T(8,128)}), f32[128,4,256]{2,0,1:T(8,128)S(1)}, u32[]{:S(2)}, u32[]{:S(2)}) async-start(f32[128,4,256]{2,0,1:T(8,128)} %fusion.1), calls=%async_computation.2 | async-start | bytes 1048576 | tf_op jit(solution)/shard_map/all_to_all | solution.py:45
  55.3 1.4 scatter_custom_fusion
  57.0 7.0 %all-to-all-done.2 = f32[128,4,256]{2,0,1:T(8,128)S(1)} async-done(((f32[128,4,256]{2,0,1:T(8,128)}), f32[128,4,256]{2,0,1:T(8,128)S(1)}, u32[]{:S(2)}, u32[]{:S(2)}) %all-to-all-start.2) | async-done | bytes 524320 | tf_op jit(solution)/shard_map/all_to_all | solution.py:45
  64.1 0.4 fusion.4
  64.6 20.3 %all_to_all.41 = f32[128,5,128]{2,1,0:T(8,128)S(1)} all-to-all(f32[128,5,128]{2,1,0:T(8,128)S(1)} %pad_maximum_fusion), channel_id=1, replica_groups=mesh['h'=2,'r8'=8,'x'=4,'k'=2] {'h','r8','x','k'}, dimensions={0} | all-to-all | bytes 655360 | tf_op jit(solution)/shard_map/all_to_all | solution.py:111
  84.9 0.2 fusion.12
  85.3 0.3 fusion.5
  85.7 9.8 %all_to_all.42 = f32[8,64,128]{2,1,0:T(8,128)S(1)} all-to-all(f32[8,64,128]{2,1,0:T(8,128)S(1)} %broadcast_in_dim.13), channel_id=1, replica_groups=mesh['h'=2,'r8'=8,'x'=4,'k'=2] {'x','k'}, dimensions={0} | all-to-all | bytes 524288 | tf_op jit(solution)/shard_map/all_to_all | solution.py:50
  95.5 0.7 convolution_bitcast_fusion
  96.3 0.2 copy.45
  96.5 13.3 %all_to_all.43 = f32[16,64,128]{2,1,0:T(8,128)S(1)} all-to-all(f32[16,64,128]{2,1,0:T(8,128)S(1)} %bitcast.72), channel_id=1, replica_groups=mesh['h'=2,'r8'=8,'x'=4,'k'=2] {'h','r8'}, dimensions={0} | all-to-all | bytes 1048576 | tf_op jit(solution)/shard_map/all_to_all | solution.py:14
  109.8 12.7 %all_to_all.44 = f32[16,64,128]{2,1,0:T(8,128)S(1)} all-to-all(f32[16,64,128]{2,1,0:T(8,128)S(1)} %broadcast_in_dim.14), channel_id=1, replica_groups=mesh['h'=2,'r8'=8,'x'=4,'k'=2] {'h','r8'}, dimensions={0} | all-to-all | bytes 1048576 | tf_op jit(solution)/shard_map/all_to_all | solution.py:50
  122.5 5.3 %fusion.20 = f32[128,8,128]{2,0,1:T(8,128)} fusion(f32[1024,128,1]{1,0,2:T(8,128)S(1)} %bitcast.68, f32[8,128,1024]{2,1,0:T(8,128)} %bitcast.70), kind=kOutput, calls=%fused_computation.56 | convolution fusion | flops 805306368 | bytes 5242880 | tf_op jit(solution)/shard_map/dot_general | solution.py:19
  127.8 7.0 %all-to-all-start.7 = ((f32[128,8,128]{2,0,1:T(8,128)}), f32[128,8,128]{2,0,1:T(8,128)}, u32[]{:S(2)}, u32[]{:S(2)}) async-start(f32[128,8,128]{2,0,1:T(8,128)} %fusion.20), calls=%async_computation.7 | async-start | bytes 1048576 | tf_op jit(solution)/shard_map/all_to_all | solution.py:27
  134.8 0.6 constant_dynamic-slice_fusion
  135.5 8.8 %all-to-all-done.7 = f32[128,8,128]{2,0,1:T(8,128)} async-done(((f32[128,8,128]{2,0,1:T(8,128)}), f32[128,8,128]{2,0,1:T(8,128)}, u32[]{:S(2)}, u32[]{:S(2)}) %all-to-all-start.7) | async-done | bytes 524320 | tf_op jit(solution)/shard_map/all_to_all | solution.py:27
  144.3 1.1 reduce_sum.49
  145.5 0.6 fusion.11
  146.1 0.8 copy.55
  (40 shorter events, 1.3 us)
Async XLA Ops:
  0.6 94.9 %copy-start = (f32[512,1024]{1,0:T(8,128)S(1)}, f32[512,1024]{1,0:T(8,128)}, u32[]{:S(2)}) copy-start(f32[512,1024]{1,0:T(8,128)} %param.16) | copy-start | bytes 6291460
  22.9 13.0 %all-to-all-start.1 = ((f32[8,128,128]{1,2,0:T(8,128)}), f32[8,128,128]{1,2,0:T(8,128)S(1)}, u32[]{:S(2)}, u32[]{:S(2)}) async-start(f32[8,128,128]{1,2,0:T(8,128)} %broadcast_in_dim.10), calls=%async_computation.1 | async-start | bytes 1048576 | tf_op jit(solution)/shard_map/all_to_all | solution.py:50
  35.9 1.2 copy-start.1
  37.1 10.2 %copy-start.6 = (s32[256]{0:T(256)S(1)}, s32[256]{0:T(256)}, u32[]{:S(2)}) copy-start(s32[256]{0:T(256)} %param.15) | copy-start | bytes 3076
  44.9 12.0 %copy-start.3 = (f32[256,128]{1,0:T(8,128)S(1)}, f32[256,128]{1,0:T(8,128)}, u32[]{:S(2)}) copy-start(f32[256,128]{1,0:T(8,128)} %param.14) | copy-start | bytes 393220
  45.8 3.3 %collective-permute-start = (f32[128,4,256]{2,0,1:T(8,128)}, f32[128,4,256]{2,0,1:T(8,128)}, u32[]{:S(2)}, u32[]{:S(2)}) collective-permute-start(f32[128,4,256]{2,0,1:T(8,128)} %select_bitcast_fusion), channel_id=1, source_target_pairs={{0,1},{1,0},{2,3},{3,2},{4,5},{5,4},{6,7},{7,6},{8,9},{9,8},{10,11... | collective-permute-start | bytes 1572872 | tf_op jit(solution)/shard_map/ppermute | solution.py:44
  47.7 38.0 %copy-start.5 = (f32[64,128]{1,0:T(8,128)S(1)}, f32[64,128]{1,0:T(8,128)}, u32[]{:S(2)}) copy-start(f32[64,128]{1,0:T(8,128)} %param.18) | copy-start | bytes 98308
  51.1 12.9 %all-to-all-start.2 = ((f32[128,4,256]{2,0,1:T(8,128)}), f32[128,4,256]{2,0,1:T(8,128)S(1)}, u32[]{:S(2)}, u32[]{:S(2)}) async-start(f32[128,4,256]{2,0,1:T(8,128)} %fusion.1), calls=%async_computation.2 | async-start | bytes 1048576 | tf_op jit(solution)/shard_map/all_to_all | solution.py:45
  109.7 25.1 %copy-start.2 = (f32[8,128,128]{1,2,0:T(8,128)S(1)}, f32[8,128,128]{1,2,0:T(8,128)}, u32[]{:S(2)}) copy-start(f32[8,128,128]{1,2,0:T(8,128)} %copy-done.1) | copy-start | bytes 1572868
  122.5 22.9 %copy-start.4 = (f32[128,128]{1,0:T(8,128)S(1)}, f32[128,128]{1,0:T(8,128)}, u32[]{:S(2)}) copy-start(f32[128,128]{1,0:T(8,128)} %param.19) | copy-start | bytes 196612
  127.8 16.5 %all-to-all-start.7 = ((f32[128,8,128]{2,0,1:T(8,128)}), f32[128,8,128]{2,0,1:T(8,128)}, u32[]{:S(2)}, u32[]{:S(2)}) async-start(f32[128,8,128]{2,0,1:T(8,128)} %fusion.20), calls=%async_computation.7 | async-start | bytes 1048576 | tf_op jit(solution)/shard_map/all_to_all | solution.py:27

commit v11 on v10

--- a/solution.py
+++ b/solution.py
@@ -125,7 +125,7 @@
         preferred_element_type=jnp.float32,
     )
     parent_solution = gather(reduce_scatter(partial_sep, ROW, rows_axis), ROW, rows_axis)
-    carried_parent = reduce_scatter_cols(parent_border, parent_solution, cols_axis, highest)
+    carried_parent = reduce_scatter_chip(parent_border, parent_solution, chips, highest)
     parent_contribution = border_rows - carried_parent
     return (child_part, parent_solution, parent_contribution)
 

time: 148 us -> 145 us (0.980)
  waiting for transfers between devices: 26.8 us -> 23.7 us
    all_to_all x1 -> x0, waiting for transfers between devices: 8.79 us -> none  [reduce_scatter_cols(): got = lax.all_to_all(blocks, COL, 1, 1, tiled=False)]
    all_to_all x1 -> x0, starting transfers between devices: 6.98 us -> none  [reduce_scatter_cols(): got = lax.all_to_all(blocks, COL, 1, 1, tiled=False)]
    dot_general x1 -> x0, matrix products: 5.3 us -> none  [reduce_scatter_cols(): lax.dot_general(vector, matrix, (((0,), (1,)), ((), ())), precision=preci...]
    dot_general x1 -> x2, matrix products: 7.82 us -> 12.3 us  [reduce_scatter_chip(): lax.dot_general(vector, matrix, (((0,), (1,)), ((), ())), precision=preci...]
    all_to_all x1 -> x2, waiting for transfers between devices: 7.03 us -> 11.4 us  [reduce_scatter_chip(): got = lax.all_to_all(summed, 'x', 1, 1, tiled=False)]
    all_to_all x1 -> x2, starting transfers between devices: 4.01 us -> 7.41 us  [reduce_scatter_chip(): got = lax.all_to_all(summed, 'x', 1, 1, tiled=False)]
    ppermute x1 -> x2, starting transfers between devices: 1.47 us -> 4.42 us  [reduce_scatter_chip(): summed = mine + lax.ppermute(other, 'k', [(0, 1), (1, 0)])]
  transfers between devices with their start and end apart: 4 -> 5, of which waited for: 4 -> 5; matrix products, arithmetic and copies ran while one was open for 2% -> 3% of each run, Pallas kernels for 0% -> 0%
where the time goes in v11:
time: 145 us; the launch traced here: 144 us
  blocking collectives  71.4 us (49%)
  waiting for transfers between devices  23.7 us (16%)
  matrix products  19.6 us (14%)
  starting transfers between devices  15.3 us (11%)
  local copies, waits for them, and re-layouts  6.89 us (5%)
  other arithmetic  6.69 us (5%)
    all_to_all x2, blocking collectives, reduce_scatter(): lax.all_to_all(x.reshape(n, x.shape[0] // n, x.shape[1]), axis, 0, 0, til...  28.6 us
    all_to_all x2, blocking collectives, gather(): lax.all_to_all(jnp.broadcast_to(x[None], (n,) + x.shape), axis, 0, 0, til...  22.4 us
    all_to_all x1, blocking collectives, local(): got = lax.all_to_all(packed, ALL, 0, 0, tiled=True)  20.3 us
    dot_general x2, matrix products, reduce_scatter_chip(): lax.dot_general(vector, matrix, (((0,), (1,)), ((), ())), precision=preci...  12.3 us
    all_to_all x2, waiting for transfers between devices, reduce_scatter_chip(): got = lax.all_to_all(summed, 'x', 1, 1, tiled=False)  11.4 us
    all_to_all x1, waiting for transfers between devices, gather(): lax.all_to_all(jnp.broadcast_to(x[None], (n,) + x.shape), axis, 0, 0, til...  9.5 us
    all_to_all x2, starting transfers between devices, reduce_scatter_chip(): got = lax.all_to_all(summed, 'x', 1, 1, tiled=False)  7.41 us
    dot_general x1, matrix products, local(): lax.dot_general(child_inverse, child_sep_rhs, contract_rows, precision=hi...  5.88 us
  transfers between devices with their start and end apart: 5, of which 5 were waited for; matrix products, arithmetic and copies ran while one was open for 3% of the time, Pallas kernels for 0%

profile of v11, /device:TPU:1, one launch (start us, length us, event | category | flops | bytes accessed | tf_op | source)
XLA Modules:
  0.0 144.5 jit_solution(9376219739422821920)
XLA Ops:
  0.6 5.9 %fusion.21 = f32[1024,128]{1,0:T(8,128)S(1)} fusion(f32[1024,1024]{1,0:T(8,128)} %param.11, f32[1024,128]{1,0:T(8,128)} %param.13), kind=kOutput, calls=%fused_computation.59 | convolution fusion | flops 805306368 | bytes 5242880 | tf_op jit(solution)/shard_map/dot_general | solution.py:73
  6.5 15.4 %all_to_all.40 = f32[8,128,128]{2,1,0:T(8,128)S(1)} all-to-all(f32[8,128,128]{2,1,0:T(8,128)S(1)} %bitcast.89), channel_id=1, replica_groups=mesh['h'=2,'r8'=8,'x'=4,'k'=2] {'r8'}, dimensions={0} | all-to-all | bytes 1048576 | tf_op jit(solution)/shard_map/all_to_all | solution.py:14
  22.0 0.8 broadcast_in_dim.10
  22.9 3.5 %all-to-all-start.1 = ((f32[8,128,128]{1,2,0:T(8,128)}), f32[8,128,128]{1,2,0:T(8,128)S(1)}, u32[]{:S(2)}, u32[]{:S(2)}) async-start(f32[8,128,128]{1,2,0:T(8,128)} %broadcast_in_dim.10), calls=%async_computation.1 | async-start | bytes 1048576 | tf_op jit(solution)/shard_map/all_to_all | solution.py:50
  26.4 9.5 %all-to-all-done.1 = f32[8,128,128]{1,2,0:T(8,128)S(1)} async-done(((f32[8,128,128]{1,2,0:T(8,128)}), f32[8,128,128]{1,2,0:T(8,128)S(1)}, u32[]{:S(2)}, u32[]{:S(2)}) %all-to-all-start.1) | async-done | bytes 524320 | tf_op jit(solution)/shard_map/all_to_all | solution.py:50
  36.2 0.9 reshape.127
  37.1 7.8 %fusion.2 = f32[128,4,2,256]{3,0,2,1:T(8,128)S(1)} fusion(f32[4,2,256,1024]{3,2,1,0:T(8,128)} %bitcast.85, f32[1024,128,1,1]{0,1,2,3:T(8,128)} %reshape.127), kind=kOutput, calls=%fused_computation.7 | convolution fusion | flops 1610612736 | bytes 9961472 | tf_op jit(solution)/shard_map/dot_general | solution.py:33
  44.9 0.9 select_bitcast_fusion
  45.8 1.5 %collective-permute-start = (f32[128,4,256]{2,0,1:T(8,128)}, f32[128,4,256]{2,0,1:T(8,128)}, u32[]{:S(2)}, u32[]{:S(2)}) collective-permute-start(f32[128,4,256]{2,0,1:T(8,128)} %select_bitcast_fusion), channel_id=1, source_target_pairs={{0,1},{1,0},{2,3},{3,2},{4,5},{5,4},{6,7},{7,6},{8,9},{9,8},{10,11... | collective-permute-start | bytes 1572872 | tf_op jit(solution)/shard_map/ppermute | solution.py:44
  47.7 1.5 %collective-permute-done = f32[128,4,256]{2,0,1:T(8,128)} collective-permute-done((f32[128,4,256]{2,0,1:T(8,128)}, f32[128,4,256]{2,0,1:T(8,128)}, u32[]{:S(2)}, u32[]{:S(2)}) %collective-permute-start) | collective-permute-done | bytes 524320 | tf_op jit(solution)/shard_map/ppermute | solution.py:44
  49.1 2.0 %fusion.1 = f32[128,4,256]{2,0,1:T(8,128)} fusion(f32[128,4,256]{2,0,1:T(8,128)} %collective-permute-done, f32[128,4,2,256]{3,0,2,1:T(8,128)S(1)} %fusion.2, pred[]{:T(512)S(6)} %eq.67), kind=kLoop, calls=%fused_computation.6 | loop fusion | flops 262144 | bytes 2097153 | tf_op jit(solution)/shard_map/add | solution.py:44
  51.1 4.0 %all-to-all-start.2 = ((f32[128,4,256]{2,0,1:T(8,128)}), f32[128,4,256]{2,0,1:T(8,128)S(1)}, u32[]{:S(2)}, u32[]{:S(2)}) async-start(f32[128,4,256]{2,0,1:T(8,128)} %fusion.1), calls=%async_computation.2 | async-start | bytes 1048576 | tf_op jit(solution)/shard_map/all_to_all | solution.py:45
  55.3 1.4 scatter_custom_fusion
  57.0 7.0 %all-to-all-done.2 = f32[128,4,256]{2,0,1:T(8,128)S(1)} async-done(((f32[128,4,256]{2,0,1:T(8,128)}), f32[128,4,256]{2,0,1:T(8,128)S(1)}, u32[]{:S(2)}, u32[]{:S(2)}) %all-to-all-start.2) | async-done | bytes 524320 | tf_op jit(solution)/shard_map/all_to_all | solution.py:45
  64.1 0.4 fusion.4
  64.6 20.3 %all_to_all.41 = f32[128,5,128]{2,1,0:T(8,128)S(1)} all-to-all(f32[128,5,128]{2,1,0:T(8,128)S(1)} %pad_maximum_fusion), channel_id=1, replica_groups=mesh['h'=2,'r8'=8,'x'=4,'k'=2] {'h','r8','x','k'}, dimensions={0} | all-to-all | bytes 655360 | tf_op jit(solution)/shard_map/all_to_all | solution.py:111
  85.3 0.3 fusion.5
  85.7 9.8 %all_to_all.42 = f32[8,64,128]{2,1,0:T(8,128)S(1)} all-to-all(f32[8,64,128]{2,1,0:T(8,128)S(1)} %broadcast_in_dim.13), channel_id=1, replica_groups=mesh['h'=2,'r8'=8,'x'=4,'k'=2] {'x','k'}, dimensions={0} | all-to-all | bytes 524288 | tf_op jit(solution)/shard_map/all_to_all | solution.py:50
  95.5 0.7 convolution_bitcast_fusion
  96.5 13.3 %all_to_all.43 = f32[16,64,128]{2,1,0:T(8,128)S(1)} all-to-all(f32[16,64,128]{2,1,0:T(8,128)S(1)} %bitcast.90), channel_id=1, replica_groups=mesh['h'=2,'r8'=8,'x'=4,'k'=2] {'h','r8'}, dimensions={0} | all-to-all | bytes 1048576 | tf_op jit(solution)/shard_map/all_to_all | solution.py:14
  109.8 12.6 %all_to_all.44 = f32[16,64,128]{2,1,0:T(8,128)S(1)} all-to-all(f32[16,64,128]{2,1,0:T(8,128)S(1)} %broadcast_in_dim.14), channel_id=1, replica_groups=mesh['h'=2,'r8'=8,'x'=4,'k'=2] {'h','r8'}, dimensions={0} | all-to-all | bytes 1048576 | tf_op jit(solution)/shard_map/all_to_all | solution.py:50
  122.4 4.4 %fusion.22 = f32[128,4,2,128]{3,0,2,1:T(8,128)S(1)} fusion(f32[1024,128,1,1]{1,0,3,2:T(8,128)S(1)} %bitcast.86, f32[4,2,128,1024]{3,2,1,0:T(8,128)} %bitcast.88), kind=kOutput, calls=%fused_computation.60 | convolution fusion | flops 805306368 | bytes 5242880 | tf_op jit(solution)/shard_map/dot_general | solution.py:33
  126.8 0.7 select_bitcast_fusion.1
  127.6 3.0 %collective-permute-start.1 = (f32[128,4,128]{2,0,1:T(8,128)}, f32[128,4,128]{2,0,1:T(8,128)S(1)}, u32[]{:S(2)}, u32[]{:S(2)}) collective-permute-start(f32[128,4,128]{2,0,1:T(8,128)} %select_bitcast_fusion.1), channel_id=1, source_target_pairs={{0,1},{1,0},{2,3},{3,2},{4,5},{5,4},{6,7},{7,6},{8,9},{9,8},{10,11... | collective-permute-start | bytes 786440 | tf_op jit(solution)/shard_map/ppermute | solution.py:44
  130.5 1.4 collective-permute-done.1
  131.9 0.7 fusion.7
  132.6 3.4 %all-to-all-start.7 = ((f32[128,4,128]{2,0,1:T(8,128)}), f32[128,4,128]{2,0,1:T(8,128)S(1)}, u32[]{:S(2)}, u32[]{:S(2)}) async-start(f32[128,4,128]{2,0,1:T(8,128)} %fusion.7), calls=%async_computation.7 | async-start | bytes 524288 | tf_op jit(solution)/shard_map/all_to_all | solution.py:45
  136.0 1.1 copy_bitcast_fusion
  137.1 0.6 constant_dynamic-slice_fusion
  137.8 4.3 %all-to-all-done.7 = f32[128,4,128]{2,0,1:T(8,128)S(1)} async-done(((f32[128,4,128]{2,0,1:T(8,128)}), f32[128,4,128]{2,0,1:T(8,128)S(1)}, u32[]{:S(2)}, u32[]{:S(2)}) %all-to-all-start.7) | async-done | bytes 262176 | tf_op jit(solution)/shard_map/all_to_all | solution.py:45
  142.2 1.5 %fusion.13 = f32[128,128]{1,0:T(8,128)} fusion(f32[128,128]{1,0:T(8,128)} %param.19, f32[192,128]{1,0:T(8,128)S(1)} %fusion.5, f32[128,128]{0,1:T(8,128)S(1)} %copy.63), kind=kLoop, calls=%fused_computation.28 | loop fusion | flops 32768 | bytes 262144 | tf_op jit(solution)/shard_map/sub | solution.py:129
  143.7 0.8 copy.72
  (40 shorter events, 2.2 us)
Async XLA Ops:
  0.6 94.9 %copy-start = (f32[512,1024]{1,0:T(8,128)S(1)}, f32[512,1024]{1,0:T(8,128)}, u32[]{:S(2)}) copy-start(f32[512,1024]{1,0:T(8,128)} %param.16) | copy-start | bytes 6291460
  22.9 13.0 %all-to-all-start.1 = ((f32[8,128,128]{1,2,0:T(8,128)}), f32[8,128,128]{1,2,0:T(8,128)S(1)}, u32[]{:S(2)}, u32[]{:S(2)}) async-start(f32[8,128,128]{1,2,0:T(8,128)} %broadcast_in_dim.10), calls=%async_computation.1 | async-start | bytes 1048576 | tf_op jit(solution)/shard_map/all_to_all | solution.py:50
  35.9 1.2 copy-start.1
  37.1 10.2 %copy-start.4 = (s32[256]{0:T(256)S(1)}, s32[256]{0:T(256)}, u32[]{:S(2)}) copy-start(s32[256]{0:T(256)} %param.15) | copy-start | bytes 3076
  44.9 12.0 %copy-start.2 = (f32[256,128]{1,0:T(8,128)S(1)}, f32[256,128]{1,0:T(8,128)}, u32[]{:S(2)}) copy-start(f32[256,128]{1,0:T(8,128)} %param.14) | copy-start | bytes 393220
  45.8 3.3 %collective-permute-start = (f32[128,4,256]{2,0,1:T(8,128)}, f32[128,4,256]{2,0,1:T(8,128)}, u32[]{:S(2)}, u32[]{:S(2)}) collective-permute-start(f32[128,4,256]{2,0,1:T(8,128)} %select_bitcast_fusion), channel_id=1, source_target_pairs={{0,1},{1,0},{2,3},{3,2},{4,5},{5,4},{6,7},{7,6},{8,9},{9,8},{10,11... | collective-permute-start | bytes 1572872 | tf_op jit(solution)/shard_map/ppermute | solution.py:44
  47.7 38.0 %copy-start.3 = (f32[64,128]{1,0:T(8,128)S(1)}, f32[64,128]{1,0:T(8,128)}, u32[]{:S(2)}) copy-start(f32[64,128]{1,0:T(8,128)} %param.18) | copy-start | bytes 98308
  51.1 12.9 %all-to-all-start.2 = ((f32[128,4,256]{2,0,1:T(8,128)}), f32[128,4,256]{2,0,1:T(8,128)S(1)}, u32[]{:S(2)}, u32[]{:S(2)}) async-start(f32[128,4,256]{2,0,1:T(8,128)} %fusion.1), calls=%async_computation.2 | async-start | bytes 1048576 | tf_op jit(solution)/shard_map/all_to_all | solution.py:45
  127.6 4.3 %collective-permute-start.1 = (f32[128,4,128]{2,0,1:T(8,128)}, f32[128,4,128]{2,0,1:T(8,128)S(1)}, u32[]{:S(2)}, u32[]{:S(2)}) collective-permute-start(f32[128,4,128]{2,0,1:T(8,128)} %select_bitcast_fusion.1), channel_id=1, source_target_pairs={{0,1},{1,0},{2,3},{3,2},{4,5},{5,4},{6,7},{7,6},{8,9},{9,8},{10,11... | collective-permute-start | bytes 786440 | tf_op jit(solution)/shard_map/ppermute | solution.py:44
  132.6 9.5 %all-to-all-start.7 = ((f32[128,4,128]{2,0,1:T(8,128)}), f32[128,4,128]{2,0,1:T(8,128)S(1)}, u32[]{:S(2)}, u32[]{:S(2)}) async-start(f32[128,4,128]{2,0,1:T(8,128)} %fusion.7), calls=%async_computation.7 | async-start | bytes 524288 | tf_op jit(solution)/shard_map/all_to_all | solution.py:45

commit v12 on v11

--- a/solution.py
+++ b/solution.py
@@ -25,6 +25,24 @@
     )
     blocks = product.reshape(product.shape[0], n, matrix.shape[0] // n)
     got = lax.all_to_all(blocks, COL, 1, 1, tiled=False)
+    return got.sum(axis=1).T
+
+
+def reduce_scatter_blocks(matrix, pieces, chips, precision):
+    first = lax.axis_index("k") == 0
+    product = lax.dot_general(
+        pieces,
+        matrix.reshape(matrix.shape[0], pieces.shape[0], pieces.shape[1]),
+        (((0, 1), (1, 2)), ((), ())),
+        precision=precision,
+        preferred_element_type=jnp.float32,
+    )
+    blocks = product.reshape(product.shape[0], chips, 2, matrix.shape[0] // (2 * chips))
+    even, odd = blocks[:, :, 0], blocks[:, :, 1]
+    mine = jnp.where(first, even, odd)
+    other = jnp.where(first, odd, even)
+    summed = mine + lax.ppermute(other, "k", [(0, 1), (1, 0)])
+    got = lax.all_to_all(summed, "x", 1, 1, tiled=False)
     return got.sum(axis=1).T
 
 
@@ -78,10 +96,20 @@
         preferred_element_type=jnp.float32,
     )
     width_rhs = partial_term.shape[1]
-    solved = gather(reduce_scatter(partial_term, "r8", half_rows), "r8", half_rows)
+    pieces = lax.all_to_all(
+        jnp.broadcast_to(
+            reduce_scatter(partial_term, "r8", half_rows)[None],
+            (half_rows, partial_term.shape[0] // half_rows, width_rhs),
+        ),
+        "r8",
+        0,
+        0,
+        tiled=False,
+    )
+    solved = pieces.reshape(partial_term.shape)
     share = width_rhs // half_rows
     child_part = lax.dynamic_slice_in_dim(solved, within * share, share, axis=1)
-    carried = reduce_scatter_chip(child_border, solved, chips, highest)
+    carried = reduce_scatter_blocks(child_border, pieces, chips, highest)
     outgoing = child_border_rhs - carried
     devices_all = rows_axis * cols_axis
     sep_dev = parent_sep_rhs.shape[0]

time: 145 us -> 147 us (1.014)
  waiting for transfers between devices: 23.7 us -> 13.3 us
  local copies, waits for them, and re-layouts: 6.89 us -> 16.7 us
  blocking collectives: 71.4 us -> 73.6 us
    unnamed x13 -> x17, local copies, waits for them, and re-layouts: 0.92 us -> 11.2 us
    dot_general x0 -> x1, matrix products: none -> 8.49 us  [reduce_scatter_blocks(): lax.dot_general(pieces, matrix.reshape(matrix.shape[0], pieces.shape[0],...]
    all_to_all x2 -> x1, waiting for transfers between devices: 11.4 us -> 3.01 us  [reduce_scatter_chip(): got = lax.all_to_all(summed, 'x', 1, 1, tiled=False)]
    dot_general x2 -> x1, matrix products: 12.3 us -> 4.45 us  [reduce_scatter_chip(): lax.dot_general(vector, matrix, (((0,), (1,)), ((), ())), precision=preci...]
    all_to_all x1 -> x2, starting transfers between devices: 3.49 us -> 7.5 us  [the longest x1 4.01 us: reduce_scatter_blocks(): got = lax.all_to_all(summed, 'x', 1, 1, tiled=False)]
    all_to_all x2 -> x1, starting transfers between devices: 7.41 us -> 3.4 us  [reduce_scatter_chip(): got = lax.all_to_all(summed, 'x', 1, 1, tiled=False)]
    all_to_all x1, blocking collectives: 20.3 us -> 22.4 us  [local(): got = lax.all_to_all(packed, ALL, 0, 0, tiled=True)]
    reshape x2 -> x0, local copies, waits for them, and re-layouts: 1.96 us -> none  [gather(): return got.reshape(n * x.shape[0], x.shape[1])]
  transfers between devices with their start and end apart: 5 -> 5, of which waited for: 5 -> 5; matrix products, arithmetic and copies ran while one was open for 3% -> 10% of each run, Pallas kernels for 0% -> 0%
where the time goes in v12:
time: 147 us; the launch traced here: 146 us
  blocking collectives  73.6 us (50%)
  matrix products  20.3 us (14%)
  local copies, waits for them, and re-layouts  16.7 us (11%)
  starting transfers between devices  15.4 us (10%)
  waiting for transfers between devices  13.3 us (9%)
  other arithmetic  6.02 us (4%)
    all_to_all x2, blocking collectives, reduce_scatter(): lax.all_to_all(x.reshape(n, x.shape[0] // n, x.shape[1]), axis, 0, 0, til...  28.6 us
    all_to_all x2, blocking collectives, gather(): lax.all_to_all(jnp.broadcast_to(x[None], (n,) + x.shape), axis, 0, 0, til...  22.5 us
    all_to_all x1, blocking collectives, local(): got = lax.all_to_all(packed, ALL, 0, 0, tiled=True)  22.4 us
    unnamed x17, local copies, waits for them, and re-layouts  11.2 us
    dot_general x1, matrix products, reduce_scatter_blocks(): lax.dot_general(pieces, matrix.reshape(matrix.shape[0], pieces.shape[0],...  8.49 us
    all_to_all x1, waiting for transfers between devices, reduce_scatter_blocks(): got = lax.all_to_all(summed, 'x', 1, 1, tiled=False)  6.85 us
    dot_general x1, matrix products, local(): lax.dot_general(child_inverse, child_sep_rhs, contract_rows, precision=hi...  5.88 us
    dot_general x1, matrix products, reduce_scatter_chip(): lax.dot_general(vector, matrix, (((0,), (1,)), ((), ())), precision=preci...  4.45 us
  transfers between devices with their start and end apart: 5, of which 5 were waited for; matrix products, arithmetic and copies ran while one was open for 10% of the time, Pallas kernels for 0%

profile of v12, /device:TPU:1, one launch (start us, length us, event | category | flops | bytes accessed | tf_op | source)
XLA Modules:
  0.0 146.2 jit_solution(1856968719307135079)
XLA Ops:
  0.6 5.9 %fusion.25 = f32[1024,128]{1,0:T(8,128)S(1)} fusion(f32[1024,1024]{1,0:T(8,128)} %param.11, f32[1024,128]{1,0:T(8,128)} %param.13), kind=kOutput, calls=%fused_computation.60 | convolution fusion | flops 805306368 | bytes 5242880 | tf_op jit(solution)/shard_map/dot_general | solution.py:91
  6.5 15.4 %all_to_all.40 = f32[8,128,128]{2,1,0:T(8,128)S(1)} all-to-all(f32[8,128,128]{2,1,0:T(8,128)S(1)} %bitcast.89), channel_id=1, replica_groups=mesh['h'=2,'r8'=8,'x'=4,'k'=2] {'r8'}, dimensions={0} | all-to-all | bytes 1048576 | tf_op jit(solution)/shard_map/all_to_all | solution.py:14
  22.0 0.8 broadcast_in_dim.10
  22.9 3.5 %all-to-all-start.1 = ((f32[8,128,128]{1,2,0:T(8,128)}), f32[8,128,128]{1,2,0:T(8,128)S(1)}, u32[]{:S(2)}, u32[]{:S(2)}) async-start(f32[8,128,128]{1,2,0:T(8,128)} %broadcast_in_dim.10), calls=%async_computation.1 | async-start | bytes 1048576 | tf_op jit(solution)/shard_map/all_to_all | solution.py:99
  26.4 8.7 %copy.79 = f32[256,8,8,128]{3,2,1,0:T(8,128)} copy(f32[256,8,8,128]{3,1,2,0:T(8,128)} %bitcast.85) | data formatting | bytes 16777216
  35.1 0.8 all-to-all-done.1
  35.9 0.8 copy-done.1
  36.7 8.5 %fusion.2 = f32[128,4,2,256]{3,0,2,1:T(8,128)S(1)} fusion(f32[4,2,256,8,128]{4,3,2,1,0:T(8,128)} %bitcast.84, f32[8,128,128]{1,2,0:T(8,128)} %copy-done.1), kind=kOutput, calls=%fused_computation.3 | convolution fusion | flops 1610612736 | bytes 9961472 | tf_op jit(solution)/shard_map/dot_general | solution.py:33
  45.2 0.9 select_bitcast_fusion
  46.1 1.5 %collective-permute-start = (f32[128,4,256]{2,0,1:T(8,128)}, f32[128,4,256]{2,0,1:T(8,128)}, u32[]{:S(2)}, u32[]{:S(2)}) collective-permute-start(f32[128,4,256]{2,0,1:T(8,128)} %select_bitcast_fusion), channel_id=1, source_target_pairs={{0,1},{1,0},{2,3},{3,2},{4,5},{5,4},{6,7},{7,6},{8,9},{9,8},{10,11... | collective-permute-start | bytes 1572872 | tf_op jit(solution)/shard_map/ppermute | solution.py:44
  47.9 1.5 %collective-permute-done = f32[128,4,256]{2,0,1:T(8,128)} collective-permute-done((f32[128,4,256]{2,0,1:T(8,128)}, f32[128,4,256]{2,0,1:T(8,128)}, u32[]{:S(2)}, u32[]{:S(2)}) %collective-permute-start) | collective-permute-done | bytes 524320 | tf_op jit(solution)/shard_map/ppermute | solution.py:44
  49.4 2.0 %fusion.6 = f32[128,4,256]{2,0,1:T(8,128)} fusion(f32[128,4,256]{2,0,1:T(8,128)} %collective-permute-done, f32[128,4,2,256]{3,0,2,1:T(8,128)S(1)} %fusion.2, pred[]{:T(512)S(6)} %eq.67), kind=kLoop, calls=%fused_computation.8 | loop fusion | flops 262144 | bytes 2097153 | tf_op jit(solution)/shard_map/add | solution.py:44
  51.4 4.0 %all-to-all-start.2 = ((f32[128,4,256]{2,0,1:T(8,128)}), f32[128,4,256]{2,0,1:T(8,128)S(1)}, u32[]{:S(2)}, u32[]{:S(2)}) async-start(f32[128,4,256]{2,0,1:T(8,128)} %fusion.6), calls=%async_computation.2 | async-start | bytes 1048576 | tf_op jit(solution)/shard_map/all_to_all | solution.py:45
  55.7 1.6 %scatter_custom_fusion = s32[512]{0:T(512)S(1)} fusion(s32[256]{0:T(256)S(1)} %get-tuple-element.28, s32[256]{0:T(256)S(1)} %get-tuple-element.29, s32[]{:T(128)} %constant.107.clone.1), kind=kCustom, calls=%fused_computation.50 | custom fusion | bytes 2052 | tf_op jit(solution)/shard_map/scatter | solution.py:130
  57.5 6.8 %all-to-all-done.2 = f32[128,4,256]{2,0,1:T(8,128)S(1)} async-done(((f32[128,4,256]{2,0,1:T(8,128)}), f32[128,4,256]{2,0,1:T(8,128)S(1)}, u32[]{:S(2)}, u32[]{:S(2)}) %all-to-all-start.2) | async-done | bytes 524320 | tf_op jit(solution)/shard_map/all_to_all | solution.py:45
  64.3 0.4 fusion.8
  64.8 22.4 %all_to_all.41 = f32[128,5,128]{2,1,0:T(8,128)S(1)} all-to-all(f32[128,5,128]{2,1,0:T(8,128)S(1)} %pad_maximum_fusion), channel_id=1, replica_groups=mesh['h'=2,'r8'=8,'x'=4,'k'=2] {'h','r8','x','k'}, dimensions={0} | all-to-all | bytes 655360 | tf_op jit(solution)/shard_map/all_to_all | solution.py:139
  88.1 9.8 %all_to_all.42 = f32[8,64,128]{2,1,0:T(8,128)S(1)} all-to-all(f32[8,64,128]{2,1,0:T(8,128)S(1)} %broadcast_in_dim.13), channel_id=1, replica_groups=mesh['h'=2,'r8'=8,'x'=4,'k'=2] {'x','k'}, dimensions={0} | all-to-all | bytes 524288 | tf_op jit(solution)/shard_map/all_to_all | solution.py:68
  97.9 0.7 convolution_bitcast_fusion
  98.8 13.3 %all_to_all.43 = f32[16,64,128]{2,1,0:T(8,128)S(1)} all-to-all(f32[16,64,128]{2,1,0:T(8,128)S(1)} %bitcast.91), channel_id=1, replica_groups=mesh['h'=2,'r8'=8,'x'=4,'k'=2] {'h','r8'}, dimensions={0} | all-to-all | bytes 1048576 | tf_op jit(solution)/shard_map/all_to_all | solution.py:14
  112.2 12.7 %all_to_all.44 = f32[16,64,128]{2,1,0:T(8,128)S(1)} all-to-all(f32[16,64,128]{2,1,0:T(8,128)S(1)} %broadcast_in_dim.14), channel_id=1, replica_groups=mesh['h'=2,'r8'=8,'x'=4,'k'=2] {'h','r8'}, dimensions={0} | all-to-all | bytes 1048576 | tf_op jit(solution)/shard_map/all_to_all | solution.py:68
  124.9 4.5 %fusion.26 = f32[128,4,2,128]{3,0,2,1:T(8,128)S(1)} fusion(f32[1024,128,1,1]{1,0,3,2:T(8,128)S(1)} %bitcast.86, f32[4,2,128,1024]{3,2,1,0:T(8,128)} %bitcast.88), kind=kOutput, calls=%fused_computation.61 | convolution fusion | flops 805306368 | bytes 5242880 | tf_op jit(solution)/shard_map/dot_general | solution.py:51
  129.4 3.0 %collective-permute-start.1 = (f32[128,4,128]{2,0,1:T(8,128)S(1)}, f32[128,4,128]{2,0,1:T(8,128)S(1)}, u32[]{:S(2)}, u32[]{:S(2)}) collective-permute-start(f32[128,4,128]{2,0,1:T(8,128)S(1)} %select_bitcast_fusion.1), channel_id=1, source_target_pairs={{0,1},{1,0},{2,3},{3,2},{4,5},{5,4},{6,7},{7,6},{8,9},{9,8},{10,11... | collective-permute-start | bytes 786440 | tf_op jit(solution)/shard_map/ppermute | solution.py:62
  132.4 1.2 collective-permute-done.1
  133.6 0.8 fusion.11
  134.3 3.4 %all-to-all-start.7 = ((f32[128,4,128]{2,0,1:T(8,128)}), f32[128,4,128]{2,0,1:T(8,128)S(1)}, u32[]{:S(2)}, u32[]{:S(2)}) async-start(f32[128,4,128]{2,0,1:T(8,128)} %fusion.11), calls=%async_computation.7 | async-start | bytes 524288 | tf_op jit(solution)/shard_map/all_to_all | solution.py:63
  137.7 1.0 copy.55
  138.7 1.2 constant_dynamic-slice_fusion
  140.0 0.8 copy.72
  140.8 3.0 %all-to-all-done.7 = f32[128,4,128]{2,0,1:T(8,128)S(1)} async-done(((f32[128,4,128]{2,0,1:T(8,128)}), f32[128,4,128]{2,0,1:T(8,128)S(1)}, u32[]{:S(2)}, u32[]{:S(2)}) %all-to-all-start.7) | async-done | bytes 262176 | tf_op jit(solution)/shard_map/all_to_all | solution.py:63
  143.9 1.5 %fusion.17 = f32[128,128]{1,0:T(8,128)} fusion(f32[128,128]{1,0:T(8,128)} %param.19, f32[192,128]{1,0:T(8,128)S(1)} %fusion.9, f32[128,128]{0,1:T(8,128)S(1)} %copy.71), kind=kLoop, calls=%fused_computation.29 | loop fusion | flops 32768 | bytes 262144 | tf_op jit(solution)/shard_map/sub | solution.py:157
  145.4 0.8 copy.85
  (42 shorter events, 2.3 us)
Async XLA Ops:
  0.6 97.3 %copy-start = (f32[512,1024]{1,0:T(8,128)S(1)}, f32[512,1024]{1,0:T(8,128)}, u32[]{:S(2)}) copy-start(f32[512,1024]{1,0:T(8,128)} %param.16) | copy-start | bytes 6291460
  22.9 13.0 %all-to-all-start.1 = ((f32[8,128,128]{1,2,0:T(8,128)}), f32[8,128,128]{1,2,0:T(8,128)S(1)}, u32[]{:S(2)}, u32[]{:S(2)}) async-start(f32[8,128,128]{1,2,0:T(8,128)} %broadcast_in_dim.10), calls=%async_computation.1 | async-start | bytes 1048576 | tf_op jit(solution)/shard_map/all_to_all | solution.py:99
  35.9 0.8 copy-start.1
  36.7 10.9 %copy-start.5 = (s32[256]{0:T(256)S(1)}, s32[256]{0:T(256)}, u32[]{:S(2)}) copy-start(s32[256]{0:T(256)} %param.15) | copy-start | bytes 3076
  45.2 10.2 %copy-start.3 = (f32[256,128]{1,0:T(8,128)S(1)}, f32[256,128]{1,0:T(8,128)}, u32[]{:S(2)}) copy-start(f32[256,128]{1,0:T(8,128)} %param.14) | copy-start | bytes 393220
  46.1 3.3 %collective-permute-start = (f32[128,4,256]{2,0,1:T(8,128)}, f32[128,4,256]{2,0,1:T(8,128)}, u32[]{:S(2)}, u32[]{:S(2)}) collective-permute-start(f32[128,4,256]{2,0,1:T(8,128)} %select_bitcast_fusion), channel_id=1, source_target_pairs={{0,1},{1,0},{2,3},{3,2},{4,5},{5,4},{6,7},{7,6},{8,9},{9,8},{10,11... | collective-permute-start | bytes 1572872 | tf_op jit(solution)/shard_map/ppermute | solution.py:44
  47.9 40.1 %copy-start.4 = (f32[64,128]{1,0:T(8,128)S(1)}, f32[64,128]{1,0:T(8,128)}, u32[]{:S(2)}) copy-start(f32[64,128]{1,0:T(8,128)} %param.18) | copy-start | bytes 98308
  51.4 12.9 %all-to-all-start.2 = ((f32[128,4,256]{2,0,1:T(8,128)}), f32[128,4,256]{2,0,1:T(8,128)S(1)}, u32[]{:S(2)}, u32[]{:S(2)}) async-start(f32[128,4,256]{2,0,1:T(8,128)} %fusion.6), calls=%async_computation.2 | async-start | bytes 1048576 | tf_op jit(solution)/shard_map/all_to_all | solution.py:45
  112.2 25.6 %copy-start.2 = (f32[8,128,128]{1,2,0:T(8,128)S(1)}, f32[8,128,128]{1,2,0:T(8,128)}, u32[]{:S(2)}) copy-start(f32[8,128,128]{1,2,0:T(8,128)} %copy-done.1) | copy-start | bytes 1572868
  129.4 4.2 %collective-permute-start.1 = (f32[128,4,128]{2,0,1:T(8,128)S(1)}, f32[128,4,128]{2,0,1:T(8,128)S(1)}, u32[]{:S(2)}, u32[]{:S(2)}) collective-permute-start(f32[128,4,128]{2,0,1:T(8,128)S(1)} %select_bitcast_fusion.1), channel_id=1, source_target_pairs={{0,1},{1,0},{2,3},{3,2},{4,5},{5,4},{6,7},{7,6},{8,9},{9,8},{10,11... | collective-permute-start | bytes 786440 | tf_op jit(solution)/shard_map/ppermute | solution.py:62
  134.3 9.5 %all-to-all-start.7 = ((f32[128,4,128]{2,0,1:T(8,128)}), f32[128,4,128]{2,0,1:T(8,128)S(1)}, u32[]{:S(2)}, u32[]{:S(2)}) async-start(f32[128,4,128]{2,0,1:T(8,128)} %fusion.11), calls=%async_computation.7 | async-start | bytes 524288 | tf_op jit(solution)/shard_map/all_to_all | solution.py:63

commit v13 on v11

--- a/solution.py
+++ b/solution.py
@@ -101,7 +101,7 @@
     send_index = (
         jnp.full((slots,), sep_dev + bord_dev, jnp.int32).at[placed].set(target)
     )
-    index_row = jnp.zeros((devices_all, 1, width_rhs), jnp.float32).at[:, 0, :capacity].set(
+    index_row = jnp.zeros((devices_all, capacity, width_rhs), jnp.float32).at[:, 0, :capacity].set(
         send_index.reshape(devices_all, capacity).astype(jnp.float32)
     )
     send_rows = jnp.dot(spread, outgoing, precision=exact, preferred_element_type=jnp.float32)

time: 145 us -> 146 us (level)
  no operation moved by 1% of the time
where the time goes in v13:
time: 146 us; the launch traced here: 145 us
  blocking collectives  71.4 us (49%)
  waiting for transfers between devices  23.7 us (16%)
  matrix products  19.6 us (13%)
  starting transfers between devices  15.5 us (11%)
  local copies, waits for them, and re-layouts  7.19 us (5%)
  other arithmetic  6.62 us (5%)
    all_to_all x2, blocking collectives, reduce_scatter(): lax.all_to_all(x.reshape(n, x.shape[0] // n, x.shape[1]), axis, 0, 0, til...  28.6 us
    all_to_all x2, blocking collectives, gather(): lax.all_to_all(jnp.broadcast_to(x[None], (n,) + x.shape), axis, 0, 0, til...  22.4 us
    all_to_all x1, blocking collectives, local(): got = lax.all_to_all(packed, ALL, 0, 0, tiled=True)  20.3 us
    dot_general x2, matrix products, reduce_scatter_chip(): lax.dot_general(vector, matrix, (((0,), (1,)), ((), ())), precision=preci...  12.3 us
    all_to_all x2, waiting for transfers between devices, reduce_scatter_chip(): got = lax.all_to_all(summed, 'x', 1, 1, tiled=False)  11.4 us
    all_to_all x1, waiting for transfers between devices, gather(): lax.all_to_all(jnp.broadcast_to(x[None], (n,) + x.shape), axis, 0, 0, til...  9.5 us
    all_to_all x2, starting transfers between devices, reduce_scatter_chip(): got = lax.all_to_all(summed, 'x', 1, 1, tiled=False)  7.54 us
    dot_general x1, matrix products, local(): lax.dot_general(child_inverse, child_sep_rhs, contract_rows, precision=hi...  5.88 us
  transfers between devices with their start and end apart: 5, of which 5 were waited for; matrix products, arithmetic and copies ran while one was open for 3% of the time, Pallas kernels for 0%

profile of v13, /device:TPU:1, one launch (start us, length us, event | category | flops | bytes accessed | tf_op | source)
XLA Modules:
  0.0 144.9 jit_solution(18066361901071272375)
XLA Ops:
  0.6 5.9 %fusion.21 = f32[1024,128]{1,0:T(8,128)S(1)} fusion(f32[1024,1024]{1,0:T(8,128)} %param.11, f32[1024,128]{1,0:T(8,128)} %param.13), kind=kOutput, calls=%fused_computation.60 | convolution fusion | flops 805306368 | bytes 5242880 | tf_op jit(solution)/shard_map/dot_general | solution.py:73
  6.5 15.4 %all_to_all.40 = f32[8,128,128]{2,1,0:T(8,128)S(1)} all-to-all(f32[8,128,128]{2,1,0:T(8,128)S(1)} %bitcast.88), channel_id=1, replica_groups=mesh['h'=2,'r8'=8,'x'=4,'k'=2] {'r8'}, dimensions={0} | all-to-all | bytes 1048576 | tf_op jit(solution)/shard_map/all_to_all | solution.py:14
  22.0 0.8 broadcast_in_dim.10
  22.9 3.5 %all-to-all-start.1 = ((f32[8,128,128]{1,2,0:T(8,128)}), f32[8,128,128]{1,2,0:T(8,128)S(1)}, u32[]{:S(2)}, u32[]{:S(2)}) async-start(f32[8,128,128]{1,2,0:T(8,128)} %broadcast_in_dim.10), calls=%async_computation.1 | async-start | bytes 1048576 | tf_op jit(solution)/shard_map/all_to_all | solution.py:50
  26.4 9.5 %all-to-all-done.1 = f32[8,128,128]{1,2,0:T(8,128)S(1)} async-done(((f32[8,128,128]{1,2,0:T(8,128)}), f32[8,128,128]{1,2,0:T(8,128)S(1)}, u32[]{:S(2)}, u32[]{:S(2)}) %all-to-all-start.1) | async-done | bytes 524320 | tf_op jit(solution)/shard_map/all_to_all | solution.py:50
  36.2 0.9 reshape.127
  37.1 7.8 %fusion.2 = f32[128,4,2,256]{3,0,2,1:T(8,128)S(1)} fusion(f32[4,2,256,1024]{3,2,1,0:T(8,128)} %bitcast.84, f32[1024,128,1,1]{0,1,2,3:T(8,128)} %reshape.127), kind=kOutput, calls=%fused_computation.8 | convolution fusion | flops 1610612736 | bytes 9961472 | tf_op jit(solution)/shard_map/dot_general | solution.py:33
  44.9 0.9 select_bitcast_fusion
  45.8 1.5 %collective-permute-start = (f32[128,4,256]{2,0,1:T(8,128)}, f32[128,4,256]{2,0,1:T(8,128)}, u32[]{:S(2)}, u32[]{:S(2)}) collective-permute-start(f32[128,4,256]{2,0,1:T(8,128)} %select_bitcast_fusion), channel_id=1, source_target_pairs={{0,1},{1,0},{2,3},{3,2},{4,5},{5,4},{6,7},{7,6},{8,9},{9,8},{10,11... | collective-permute-start | bytes 1572872 | tf_op jit(solution)/shard_map/ppermute | solution.py:44
  47.7 1.5 %collective-permute-done = f32[128,4,256]{2,0,1:T(8,128)} collective-permute-done((f32[128,4,256]{2,0,1:T(8,128)}, f32[128,4,256]{2,0,1:T(8,128)}, u32[]{:S(2)}, u32[]{:S(2)}) %collective-permute-start) | collective-permute-done | bytes 524320 | tf_op jit(solution)/shard_map/ppermute | solution.py:44
  49.1 2.0 %fusion.1 = f32[128,4,256]{2,0,1:T(8,128)} fusion(f32[128,4,256]{2,0,1:T(8,128)} %collective-permute-done, f32[128,4,2,256]{3,0,2,1:T(8,128)S(1)} %fusion.2, pred[]{:T(512)S(6)} %eq.67), kind=kLoop, calls=%fused_computation.7 | loop fusion | flops 262144 | bytes 2097153 | tf_op jit(solution)/shard_map/add | solution.py:44
  51.1 4.1 %all-to-all-start.2 = ((f32[128,4,256]{2,0,1:T(8,128)}), f32[128,4,256]{2,0,1:T(8,128)S(1)}, u32[]{:S(2)}, u32[]{:S(2)}) async-start(f32[128,4,256]{2,0,1:T(8,128)} %fusion.1), calls=%async_computation.2 | async-start | bytes 1048576 | tf_op jit(solution)/shard_map/all_to_all | solution.py:45
  55.5 1.4 scatter_custom_fusion
  57.1 7.0 %all-to-all-done.2 = f32[128,4,256]{2,0,1:T(8,128)S(1)} async-done(((f32[128,4,256]{2,0,1:T(8,128)}), f32[128,4,256]{2,0,1:T(8,128)S(1)}, u32[]{:S(2)}, u32[]{:S(2)}) %all-to-all-start.2) | async-done | bytes 524320 | tf_op jit(solution)/shard_map/all_to_all | solution.py:45
  64.2 0.4 fusion.4
  65.0 20.3 %all_to_all.41 = f32[128,8,128]{2,1,0:T(8,128)S(1)} all-to-all(f32[128,8,128]{2,1,0:T(8,128)S(1)} %copy.58), channel_id=1, replica_groups=mesh['h'=2,'r8'=8,'x'=4,'k'=2] {'h','r8','x','k'}, dimensions={0} | all-to-all | bytes 1048576 | tf_op jit(solution)/shard_map/all_to_all | solution.py:111
  85.7 0.3 fusion.5
  86.1 9.8 %all_to_all.42 = f32[8,64,128]{2,1,0:T(8,128)S(1)} all-to-all(f32[8,64,128]{2,1,0:T(8,128)S(1)} %broadcast_in_dim.13), channel_id=1, replica_groups=mesh['h'=2,'r8'=8,'x'=4,'k'=2] {'x','k'}, dimensions={0} | all-to-all | bytes 524288 | tf_op jit(solution)/shard_map/all_to_all | solution.py:50
  95.9 0.7 convolution_bitcast_fusion
  96.9 13.3 %all_to_all.43 = f32[16,64,128]{2,1,0:T(8,128)S(1)} all-to-all(f32[16,64,128]{2,1,0:T(8,128)S(1)} %bitcast.89), channel_id=1, replica_groups=mesh['h'=2,'r8'=8,'x'=4,'k'=2] {'h','r8'}, dimensions={0} | all-to-all | bytes 1048576 | tf_op jit(solution)/shard_map/all_to_all | solution.py:14
  110.2 12.6 %all_to_all.44 = f32[16,64,128]{2,1,0:T(8,128)S(1)} all-to-all(f32[16,64,128]{2,1,0:T(8,128)S(1)} %broadcast_in_dim.14), channel_id=1, replica_groups=mesh['h'=2,'r8'=8,'x'=4,'k'=2] {'h','r8'}, dimensions={0} | all-to-all | bytes 1048576 | tf_op jit(solution)/shard_map/all_to_all | solution.py:50
  122.8 4.5 %fusion.22 = f32[128,4,2,128]{3,0,2,1:T(8,128)S(1)} fusion(f32[1024,128,1,1]{1,0,3,2:T(8,128)S(1)} %bitcast.85, f32[4,2,128,1024]{3,2,1,0:T(8,128)} %bitcast.87), kind=kOutput, calls=%fused_computation.61 | convolution fusion | flops 805306368 | bytes 5242880 | tf_op jit(solution)/shard_map/dot_general | solution.py:33
  127.2 0.7 select_bitcast_fusion.1
  128.0 3.0 %collective-permute-start.1 = (f32[128,4,128]{2,0,1:T(8,128)}, f32[128,4,128]{2,0,1:T(8,128)S(1)}, u32[]{:S(2)}, u32[]{:S(2)}) collective-permute-start(f32[128,4,128]{2,0,1:T(8,128)} %select_bitcast_fusion.1), channel_id=1, source_target_pairs={{0,1},{1,0},{2,3},{3,2},{4,5},{5,4},{6,7},{7,6},{8,9},{9,8},{10,11... | collective-permute-start | bytes 786440 | tf_op jit(solution)/shard_map/ppermute | solution.py:44
  130.9 1.4 collective-permute-done.1
  132.3 0.7 fusion.7
  133.0 3.4 %all-to-all-start.7 = ((f32[128,4,128]{2,0,1:T(8,128)}), f32[128,4,128]{2,0,1:T(8,128)S(1)}, u32[]{:S(2)}, u32[]{:S(2)}) async-start(f32[128,4,128]{2,0,1:T(8,128)} %fusion.7), calls=%async_computation.7 | async-start | bytes 524288 | tf_op jit(solution)/shard_map/all_to_all | solution.py:45
  136.4 1.1 copy_bitcast_fusion
  137.5 0.6 constant_dynamic-slice_fusion
  138.2 4.3 %all-to-all-done.7 = f32[128,4,128]{2,0,1:T(8,128)S(1)} async-done(((f32[128,4,128]{2,0,1:T(8,128)}), f32[128,4,128]{2,0,1:T(8,128)S(1)}, u32[]{:S(2)}, u32[]{:S(2)}) %all-to-all-start.7) | async-done | bytes 262176 | tf_op jit(solution)/shard_map/all_to_all | solution.py:45
  142.6 1.5 %fusion.13 = f32[128,128]{1,0:T(8,128)} fusion(f32[128,128]{1,0:T(8,128)} %param.19, f32[192,128]{1,0:T(8,128)S(1)} %fusion.5, f32[128,128]{0,1:T(8,128)S(1)} %copy.65), kind=kLoop, calls=%fused_computation.29 | loop fusion | flops 32768 | bytes 262144 | tf_op jit(solution)/shard_map/sub | solution.py:129
  144.1 0.8 copy.74
  (41 shorter events, 2.4 us)
Async XLA Ops:
  0.6 95.3 %copy-start = (f32[512,1024]{1,0:T(8,128)S(1)}, f32[512,1024]{1,0:T(8,128)}, u32[]{:S(2)}) copy-start(f32[512,1024]{1,0:T(8,128)} %param.16) | copy-start | bytes 6291460
  22.9 13.0 %all-to-all-start.1 = ((f32[8,128,128]{1,2,0:T(8,128)}), f32[8,128,128]{1,2,0:T(8,128)S(1)}, u32[]{:S(2)}, u32[]{:S(2)}) async-start(f32[8,128,128]{1,2,0:T(8,128)} %broadcast_in_dim.10), calls=%async_computation.1 | async-start | bytes 1048576 | tf_op jit(solution)/shard_map/all_to_all | solution.py:50
  35.9 1.2 copy-start.1
  37.1 10.2 %copy-start.4 = (s32[256]{0:T(256)S(1)}, s32[256]{0:T(256)}, u32[]{:S(2)}) copy-start(s32[256]{0:T(256)} %param.15) | copy-start | bytes 3076
  44.9 12.1 %copy-start.2 = (f32[256,128]{1,0:T(8,128)S(1)}, f32[256,128]{1,0:T(8,128)}, u32[]{:S(2)}) copy-start(f32[256,128]{1,0:T(8,128)} %param.14) | copy-start | bytes 393220
  45.8 3.3 %collective-permute-start = (f32[128,4,256]{2,0,1:T(8,128)}, f32[128,4,256]{2,0,1:T(8,128)}, u32[]{:S(2)}, u32[]{:S(2)}) collective-permute-start(f32[128,4,256]{2,0,1:T(8,128)} %select_bitcast_fusion), channel_id=1, source_target_pairs={{0,1},{1,0},{2,3},{3,2},{4,5},{5,4},{6,7},{7,6},{8,9},{9,8},{10,11... | collective-permute-start | bytes 1572872 | tf_op jit(solution)/shard_map/ppermute | solution.py:44
  51.1 34.9 %copy-start.3 = (f32[64,128]{1,0:T(8,128)S(1)}, f32[64,128]{1,0:T(8,128)}, u32[]{:S(2)}) copy-start(f32[64,128]{1,0:T(8,128)} %param.18) | copy-start | bytes 98308
  51.1 13.1 %all-to-all-start.2 = ((f32[128,4,256]{2,0,1:T(8,128)}), f32[128,4,256]{2,0,1:T(8,128)S(1)}, u32[]{:S(2)}, u32[]{:S(2)}) async-start(f32[128,4,256]{2,0,1:T(8,128)} %fusion.1), calls=%async_computation.2 | async-start | bytes 1048576 | tf_op jit(solution)/shard_map/all_to_all | solution.py:45
  128.0 4.3 %collective-permute-start.1 = (f32[128,4,128]{2,0,1:T(8,128)}, f32[128,4,128]{2,0,1:T(8,128)S(1)}, u32[]{:S(2)}, u32[]{:S(2)}) collective-permute-start(f32[128,4,128]{2,0,1:T(8,128)} %select_bitcast_fusion.1), channel_id=1, source_target_pairs={{0,1},{1,0},{2,3},{3,2},{4,5},{5,4},{6,7},{7,6},{8,9},{9,8},{10,11... | collective-permute-start | bytes 786440 | tf_op jit(solution)/shard_map/ppermute | solution.py:44
  133.0 9.5 %all-to-all-start.7 = ((f32[128,4,128]{2,0,1:T(8,128)}), f32[128,4,128]{2,0,1:T(8,128)S(1)}, u32[]{:S(2)}, u32[]{:S(2)}) async-start(f32[128,4,128]{2,0,1:T(8,128)} %fusion.7), calls=%async_computation.7 | async-start | bytes 524288 | tf_op jit(solution)/shard_map/all_to_all | solution.py:45

commit v14 on v13

--- a/solution.py
+++ b/solution.py
@@ -42,8 +42,8 @@
     mine = jnp.where(first, even, odd)
     other = jnp.where(first, odd, even)
     summed = mine + lax.ppermute(other, "k", [(0, 1), (1, 0)])
-    got = lax.all_to_all(summed, "x", 1, 1, tiled=False)
-    return got.sum(axis=1).T
+    got = lax.all_to_all(jnp.transpose(summed, (1, 2, 0)), "x", 0, 0, tiled=False)
+    return got.sum(axis=0)
 
 
 def gather(x, axis, n):

time: 146 us -> 146 us (level)
    add x2 -> x0, other arithmetic: 2.68 us -> none  [reduce_scatter_chip(): summed = mine + lax.ppermute(other, 'k', [(0, 1), (1, 0)])]
    transpose x0 -> x2, other arithmetic: none -> 2.68 us  [reduce_scatter_chip(): jnp.transpose(summed, (1, 2, 0))]
where the time goes in v14:
time: 146 us; the launch traced here: 145 us
  blocking collectives  71.4 us (49%)
  waiting for transfers between devices  23.7 us (16%)
  matrix products  19.6 us (13%)
  starting transfers between devices  15.5 us (11%)
  local copies, waits for them, and re-layouts  7.19 us (5%)
  other arithmetic  6.62 us (5%)
    all_to_all x2, blocking collectives, reduce_scatter(): lax.all_to_all(x.reshape(n, x.shape[0] // n, x.shape[1]), axis, 0, 0, til...  28.6 us
    all_to_all x2, blocking collectives, gather(): lax.all_to_all(jnp.broadcast_to(x[None], (n,) + x.shape), axis, 0, 0, til...  22.4 us
    all_to_all x1, blocking collectives, local(): got = lax.all_to_all(packed, ALL, 0, 0, tiled=True)  20.3 us
    dot_general x2, matrix products, reduce_scatter_chip(): lax.dot_general(vector, matrix, (((0,), (1,)), ((), ())), precision=preci...  12.3 us
    all_to_all x2, waiting for transfers between devices, reduce_scatter_chip(): lax.all_to_all(jnp.transpose(summed, (1, 2, 0)), 'x', 0, 0, tiled=False)  11.4 us
    all_to_all x1, waiting for transfers between devices, gather(): lax.all_to_all(jnp.broadcast_to(x[None], (n,) + x.shape), axis, 0, 0, til...  9.5 us
    all_to_all x2, starting transfers between devices, reduce_scatter_chip(): lax.all_to_all(jnp.transpose(summed, (1, 2, 0)), 'x', 0, 0, tiled=False)  7.54 us
    dot_general x1, matrix products, local(): lax.dot_general(child_inverse, child_sep_rhs, contract_rows, precision=hi...  5.88 us
  transfers between devices with their start and end apart: 5, of which 5 were waited for; matrix products, arithmetic and copies ran while one was open for 3% of the time, Pallas kernels for 0%

profile of v14, /device:TPU:1, one launch (start us, length us, event | category | flops | bytes accessed | tf_op | source)
XLA Modules:
  0.0 144.9 jit_solution(7746285695730286260)
XLA Ops:
  0.6 5.9 %fusion.24 = f32[1024,128]{1,0:T(8,128)S(1)} fusion(f32[1024,1024]{1,0:T(8,128)} %param.11, f32[1024,128]{1,0:T(8,128)} %param.13), kind=kOutput, calls=%fused_computation.62 | convolution fusion | flops 805306368 | bytes 5242880 | tf_op jit(solution)/shard_map/dot_general | solution.py:73
  6.5 15.4 %all_to_all.40 = f32[8,128,128]{2,1,0:T(8,128)S(1)} all-to-all(f32[8,128,128]{2,1,0:T(8,128)S(1)} %bitcast.95), channel_id=1, replica_groups=mesh['h'=2,'r8'=8,'x'=4,'k'=2] {'r8'}, dimensions={0} | all-to-all | bytes 1048576 | tf_op jit(solution)/shard_map/all_to_all | solution.py:14
  22.0 0.8 broadcast_in_dim.10
  22.9 3.5 %all-to-all-start.1 = ((f32[8,128,128]{1,2,0:T(8,128)}), f32[8,128,128]{1,2,0:T(8,128)S(1)}, u32[]{:S(2)}, u32[]{:S(2)}) async-start(f32[8,128,128]{1,2,0:T(8,128)} %broadcast_in_dim.10), calls=%async_computation.1 | async-start | bytes 1048576 | tf_op jit(solution)/shard_map/all_to_all | solution.py:50
  26.4 9.5 %all-to-all-done.1 = f32[8,128,128]{1,2,0:T(8,128)S(1)} async-done(((f32[8,128,128]{1,2,0:T(8,128)}), f32[8,128,128]{1,2,0:T(8,128)S(1)}, u32[]{:S(2)}, u32[]{:S(2)}) %all-to-all-start.1) | async-done | bytes 524320 | tf_op jit(solution)/shard_map/all_to_all | solution.py:50
  36.2 0.9 reshape.127
  37.1 7.8 %fusion.3 = f32[128,4,2,256]{3,0,2,1:T(8,128)S(1)} fusion(f32[4,2,256,1024]{3,2,1,0:T(8,128)} %bitcast.91, f32[1024,128,1,1]{0,1,2,3:T(8,128)} %reshape.127), kind=kOutput, calls=%fused_computation.9 | convolution fusion | flops 1610612736 | bytes 9961472 | tf_op jit(solution)/shard_map/dot_general | solution.py:33
  44.9 0.9 select_bitcast_fusion
  45.8 1.5 %collective-permute-start = (f32[128,4,256]{2,0,1:T(8,128)}, f32[128,4,256]{2,0,1:T(8,128)}, u32[]{:S(2)}, u32[]{:S(2)}) collective-permute-start(f32[128,4,256]{2,0,1:T(8,128)} %select_bitcast_fusion), channel_id=1, source_target_pairs={{0,1},{1,0},{2,3},{3,2},{4,5},{5,4},{6,7},{7,6},{8,9},{9,8},{10,11... | collective-permute-start | bytes 1572872 | tf_op jit(solution)/shard_map/ppermute | solution.py:44
  47.7 1.5 %collective-permute-done = f32[128,4,256]{2,0,1:T(8,128)} collective-permute-done((f32[128,4,256]{2,0,1:T(8,128)}, f32[128,4,256]{2,0,1:T(8,128)}, u32[]{:S(2)}, u32[]{:S(2)}) %collective-permute-start) | collective-permute-done | bytes 524320 | tf_op jit(solution)/shard_map/ppermute | solution.py:44
  49.1 2.0 %fusion.2 = f32[4,256,128]{1,2,0:T(8,128)} fusion(f32[128,4,256]{2,0,1:T(8,128)} %collective-permute-done, f32[128,4,2,256]{3,0,2,1:T(8,128)S(1)} %fusion.3, pred[]{:T(512)S(6)} %eq.67), kind=kLoop, calls=%fused_computation.8 | loop fusion | flops 262144 | bytes 2097153 | tf_op jit(solution)/shard_map/transpose | solution.py:45
  51.1 4.1 %all-to-all-start.2 = ((f32[4,256,128]{1,2,0:T(8,128)}), f32[4,256,128]{1,2,0:T(8,128)S(1)}, u32[]{:S(2)}, u32[]{:S(2)}) async-start(f32[4,256,128]{1,2,0:T(8,128)} %fusion.2), calls=%async_computation.2 | async-start | bytes 1048576 | tf_op jit(solution)/shard_map/all_to_all | solution.py:45
  55.5 1.4 scatter_custom_fusion
  57.1 7.0 %all-to-all-done.2 = f32[4,256,128]{1,2,0:T(8,128)S(1)} async-done(((f32[4,256,128]{1,2,0:T(8,128)}), f32[4,256,128]{1,2,0:T(8,128)S(1)}, u32[]{:S(2)}, u32[]{:S(2)}) %all-to-all-start.2) | async-done | bytes 524320 | tf_op jit(solution)/shard_map/all_to_all | solution.py:45
  64.2 0.4 fusion.5
  65.0 20.3 %all_to_all.41 = f32[128,8,128]{2,1,0:T(8,128)S(1)} all-to-all(f32[128,8,128]{2,1,0:T(8,128)S(1)} %copy.58), channel_id=1, replica_groups=mesh['h'=2,'r8'=8,'x'=4,'k'=2] {'h','r8','x','k'}, dimensions={0} | all-to-all | bytes 1048576 | tf_op jit(solution)/shard_map/all_to_all | solution.py:111
  85.7 0.3 fusion.6
  86.1 9.8 %all_to_all.42 = f32[8,64,128]{2,1,0:T(8,128)S(1)} all-to-all(f32[8,64,128]{2,1,0:T(8,128)S(1)} %broadcast_in_dim.13), channel_id=1, replica_groups=mesh['h'=2,'r8'=8,'x'=4,'k'=2] {'x','k'}, dimensions={0} | all-to-all | bytes 524288 | tf_op jit(solution)/shard_map/all_to_all | solution.py:50
  95.9 0.7 convolution_bitcast_fusion
  96.9 13.3 %all_to_all.43 = f32[16,64,128]{2,1,0:T(8,128)S(1)} all-to-all(f32[16,64,128]{2,1,0:T(8,128)S(1)} %bitcast.96), channel_id=1, replica_groups=mesh['h'=2,'r8'=8,'x'=4,'k'=2] {'h','r8'}, dimensions={0} | all-to-all | bytes 1048576 | tf_op jit(solution)/shard_map/all_to_all | solution.py:14
  110.2 12.6 %all_to_all.44 = f32[16,64,128]{2,1,0:T(8,128)S(1)} all-to-all(f32[16,64,128]{2,1,0:T(8,128)S(1)} %broadcast_in_dim.14), channel_id=1, replica_groups=mesh['h'=2,'r8'=8,'x'=4,'k'=2] {'h','r8'}, dimensions={0} | all-to-all | bytes 1048576 | tf_op jit(solution)/shard_map/all_to_all | solution.py:50
  122.8 4.5 %fusion.25 = f32[128,4,2,128]{3,0,2,1:T(8,128)S(1)} fusion(f32[1024,128,1,1]{1,0,3,2:T(8,128)S(1)} %bitcast.92, f32[4,2,128,1024]{3,2,1,0:T(8,128)} %bitcast.94), kind=kOutput, calls=%fused_computation.63 | convolution fusion | flops 805306368 | bytes 5242880 | tf_op jit(solution)/shard_map/dot_general | solution.py:33
  127.2 0.7 select_bitcast_fusion.1
  128.0 3.0 %collective-permute-start.1 = (f32[128,4,128]{2,0,1:T(8,128)}, f32[128,4,128]{2,0,1:T(8,128)S(1)}, u32[]{:S(2)}, u32[]{:S(2)}) collective-permute-start(f32[128,4,128]{2,0,1:T(8,128)} %select_bitcast_fusion.1), channel_id=1, source_target_pairs={{0,1},{1,0},{2,3},{3,2},{4,5},{5,4},{6,7},{7,6},{8,9},{9,8},{10,11... | collective-permute-start | bytes 786440 | tf_op jit(solution)/shard_map/ppermute | solution.py:44
  130.9 1.4 collective-permute-done.1
  132.3 0.7 fusion.9
  133.0 3.4 %all-to-all-start.7 = ((f32[4,128,128]{1,2,0:T(8,128)}), f32[4,128,128]{1,2,0:T(8,128)S(1)}, u32[]{:S(2)}, u32[]{:S(2)}) async-start(f32[4,128,128]{1,2,0:T(8,128)} %fusion.9), calls=%async_computation.7 | async-start | bytes 524288 | tf_op jit(solution)/shard_map/all_to_all | solution.py:45
  136.4 1.1 copy_bitcast_fusion
  137.5 0.6 constant_dynamic-slice_fusion
  138.2 4.3 %all-to-all-done.7 = f32[4,128,128]{1,2,0:T(8,128)S(1)} async-done(((f32[4,128,128]{1,2,0:T(8,128)}), f32[4,128,128]{1,2,0:T(8,128)S(1)}, u32[]{:S(2)}, u32[]{:S(2)}) %all-to-all-start.7) | async-done | bytes 262176 | tf_op jit(solution)/shard_map/all_to_all | solution.py:45
  142.6 1.5 %fusion.16 = f32[128,128]{1,0:T(8,128)} fusion(f32[128,128]{1,0:T(8,128)S(1)} %copy.65, f32[128,128]{1,0:T(8,128)} %param.19, f32[192,128]{1,0:T(8,128)S(1)} %fusion.6), kind=kLoop, calls=%fused_computation.31 | loop fusion | flops 32768 | bytes 262144 | tf_op jit(solution)/shard_map/sub | solution.py:129
  144.1 0.8 copy.74
  (41 shorter events, 2.4 us)
Async XLA Ops:
  0.6 95.3 %copy-start = (f32[512,1024]{1,0:T(8,128)S(1)}, f32[512,1024]{1,0:T(8,128)}, u32[]{:S(2)}) copy-start(f32[512,1024]{1,0:T(8,128)} %param.16) | copy-start | bytes 6291460
  22.9 13.0 %all-to-all-start.1 = ((f32[8,128,128]{1,2,0:T(8,128)}), f32[8,128,128]{1,2,0:T(8,128)S(1)}, u32[]{:S(2)}, u32[]{:S(2)}) async-start(f32[8,128,128]{1,2,0:T(8,128)} %broadcast_in_dim.10), calls=%async_computation.1 | async-start | bytes 1048576 | tf_op jit(solution)/shard_map/all_to_all | solution.py:50
  35.9 1.2 copy-start.1
  37.1 10.2 %copy-start.4 = (s32[256]{0:T(256)S(1)}, s32[256]{0:T(256)}, u32[]{:S(2)}) copy-start(s32[256]{0:T(256)} %param.15) | copy-start | bytes 3076
  44.9 12.1 %copy-start.2 = (f32[256,128]{1,0:T(8,128)S(1)}, f32[256,128]{1,0:T(8,128)}, u32[]{:S(2)}) copy-start(f32[256,128]{1,0:T(8,128)} %param.14) | copy-start | bytes 393220
  45.8 3.3 %collective-permute-start = (f32[128,4,256]{2,0,1:T(8,128)}, f32[128,4,256]{2,0,1:T(8,128)}, u32[]{:S(2)}, u32[]{:S(2)}) collective-permute-start(f32[128,4,256]{2,0,1:T(8,128)} %select_bitcast_fusion), channel_id=1, source_target_pairs={{0,1},{1,0},{2,3},{3,2},{4,5},{5,4},{6,7},{7,6},{8,9},{9,8},{10,11... | collective-permute-start | bytes 1572872 | tf_op jit(solution)/shard_map/ppermute | solution.py:44
  51.1 34.9 %copy-start.3 = (f32[64,128]{1,0:T(8,128)S(1)}, f32[64,128]{1,0:T(8,128)}, u32[]{:S(2)}) copy-start(f32[64,128]{1,0:T(8,128)} %param.18) | copy-start | bytes 98308
  51.1 13.1 %all-to-all-start.2 = ((f32[4,256,128]{1,2,0:T(8,128)}), f32[4,256,128]{1,2,0:T(8,128)S(1)}, u32[]{:S(2)}, u32[]{:S(2)}) async-start(f32[4,256,128]{1,2,0:T(8,128)} %fusion.2), calls=%async_computation.2 | async-start | bytes 1048576 | tf_op jit(solution)/shard_map/all_to_all | solution.py:45
  128.0 4.3 %collective-permute-start.1 = (f32[128,4,128]{2,0,1:T(8,128)}, f32[128,4,128]{2,0,1:T(8,128)S(1)}, u32[]{:S(2)}, u32[]{:S(2)}) collective-permute-start(f32[128,4,128]{2,0,1:T(8,128)} %select_bitcast_fusion.1), channel_id=1, source_target_pairs={{0,1},{1,0},{2,3},{3,2},{4,5},{5,4},{6,7},{7,6},{8,9},{9,8},{10,11... | collective-permute-start | bytes 786440 | tf_op jit(solution)/shard_map/ppermute | solution.py:44
  133.0 9.5 %all-to-all-start.7 = ((f32[4,128,128]{1,2,0:T(8,128)}), f32[4,128,128]{1,2,0:T(8,128)S(1)}, u32[]{:S(2)}, u32[]{:S(2)}) async-start(f32[4,128,128]{1,2,0:T(8,128)} %fusion.9), calls=%async_computation.7 | async-start | bytes 524288 | tf_op jit(solution)/shard_map/all_to_all | solution.py:45

commit v15 on v14

--- a/solution.py
+++ b/solution.py
@@ -38,10 +38,8 @@
         preferred_element_type=jnp.float32,
     )
     blocks = product.reshape(product.shape[0], chips, 2, matrix.shape[0] // (2 * chips))
-    even, odd = blocks[:, :, 0], blocks[:, :, 1]
-    mine = jnp.where(first, even, odd)
-    other = jnp.where(first, odd, even)
-    summed = mine + lax.ppermute(other, "k", [(0, 1), (1, 0)])
+    both = blocks + lax.ppermute(blocks, "k", [(0, 1), (1, 0)])
+    summed = jnp.where(first, both[:, :, 0], both[:, :, 1])
     got = lax.all_to_all(jnp.transpose(summed, (1, 2, 0)), "x", 0, 0, tiled=False)
     return got.sum(axis=0)
 

time: 146 us -> 150 us (1.027)
  blocking collectives: 71.4 us -> 84.2 us
  waiting for transfers between devices: 23.7 us -> 16.5 us
  starting transfers between devices: 15.5 us -> 12.1 us
  matrix products: 19.6 us -> 21.2 us
    all_to_all x2 -> x3, blocking collectives: 22.4 us -> 34.3 us  [gather(): lax.all_to_all(jnp.broadcast_to(x[None], (n,) + x.shape), axis, 0, 0, til...]
    all_to_all x1 -> x0, waiting for transfers between devices: 9.5 us -> none  [gather(): lax.all_to_all(jnp.broadcast_to(x[None], (n,) + x.shape), axis, 0, 0, til...]
    all_to_all x1 -> x0, starting transfers between devices: 3.49 us -> none  [gather(): lax.all_to_all(jnp.broadcast_to(x[None], (n,) + x.shape), axis, 0, 0, til...]
    add x0 -> x2, other arithmetic: none -> 2.96 us  [reduce_scatter_chip(): both = blocks + lax.ppermute(blocks, 'k', [(0, 1), (1, 0)])]
    dot_general x2, matrix products: 12.3 us -> 13.9 us  [reduce_scatter_chip(): lax.dot_general(vector, matrix, (((0,), (1,)), ((), ())), precision=preci...]
    select_n x2 -> x0, other arithmetic: 1.6 us -> none  [reduce_scatter_chip(): other = jnp.where(first, odd, even)]
  transfers between devices with their start and end apart: 5 -> 4, of which waited for: 5 -> 4; matrix products, arithmetic and copies ran while one was open for 3% -> 2% of each run, Pallas kernels for 0% -> 0%
where the time goes in v15:
time: 150 us; the launch traced here: 149 us
  blocking collectives  84.2 us (56%)
  matrix products  21.2 us (14%)
  waiting for transfers between devices  16.5 us (11%)
  starting transfers between devices  12.1 us (8%)
  local copies, waits for them, and re-layouts  7.2 us (5%)
  other arithmetic  6.88 us (5%)
    all_to_all x3, blocking collectives, gather(): lax.all_to_all(jnp.broadcast_to(x[None], (n,) + x.shape), axis, 0, 0, til...  34.3 us
    all_to_all x2, blocking collectives, reduce_scatter(): lax.all_to_all(x.reshape(n, x.shape[0] // n, x.shape[1]), axis, 0, 0, til...  29.4 us
    all_to_all x1, blocking collectives, local(): got = lax.all_to_all(packed, ALL, 0, 0, tiled=True)  20.5 us
    dot_general x2, matrix products, reduce_scatter_chip(): lax.dot_general(vector, matrix, (((0,), (1,)), ((), ())), precision=preci...  13.9 us
    all_to_all x2, waiting for transfers between devices, reduce_scatter_chip(): lax.all_to_all(jnp.transpose(summed, (1, 2, 0)), 'x', 0, 0, tiled=False)  12.4 us
    all_to_all x2, starting transfers between devices, reduce_scatter_chip(): lax.all_to_all(jnp.transpose(summed, (1, 2, 0)), 'x', 0, 0, tiled=False)  7.55 us
    dot_general x1, matrix products, local(): lax.dot_general(child_inverse, child_sep_rhs, contract_rows, precision=hi...  5.88 us
    ppermute x2, starting transfers between devices, reduce_scatter_chip(): both = blocks + lax.ppermute(blocks, 'k', [(0, 1), (1, 0)])  4.6 us
  transfers between devices with their start and end apart: 4, of which 4 were waited for; matrix products, arithmetic and copies ran while one was open for 2% of the time, Pallas kernels for 0%

profile of v15, /device:TPU:1, one launch (start us, length us, event | category | flops | bytes accessed | tf_op | source)
XLA Modules:
  0.0 149.1 jit_solution(6079952733022131179)
XLA Ops:
  0.6 5.9 %fusion.20 = f32[1024,128]{1,0:T(8,128)S(1)} fusion(f32[1024,1024]{1,0:T(8,128)} %param.11, f32[1024,128]{1,0:T(8,128)} %param.13), kind=kOutput, calls=%fused_computation.56 | convolution fusion | flops 805306368 | bytes 5242880 | tf_op jit(solution)/shard_map/dot_general | solution.py:71
  6.5 15.4 %all_to_all.40 = f32[8,128,128]{2,1,0:T(8,128)S(1)} all-to-all(f32[8,128,128]{2,1,0:T(8,128)S(1)} %bitcast.55), channel_id=1, replica_groups=mesh['h'=2,'r8'=8,'x'=4,'k'=2] {'r8'}, dimensions={0} | all-to-all | bytes 1048576 | tf_op jit(solution)/shard_map/all_to_all | solution.py:14
  22.1 11.4 %all_to_all.41 = f32[8,128,128]{1,2,0:T(8,128)S(1)} all-to-all(f32[8,128,128]{1,2,0:T(8,128)S(1)} %broadcast_in_dim.10), channel_id=1, replica_groups=mesh['h'=2,'r8'=8,'x'=4,'k'=2] {'r8'}, dimensions={0} | all-to-all | bytes 1048576 | tf_op jit(solution)/shard_map/all_to_all | solution.py:48
  33.5 1.1 copy.25
  34.6 1.1 reshape.123
  35.7 8.6 %fusion.1 = f32[128,4,2,256]{3,0,2,1:T(8,128)} fusion(f32[4,2,256,1024]{3,2,1,0:T(8,128)} %bitcast.51, f32[1024,128,1,1]{0,1,2,3:T(8,128)S(1)} %reshape.123), kind=kOutput, calls=%fused_computation.7 | convolution fusion | flops 1610612736 | bytes 9961472 | tf_op jit(solution)/shard_map/dot_general | solution.py:33
  44.3 2.1 %collective-permute-start = (f32[128,4,2,256]{3,0,2,1:T(8,128)}, f32[128,4,2,256]{3,0,2,1:T(8,128)}, u32[]{:S(2)}, u32[]{:S(2)}) collective-permute-start(f32[128,4,2,256]{3,0,2,1:T(8,128)} %fusion.1), channel_id=1, source_target_pairs={{0,1},{1,0},{2,3},{3,2},{4,5},{5,4},{6,7},{7,6},{8,9},{9,8},{10,11... | collective-permute-start | bytes 3145736 | tf_op jit(solution)/shard_map/ppermute | solution.py:41
  46.8 2.2 %collective-permute-done = f32[128,4,2,256]{3,0,2,1:T(8,128)} collective-permute-done((f32[128,4,2,256]{3,0,2,1:T(8,128)}, f32[128,4,2,256]{3,0,2,1:T(8,128)}, u32[]{:S(2)}, u32[]{:S(2)}) %collective-permute-start) | collective-permute-done | bytes 1048608 | tf_op jit(solution)/shard_map/ppermute | solution.py:41
  49.0 1.7 %add.50 = f32[128,4,2,256]{3,0,2,1:T(8,128)S(1)} add(f32[128,4,2,256]{3,0,2,1:T(8,128)} %fusion.1, f32[128,4,2,256]{3,0,2,1:T(8,128)} %collective-permute-done) | non-fusion elementwise | flops 262144 | bytes 3145728 | tf_op jit(solution)/shard_map/add | solution.py:41
  50.8 0.9 fusion
  51.6 4.1 %all-to-all-start.2 = ((f32[4,256,128]{1,2,0:T(8,128)}), f32[4,256,128]{1,2,0:T(8,128)S(1)}, u32[]{:S(2)}, u32[]{:S(2)}) async-start(f32[4,256,128]{1,2,0:T(8,128)} %fusion), calls=%async_computation.2 | async-start | bytes 1048576 | tf_op jit(solution)/shard_map/all_to_all | solution.py:43
  56.0 1.4 scatter_custom_fusion
  57.6 7.0 %all-to-all-done.2 = f32[4,256,128]{1,2,0:T(8,128)S(1)} async-done(((f32[4,256,128]{1,2,0:T(8,128)}), f32[4,256,128]{1,2,0:T(8,128)S(1)}, u32[]{:S(2)}, u32[]{:S(2)}) %all-to-all-start.2) | async-done | bytes 524320 | tf_op jit(solution)/shard_map/all_to_all | solution.py:43
  64.7 0.4 fusion.3
  65.2 0.3 copy.30
  65.5 20.5 %all_to_all.42 = f32[128,8,128]{2,1,0:T(8,128)S(1)} all-to-all(f32[128,8,128]{2,1,0:T(8,128)S(1)} %copy.30), channel_id=1, replica_groups=mesh['h'=2,'r8'=8,'x'=4,'k'=2] {'h','r8','x','k'}, dimensions={0} | all-to-all | bytes 1048576 | tf_op jit(solution)/shard_map/all_to_all | solution.py:109
  86.4 0.3 fusion.4
  86.8 9.8 %all_to_all.43 = f32[8,64,128]{2,1,0:T(8,128)S(1)} all-to-all(f32[8,64,128]{2,1,0:T(8,128)S(1)} %broadcast_in_dim.13), channel_id=1, replica_groups=mesh['h'=2,'r8'=8,'x'=4,'k'=2] {'x','k'}, dimensions={0} | all-to-all | bytes 524288 | tf_op jit(solution)/shard_map/all_to_all | solution.py:48
  96.7 0.7 convolution_bitcast_fusion
  97.4 1.0 copy.31
  98.4 14.1 %all_to_all.44 = f32[16,64,128]{2,1,0:T(8,128)S(1)} all-to-all(f32[16,64,128]{2,1,0:T(8,128)} %bitcast.56), channel_id=1, replica_groups=mesh['h'=2,'r8'=8,'x'=4,'k'=2] {'h','r8'}, dimensions={0} | all-to-all | bytes 1048576 | tf_op jit(solution)/shard_map/all_to_all | solution.py:14
  112.5 13.1 %all_to_all.45 = f32[16,64,128]{2,1,0:T(8,128)S(1)} all-to-all(f32[16,64,128]{2,1,0:T(8,128)S(1)} %broadcast_in_dim.14), channel_id=1, replica_groups=mesh['h'=2,'r8'=8,'x'=4,'k'=2] {'h','r8'}, dimensions={0} | all-to-all | bytes 1048576 | tf_op jit(solution)/shard_map/all_to_all | solution.py:48
  125.6 5.2 %fusion.21 = f32[128,4,2,128]{3,0,2,1:T(8,128)} fusion(f32[1024,128,1,1]{1,0,3,2:T(8,128)S(1)} %bitcast.52, f32[4,2,128,1024]{3,2,1,0:T(8,128)} %bitcast.54), kind=kOutput, calls=%fused_computation.57 | convolution fusion | flops 805306368 | bytes 5242880 | tf_op jit(solution)/shard_map/dot_general | solution.py:33
  130.9 2.5 %collective-permute-start.1 = (f32[128,4,2,128]{3,0,2,1:T(8,128)}, f32[128,4,2,128]{3,0,2,1:T(8,128)}, u32[]{:S(2)}, u32[]{:S(2)}) collective-permute-start(f32[128,4,2,128]{3,0,2,1:T(8,128)} %fusion.21), channel_id=1, source_target_pairs={{0,1},{1,0},{2,3},{3,2},{4,5},{5,4},{6,7},{7,6},{8,9},{9,8},{10,11... | collective-permute-start | bytes 1572872 | tf_op jit(solution)/shard_map/ppermute | solution.py:41
  133.4 1.9 %collective-permute-done.1 = f32[128,4,2,128]{3,0,2,1:T(8,128)} collective-permute-done((f32[128,4,2,128]{3,0,2,1:T(8,128)}, f32[128,4,2,128]{3,0,2,1:T(8,128)}, u32[]{:S(2)}, u32[]{:S(2)}) %collective-permute-start.1) | collective-permute-done | bytes 524320 | tf_op jit(solution)/shard_map/ppermute | solution.py:41
  135.3 1.3 add.58
  136.5 0.7 fusion.5
  137.2 3.4 %all-to-all-start.7 = ((f32[4,128,128]{1,2,0:T(8,128)}), f32[4,128,128]{1,2,0:T(8,128)S(1)}, u32[]{:S(2)}, u32[]{:S(2)}) async-start(f32[4,128,128]{1,2,0:T(8,128)} %fusion.5), calls=%async_computation.7 | async-start | bytes 524288 | tf_op jit(solution)/shard_map/all_to_all | solution.py:43
  140.7 0.6 constant_dynamic-slice_fusion
  141.4 5.4 %all-to-all-done.7 = f32[4,128,128]{1,2,0:T(8,128)S(1)} async-done(((f32[4,128,128]{1,2,0:T(8,128)}), f32[4,128,128]{1,2,0:T(8,128)S(1)}, u32[]{:S(2)}, u32[]{:S(2)}) %all-to-all-start.7) | async-done | bytes 262176 | tf_op jit(solution)/shard_map/all_to_all | solution.py:43
  146.8 1.5 fusion.12
  148.3 0.8 copy.40
  (38 shorter events, 1.7 us)
Async XLA Ops:
  0.6 96.0 %copy-start = (f32[512,1024]{1,0:T(8,128)S(1)}, f32[512,1024]{1,0:T(8,128)}, u32[]{:S(2)}) copy-start(f32[512,1024]{1,0:T(8,128)} %param.16) | copy-start | bytes 6291460
  35.7 10.7 %copy-start.3 = (s32[256]{0:T(256)S(1)}, s32[256]{0:T(256)}, u32[]{:S(2)}) copy-start(s32[256]{0:T(256)} %param.15) | copy-start | bytes 3076
  44.3 13.2 %copy-start.1 = (f32[256,128]{1,0:T(8,128)S(1)}, f32[256,128]{1,0:T(8,128)}, u32[]{:S(2)}) copy-start(f32[256,128]{1,0:T(8,128)} %param.14) | copy-start | bytes 393220
  44.3 4.7 %collective-permute-start = (f32[128,4,2,256]{3,0,2,1:T(8,128)}, f32[128,4,2,256]{3,0,2,1:T(8,128)}, u32[]{:S(2)}, u32[]{:S(2)}) collective-permute-start(f32[128,4,2,256]{3,0,2,1:T(8,128)} %fusion.1), channel_id=1, source_target_pairs={{0,1},{1,0},{2,3},{3,2},{4,5},{5,4},{6,7},{7,6},{8,9},{9,8},{10,11... | collective-permute-start | bytes 3145736 | tf_op jit(solution)/shard_map/ppermute | solution.py:41
  51.6 35.1 %copy-start.2 = (f32[64,128]{1,0:T(8,128)S(1)}, f32[64,128]{1,0:T(8,128)}, u32[]{:S(2)}) copy-start(f32[64,128]{1,0:T(8,128)} %param.18) | copy-start | bytes 98308
  51.6 13.1 %all-to-all-start.2 = ((f32[4,256,128]{1,2,0:T(8,128)}), f32[4,256,128]{1,2,0:T(8,128)S(1)}, u32[]{:S(2)}, u32[]{:S(2)}) async-start(f32[4,256,128]{1,2,0:T(8,128)} %fusion), calls=%async_computation.2 | async-start | bytes 1048576 | tf_op jit(solution)/shard_map/all_to_all | solution.py:43
  130.9 4.4 %collective-permute-start.1 = (f32[128,4,2,128]{3,0,2,1:T(8,128)}, f32[128,4,2,128]{3,0,2,1:T(8,128)}, u32[]{:S(2)}, u32[]{:S(2)}) collective-permute-start(f32[128,4,2,128]{3,0,2,1:T(8,128)} %fusion.21), channel_id=1, source_target_pairs={{0,1},{1,0},{2,3},{3,2},{4,5},{5,4},{6,7},{7,6},{8,9},{9,8},{10,11... | collective-permute-start | bytes 1572872 | tf_op jit(solution)/shard_map/ppermute | solution.py:41
  137.2 9.5 %all-to-all-start.7 = ((f32[4,128,128]{1,2,0:T(8,128)}), f32[4,128,128]{1,2,0:T(8,128)S(1)}, u32[]{:S(2)}, u32[]{:S(2)}) async-start(f32[4,128,128]{1,2,0:T(8,128)} %fusion.5), calls=%async_computation.7 | async-start | bytes 524288 | tf_op jit(solution)/shard_map/all_to_all | solution.py:43
